TPU v7x, 32 devices: a whole 2x2x4 slice. The times are simulated.
32 devices in a mesh: row: 4 (over x, core), col: 8 (over z, y).
Axes of the slice: x: 2, y: 2, z: 4, core: 2. Of those that a mesh axis runs over, the one named last changes fastest.
Arguments:
- embed: bfloat16 [1024, 768], P(('row', 'col'))
- beta: bfloat16 [1024], P(('row', 'col')), may hold values from 16 to 400
- block_mask: int32 [8, 8], P('row'), may hold values from 0 to 1, as said below
- counts: int32 [8], replicated, may hold values from 2 to 128
- probes: float32 [64, 1024], P(None, ('row', 'col')), may hold values from -6 to 6
Outputs:
- spectral: float32 [64, 1024], P(None, ('row', 'col'))
Inputs may be any that keep to these rules, and one draw needn't show every extreme that they name: `block_mask`: every diagonal entry is 1.
All inputs are finite; a program needn't handle non-finite values.
Results may differ from a plain program's by a relative error of at most 0.012.
The roundings to bfloat16 on the way count: a program that leaves them out, or rounds other values in their place, can miss the bound.
Values may be sent and summed in bfloat16 or wider, within the bound.
No kernel may reach another device: no remote copies, remote signals or barrier semaphores. Data moves between devices by JAX's collectives and lax.ppermute only.
A program may use at most 64 MiB of HBM per device.

v0:
```python
import jax
import jax.numpy as jnp
from jax import lax
from jax.sharding import PartitionSpec as P

ITERS = 2


def spread(shard, axis, root):
    mine = lax.axis_index(axis) == root
    return lax.psum(jnp.where(mine, shard, jnp.zeros_like(shard)), axis)


def own_piece(totals, col_ratio, n_row, row_index, col_index):
    shard_len = totals.shape[1] // n_row
    chosen = jnp.zeros_like(totals)
    for root_k in range(col_ratio):
        received = spread(totals, "col", col_ratio * row_index + root_k)
        chosen = jnp.where(col_index // n_row == root_k, received, chosen)
    return lax.dynamic_slice_in_dim(chosen, col_index % n_row * shard_len, shard_len, 1)


def body(embed, beta, block_mask, counts, probes):
    n_row = lax.axis_size("row")
    n_col = lax.axis_size("col")
    col_ratio = n_col // n_row
    row_index = lax.axis_index("row")
    col_index = lax.axis_index("col")
    shard_len, feat_width = embed.shape
    row_files = shard_len * n_col
    col_files = shard_len * n_row
    values = embed.astype(jnp.float32)
    unit_vec = (
        values * lax.rsqrt(jnp.mean(values * values, axis=1, keepdims=True) + 1e-06)
    ).astype(jnp.bfloat16)
    unit_rows, beta_rows = (
        lax.all_gather(unit_vec, "col", axis=0, tiled=True),
        lax.all_gather(beta, "col", axis=0, tiled=True),
    )
    half_pick = col_index % col_ratio
    col_seq = lax.iota(jnp.int32, col_files)
    unit_cols = spread(
        lax.dynamic_slice_in_dim(unit_rows, half_pick * col_files, col_files, 0),
        "row",
        col_index // col_ratio,
    )
    col_ids = col_index * col_files + col_seq
    gram_tile = lax.dot_general(
        unit_rows, unit_cols, (((1,), (1,)), ((), ())), preferred_element_type=jnp.float32
    )
    scores = gram_tile * (beta_rows.astype(jnp.float32) / feat_width)[:, None]
    row_blocks = block_mask.shape[0]
    blk_size = row_files // row_blocks
    col_block = col_ids // blk_size
    col_live = col_ids % blk_size < jnp.take(counts, col_block, axis=0)
    mask_cols = jnp.take(block_mask, col_block, axis=1) == 1
    block_wide = jnp.broadcast_to(mask_cols[:, None, :], (row_blocks, blk_size, col_files)).reshape(
        row_files, col_files
    )
    row_ids = row_index * row_files + lax.iota(jnp.int32, row_files)
    allowed = block_wide & col_live[None, :] & (row_ids[:, None] != col_ids[None, :])
    masked = jnp.where(allowed, scores, -1e30)
    local_top = jnp.max(masked, axis=1)
    row_top = lax.pmax(local_top, "col")
    row_mass = lax.psum(
        jnp.sum(jnp.where(allowed, jnp.exp(masked - row_top[:, None]), 0.0), axis=1), "col"
    )
    weights = jnp.where(allowed, jnp.exp(masked - row_top[:, None]) / row_mass[:, None], 0.0)
    col_mass = lax.psum(jnp.sum(weights, axis=0), "row")
    own_mass = own_piece(col_mass[None, :], col_ratio, n_row, row_index, col_index)[0]
    inv_root = lax.rsqrt((1.0 + own_mass) * 0.5)
    affinity = weights.astype(jnp.bfloat16)
    probe_state = probes
    for sweep in range(ITERS):
        scaled = (probe_state * inv_root[None, :]).astype(jnp.bfloat16)
        probe_rows = lax.all_gather(scaled, "col", axis=1, tiled=True)
        probe_cols = spread(
            lax.dynamic_slice_in_dim(probe_rows, half_pick * col_files, col_files, 1),
            "row",
            col_index // col_ratio,
        )
        row_part = lax.dot_general(
            probe_cols, affinity, (((1,), (1,)), ((), ())), preferred_element_type=jnp.float32
        )
        col_part = jnp.dot(probe_rows, affinity, preferred_element_type=jnp.float32)
        own_rows = lax.psum_scatter(
            row_part.astype(jnp.bfloat16), "col", scatter_dimension=1, tiled=True
        ).astype(jnp.float32)
        col_total = lax.psum(col_part, "row")
        own_cols = own_piece(col_total, col_ratio, n_row, row_index, col_index)
        probe_state = (own_rows + own_cols) * (0.5 * inv_root)[None, :]
    return probe_state


def solution(mesh):
    placed = (
        P(("row", "col"), None),
        P(("row", "col")),
        P("row", None),
        P(),
        P(None, ("row", "col")),
    )
    return jax.shard_map(
        body, mesh=mesh, in_specs=placed, out_specs=P(None, ("row", "col")), check_vma=False
    )
```

profile of v0, /device:TPU:0, one launch (start us, length us, event | category | flops | bytes accessed | tf_op | source)
XLA Modules:
  0.0 495.1 jit_solution(6957773946014642195)
XLA Ops:
  6.5 0.0 copy-start
  6.5 0.0 all-reduce.8.cloned.1.call-start
  6.5 0.8 copy-done
  7.3 0.1 fusion.1
  7.5 0.1 fusion.2
  7.5 32.7 %all_gather.12 = bf16[256,768]{1,0:T(8,128)(2,1)S(1)} all-gather(bf16[32,768]{1,0:T(8,128)(2,1)S(1)} %fusion.2), channel_id=1, replica_groups=mesh['row'=4,'col'=8] {'col'}, dimensions={0}, use_global_device_ids=true | all-gather | bytes 442368 | tf_op jit(solution)/shard_map/all_gather | solution.py:37
  40.3 0.7 dynamic-slice_select_fusion
  41.0 0.0 all-reduce.8.cloned.1.call-update
  41.0 0.0 reduce-scatter.3.cloned.1.call-start
  41.2 0.0 copy-start.1
  41.2 0.6 copy-done.1
  41.8 0.7 fusion.21
  42.5 0.0 copy-start.3
  42.5 0.7 copy-done.3
  43.2 0.1 copy.9
  43.3 0.6 gather_fusion
  43.9 0.1 fusion.3
  44.0 0.1 copy.10
  44.1 0.1 copy.11
  44.2 0.0 copy-start.5
  44.3 0.6 copy-done.5
  44.9 0.6 dynamic-slice
  46.1 0.0 copy-start.4
  46.2 0.6 copy-done.4
  46.8 0.2 dynamic-update-slice
  47.0 21.5 %all-reduce = bf16[256]{0:T(256)(128)(2,1)S(1)} all-reduce(bf16[256]{0:T(256)(128)(2,1)S(1)} %dynamic-update-slice), channel_id=1, replica_groups=mesh['row'=4,'col'=8] {'col'}, use_global_device_ids=true, to_apply=%add | all-reduce | flops 256 | bytes 1024
  68.5 5.1 %fusion.12 = pred[128]{0:T(512)(128)(4,1)S(1)} fusion(s32[]{:T(128)} %bitcast.3, s32[]{:T(128)} %bitcast.4, s32[]{:T(128)} %bitcast.5, s32[]{:T(128)} %bitcast.6, s32[]{:T(128)} %bitcast.7, s32[]{:T(128)} %bitcast.8, s32[]{:T(128)} %bitcast.9, s32[]{:T(128)} %bitcast.10, s32[]{:T(128)S(6)} %mul.86), kind=kLoop, calls=%fused_computation.62 | loop fusion | flops 7808 | bytes 164 | tf_op jit(solution)/shard_map/lt | solution.py:55
  73.6 0.4 all-reduce.8.cloned.1.call-done
  74.0 1.2 fusion.22
  75.2 21.3 %pmax.7 = f32[256]{0:T(256)S(1)} all-reduce(f32[256]{0:T(256)S(1)} %get-tuple-element.29), channel_id=1, replica_groups=mesh['row'=4,'col'=8] {'col'}, use_global_device_ids=true, to_apply=%region_3.4 | all-reduce | flops 256 | bytes 2048 | tf_op jit(solution)/shard_map/pmax | solution.py:64
  96.6 0.1 select_reduce_fusion
  96.7 17.1 %psum.92 = f32[256]{0:T(256)S(1)} all-reduce(f32[256]{0:T(256)S(1)} %select_reduce_fusion), channel_id=1, replica_groups=mesh['row'=4,'col'=8] {'col'}, use_global_device_ids=true, to_apply=%region_5.6 | all-reduce | flops 256 | bytes 2048 | tf_op jit(solution)/shard_map/psum | solution.py:65
  113.8 0.2 fusion.11
  114.0 0.0 copy-start.2
  114.0 5.9 %psum.93 = f32[128]{0:T(128)S(1)} all-reduce(f32[128]{0:T(128)S(1)} %get-tuple-element.13), channel_id=1, replica_groups=mesh['row'=4,'col'=8] {'row'}, use_global_device_ids=true, to_apply=%region_7.8 | all-reduce | flops 128 | bytes 1024 | tf_op jit(solution)/shard_map/psum | solution.py:69
  119.9 19.1 %all-reduce.3 = (f32[1,128]{1,0:T(1,128)S(1)}, f32[1,128]{1,0:T(1,128)S(1)}) all-reduce(f32[1,128]{1,0:T(1,128)S(1)} %get-tuple-element.20, f32[1,128]{1,0:T(1,128)S(1)} %get-tuple-element.19), channel_id=1, replica_groups=mesh['row'=4,'col'=8] {'col'}, use_global_device_ids=true, to_apply=%region_8.9 | all-reduce | flops 256 | bytes 2048 | tf_op jit(solution)/shard_map/psum | solution.py:11
  139.0 0.1 multiply_bitcast_fusion
  139.1 0.0 copy-done.2
  139.1 0.1 multiply_convert_fusion
  139.2 30.5 %all_gather.14 = bf16[64,256]{0,1:T(8,128)(2,1)S(1)} all-gather(bf16[64,32]{0,1:T(8,128)(2,1)S(1)} %multiply_convert_fusion), channel_id=1, replica_groups=mesh['row'=4,'col'=8] {'col'}, dimensions={1}, use_global_device_ids=true | all-gather | bytes 36864 | tf_op jit(solution)/shard_map/all_gather | solution.py:76
  169.7 10.3 %psum.96 = bf16[64,128]{0,1:T(8,128)(2,1)S(1)} all-reduce(bf16[64,128]{0,1:T(8,128)(2,1)S(1)} %dynamic-slice_select_fusion.2), channel_id=1, replica_groups=mesh['row'=4,'col'=8] {'row'}, use_global_device_ids=true, to_apply=%region_10.11 | all-reduce | flops 8192 | bytes 32768 | tf_op jit(solution)/shard_map/psum | solution.py:11
  180.0 0.1 fusion.23
  180.1 0.8 convolution_convert_fusion.1
  181.0 0.0 reduce-scatter.3.cloned.1.call-update
  181.0 0.0 all-reduce.12.cloned.1.call-start
  181.0 10.7 %psum.97 = f32[64,128]{0,1:T(8,128)S(1)} all-reduce(f32[64,128]{0,1:T(8,128)S(1)} %fusion.23), channel_id=1, replica_groups=mesh['row'=4,'col'=8] {'row'}, use_global_device_ids=true, to_apply=%region_12.13 | all-reduce | flops 8192 | bytes 65536 | tf_op jit(solution)/shard_map/psum | solution.py:89
  191.8 0.7 broadcast_select_fusion.2
  192.4 0.0 all-reduce.12.cloned.1.call-update
  192.4 0.0 reduce-scatter.5.cloned.1.call-start
  192.5 46.2 %reduce-scatter.3.cloned.1.call-done = bf16[64,32]{0,1:T(8,128)(2,1)} async-done(((bf16[64,256]{0,1:T(8,128)(2,1)}), bf16[64,32]{0,1:T(8,128)(2,1)}) %reduce-scatter.3.cloned.1.call-update) | async-done | bytes 4112 | tf_op jit(solution)/shard_map/reduce_scatter | solution.py:86
  238.7 72.8 %all-reduce.12.cloned.1.call-done = (f32[64,128]{0,1:T(8,128)}, f32[64,128]{0,1:T(8,128)}) async-done(((f32[64,128]{0,1:T(8,128)}, f32[64,128]{0,1:T(8,128)}), (f32[64,128]{0,1:T(8,128)}, f32[64,128]{0,1:T(8,128)})) %all-reduce.12.cloned.1.call-update) | async-done | bytes 65552 | tf_op jit(solution)/shard_map/psum | solution.py:11
  311.5 0.8 fusion.9
  312.3 30.5 %all_gather.15 = bf16[64,256]{0,1:T(8,128)(2,1)S(1)} all-gather(bf16[64,32]{0,1:T(8,128)(2,1)S(1)} %fusion.9), channel_id=1, replica_groups=mesh['row'=4,'col'=8] {'col'}, dimensions={1}, use_global_device_ids=true | all-gather | bytes 36864 | tf_op jit(solution)/shard_map/all_gather | solution.py:76
  342.8 0.1 fusion.24
  343.0 10.3 %psum.100 = bf16[64,128]{0,1:T(8,128)(2,1)S(1)} all-reduce(bf16[64,128]{0,1:T(8,128)(2,1)S(1)} %dynamic-slice_select_fusion.1), channel_id=1, replica_groups=mesh['row'=4,'col'=8] {'row'}, use_global_device_ids=true, to_apply=%region_15.16 | all-reduce | flops 8192 | bytes 32768 | tf_op jit(solution)/shard_map/psum | solution.py:11
  353.3 0.8 convolution_convert_fusion
  354.1 0.0 reduce-scatter.5.cloned.1.call-update
  354.1 0.0 all-reduce.10.cloned.1.call-start
  354.2 11.8 %psum.101 = f32[64,128]{0,1:T(8,128)S(1)} all-reduce(f32[64,128]{0,1:T(8,128)S(1)} %fusion.24), channel_id=1, replica_groups=mesh['row'=4,'col'=8] {'row'}, use_global_device_ids=true, to_apply=%region_17.18 | all-reduce | flops 8192 | bytes 65536 | tf_op jit(solution)/shard_map/psum | solution.py:89
  366.0 0.7 broadcast_select_fusion.1
  366.6 0.0 all-reduce.10.cloned.1.call-update
  366.7 48.3 %reduce-scatter.5.cloned.1.call-done = bf16[64,32]{0,1:T(8,128)(2,1)} async-done(((bf16[64,256]{0,1:T(8,128)(2,1)}), bf16[64,32]{0,1:T(8,128)(2,1)}) %reduce-scatter.5.cloned.1.call-update) | async-done | bytes 4112 | tf_op jit(solution)/shard_map/reduce_scatter | solution.py:86
  415.0 72.3 %all-reduce.10.cloned.1.call-done = (f32[64,128]{0,1:T(8,128)}, f32[64,128]{0,1:T(8,128)}) async-done(((f32[64,128]{0,1:T(8,128)}, f32[64,128]{0,1:T(8,128)}), (f32[64,128]{0,1:T(8,128)}, f32[64,128]{0,1:T(8,128)})) %all-reduce.10.cloned.1.call-update) | async-done | bytes 65552 | tf_op jit(solution)/shard_map/psum | solution.py:11
  487.2 1.4 fusion.5
  (13 shorter events, 0.1 us)
Async XLA Ops:
  6.5 0.8 copy-start
  6.5 67.5 %all-reduce.8.cloned.1.call-start = ((), (), s32[]{:S(2)}) async-start(), calls=%async_computation.2 | async-start | bytes 393216 | tf_op jit(solution)/shard_map/psum | solution.py:11
  41.0 197.7 %reduce-scatter.3.cloned.1.call-start = ((), (), s32[]{:S(2)}) async-start(), calls=%async_computation.3 | async-start | bytes 73728 | tf_op jit(solution)/shard_map/reduce_scatter | solution.py:86
  41.2 0.7 copy-start.1
  42.5 0.7 copy-start.3
  44.2 0.7 copy-start.5
  46.1 0.7 copy-start.4
  114.0 25.1 %copy-start.2 = (f32[64,32]{0,1:T(8,128)S(1)}, f32[64,32]{0,1:T(8,128)}, u32[]{:S(2)}) copy-start(f32[64,32]{0,1:T(8,128)} %param.9) | copy-start | bytes 24580
  181.0 130.5 %all-reduce.12.cloned.1.call-start = ((), (), s32[]{:S(2)}) async-start(), calls=%async_computation.6 | async-start | bytes 262144 | tf_op jit(solution)/shard_map/psum | solution.py:11
  192.4 222.5 %reduce-scatter.5.cloned.1.call-start = ((), (), s32[]{:S(2)}) async-start(), calls=%async_computation.4 | async-start | bytes 73728 | tf_op jit(solution)/shard_map/reduce_scatter | solution.py:86
  354.1 133.1 %all-reduce.10.cloned.1.call-start = ((), (), s32[]{:S(2)}) async-start(), calls=%async_computation.5 | async-start | bytes 262144 | tf_op jit(solution)/shard_map/psum | solution.py:11
Sparse Core Ops, SparseCore 0:
  41.1 32.8 all-reduce.7
  181.1 57.5 reduce-scatter.2
  242.6 68.8 all-reduce.11
  354.3 60.6 reduce-scatter.4
  418.3 68.8 all-reduce.9
where the time goes:
time: 496 us; the launch traced here: 495 us
  waiting for transfers between devices  240 us (48%)
  blocking collectives  222 us (45%)
  between operations  14 us (3%)
  other arithmetic  10.2 us (2%)
  local copies, waits for them, and re-layouts  5.8 us (1%)
    psum x3, waiting for transfers between devices, spread(): return lax.psum(jnp.where(mine, shard, jnp.zeros_like(shard)), axis)  145 us
    reduce_scatter x2, waiting for transfers between devices, body(): lax.psum_scatter(row_part.astype(jnp.bfloat16), 'col', scatter_dimension=...  94.5 us
    all_gather x2, blocking collectives, body(): probe_rows = lax.all_gather(scaled, 'col', axis=1, tiled=True)  61 us
    psum x3, blocking collectives, spread(): return lax.psum(jnp.where(mine, shard, jnp.zeros_like(shard)), axis)  39.7 us
    all_gather x1, blocking collectives, body(): lax.all_gather(unit_vec, 'col', axis=0, tiled=True)  32.7 us
    psum x2, blocking collectives, body(): col_total = lax.psum(col_part, 'row')  22.5 us
    unnamed x1, blocking collectives  21.5 us
    pmax x1, blocking collectives, body(): row_top = lax.pmax(local_top, 'col')  21.3 us
  transfers between devices with their start and end apart: 5, of which 5 were waited for; matrix products, arithmetic and copies ran while one was open for 2% of the time, Pallas kernels for 0%

commit v1 on v0

v1 whole, which is shorter than its diff:
```python
import jax
import jax.numpy as jnp
from jax import lax
from jax.sharding import PartitionSpec as P

ITERS = 2
AXES = ("row", "col")
A2A_BYTES = 8 << 20
REPLICATE_CELLS = 1 << 21


def gather_rows(x, n_dev):
    if n_dev * x.size * x.dtype.itemsize <= A2A_BYTES:
        wide = jnp.broadcast_to(x[None], (n_dev,) + x.shape)
        return lax.all_to_all(wide, AXES, 0, 0, tiled=True)
    return lax.all_gather(x, AXES, axis=0, tiled=False)


def normalize(embed):
    values = embed.astype(jnp.float32)
    return (values * lax.rsqrt(jnp.mean(values * values, axis=1, keepdims=True) + 1e-06)).astype(
        jnp.bfloat16
    )


def pack_rows(flat, width):
    rows = -(-flat.shape[0] // width)
    return jnp.pad(flat, (0, rows * width - flat.shape[0])).reshape(rows, width), rows


def body(embed, beta, block_mask, counts, probes):
    n_dev = lax.axis_size("row") * lax.axis_size("col")
    n_row = lax.axis_size("row")
    me = lax.axis_index(AXES)
    shard, feat = embed.shape
    files = shard * n_dev
    nb = block_mask.shape[1]
    blk = files // nb
    local_blocks = block_mask.shape[0]

    unit_own = normalize(embed)
    beta_rows, beta_n = pack_rows(beta, feat)
    mask_rows, mask_n = pack_rows(block_mask.reshape(-1).astype(jnp.bfloat16), feat)
    replicate = files * files <= REPLICATE_CELLS
    if replicate:
        got = gather_rows(jnp.concatenate([unit_own, beta_rows, mask_rows], axis=0), n_dev)
        unit_all = got[:, :shard].reshape(files, feat)
        extra = got[:, shard:]
    else:
        unit_all = gather_rows(unit_own, n_dev).reshape(files, feat)
        extra = gather_rows(jnp.concatenate([beta_rows, mask_rows], axis=0), n_dev)
    beta_all = extra[:, 0, :shard].reshape(files)
    mask_got = extra[:, beta_n:, :].reshape(n_dev, -1)[:, : local_blocks * nb]
    per_row = n_dev // n_row
    mask_full = (
        mask_got.reshape(n_row, per_row, local_blocks, nb)[:, 0].reshape(nb, nb).astype(jnp.int32)
    )
    scale_all = beta_all.astype(jnp.float32) / feat

    col_ids = lax.iota(jnp.int32, files)
    col_block = col_ids // blk
    col_live = col_ids % blk < jnp.take(counts, col_block, axis=0)

    if replicate:
        probes_all = gather_rows(probes, n_dev)
        probes_all = jnp.transpose(probes_all, (1, 0, 2)).reshape(probes.shape[0], files)
        gram = lax.dot_general(
            unit_all, unit_all, (((1,), (1,)), ((), ())), preferred_element_type=jnp.float32
        )
        scores = gram * scale_all[:, None]
        block_ok = jnp.take(jnp.take(mask_full, col_block, axis=0), col_block, axis=1) == 1
        allowed = block_ok & col_live[None, :] & (col_ids[:, None] != col_ids[None, :])
        masked = jnp.where(allowed, scores, -1e30)
        row_top = jnp.max(masked, axis=1)
        row_mass = jnp.sum(jnp.where(allowed, jnp.exp(masked - row_top[:, None]), 0.0), axis=1)
        weights = jnp.where(allowed, jnp.exp(masked - row_top[:, None]) / row_mass[:, None], 0.0)
        col_mass = jnp.sum(weights, axis=0)
        inv_root = lax.rsqrt((1.0 + col_mass) * 0.5)
        affinity = weights.astype(jnp.bfloat16)
        state = probes_all
        for sweep in range(ITERS):
            scaled = (state * inv_root[None, :]).astype(jnp.bfloat16)
            row_part = lax.dot_general(
                scaled, affinity, (((1,), (1,)), ((), ())), preferred_element_type=jnp.float32
            )
            col_part = jnp.dot(scaled, affinity, preferred_element_type=jnp.float32)
            state = (row_part + col_part) * (0.5 * inv_root)[None, :]
        return lax.dynamic_slice_in_dim(state, me * shard, shard, 1)

    own_ids = me * shard + lax.iota(jnp.int32, shard)
    own_block = own_ids // blk
    gram = lax.dot_general(
        unit_own, unit_all, (((1,), (1,)), ((), ())), preferred_element_type=jnp.float32
    )
    own_scale = lax.dynamic_slice_in_dim(scale_all, me * shard, shard, 0)
    scores = gram * own_scale[:, None]
    row_ok = jnp.take(jnp.take(mask_full, own_block, axis=0), col_block, axis=1) == 1
    allowed = row_ok & col_live[None, :] & (own_ids[:, None] != col_ids[None, :])
    masked = jnp.where(allowed, scores, -1e30)
    row_top = jnp.max(masked, axis=1)
    row_mass = jnp.sum(jnp.where(allowed, jnp.exp(masked - row_top[:, None]), 0.0), axis=1)
    weights = jnp.where(allowed, jnp.exp(masked - row_top[:, None]) / row_mass[:, None], 0.0)
    stats = gather_rows(jnp.stack([row_top, row_mass], axis=1), n_dev).reshape(files, 2)
    top_all, mass_all = stats[:, 0], stats[:, 1]
    scores_t = gram * scale_all[None, :]
    own_live = jnp.take(col_live, own_ids, axis=0)
    col_ok = jnp.take(jnp.take(mask_full, col_block, axis=0), own_block, axis=1).T == 1
    allowed_t = col_ok & own_live[:, None] & (own_ids[:, None] != col_ids[None, :])
    masked_t = jnp.where(allowed_t, scores_t, -1e30)
    weights_t = jnp.where(
        allowed_t, jnp.exp(masked_t - top_all[None, :]) / mass_all[None, :], 0.0
    )
    col_mass = jnp.sum(weights_t, axis=1)
    inv_root = lax.rsqrt((1.0 + col_mass) * 0.5)
    aff_rows = weights.astype(jnp.bfloat16)
    aff_cols = weights_t.astype(jnp.bfloat16)
    state = probes
    for sweep in range(ITERS):
        scaled = (state * inv_root[None, :]).astype(jnp.bfloat16)
        scaled_all = gather_rows(scaled.T, n_dev).reshape(files, probes.shape[0])
        row_part = jnp.dot(aff_rows, scaled_all, preferred_element_type=jnp.float32)
        col_part = jnp.dot(aff_cols, scaled_all, preferred_element_type=jnp.float32)
        state = ((row_part + col_part) * (0.5 * inv_root)[:, None]).T
    return state


def solution(mesh):
    placed = (
        P(AXES, None),
        P(AXES),
        P("row", None),
        P(),
        P(None, AXES),
    )
    return jax.shard_map(body, mesh=mesh, in_specs=placed, out_specs=P(None, AXES), check_vma=False)
```

time: 496 us -> 92 us (0.19)
  blocking collectives: 222 us -> 0 us
  waiting for transfers between devices: 240 us -> 46.7 us
  between operations: 14 us -> 0.21 us
  starting transfers between devices: 0.17 us -> 10 us
  local copies, waits for them, and re-layouts: 5.8 us -> 15.2 us
    psum x3 -> x0, waiting for transfers between devices: 145 us -> none  [spread(): return lax.psum(jnp.where(mine, shard, jnp.zeros_like(shard)), axis)]
    reduce_scatter x2 -> x0, waiting for transfers between devices: 94.5 us -> none  [body(): lax.psum_scatter(row_part.astype(jnp.bfloat16), 'col', scatter_dimension=...]
    all_gather x3 -> x0, blocking collectives: 93.7 us -> none  [the longest x2 61 us: body(): probe_rows = lax.all_gather(scaled, 'col', axis=1, tiled=True)]
    psum x7 -> x0, blocking collectives: 85.2 us -> none  [the longest x3 39.7 us: spread(): return lax.psum(jnp.where(mine, shard, jnp.zeros_like(shard)), axis)]
    all_to_all x0 -> x2, waiting for transfers between devices: none -> 46.7 us  [gather_rows(): return lax.all_to_all(wide, AXES, 0, 0, tiled=True)]
    unnamed x1 -> x0, blocking collectives: 21.5 us -> none
    pmax x1 -> x0, blocking collectives: 21.3 us -> none  [body(): row_top = lax.pmax(local_top, 'col')]
    all_to_all x0 -> x2, starting transfers between devices: none -> 10 us  [gather_rows(): return lax.all_to_all(wide, AXES, 0, 0, tiled=True)]
  transfers between devices with their start and end apart: 5 -> 2, of which waited for: 5 -> 2; matrix products, arithmetic and copies ran while one was open for 2% -> 12% of each run, Pallas kernels for 0% -> 0%
where the time goes in v1:
time: 92 us; the launch traced here: 91.5 us
  waiting for transfers between devices  46.7 us (51%)
  local copies, waits for them, and re-layouts  15.2 us (17%)
  other arithmetic  11.9 us (13%)
  starting transfers between devices  10 us (11%)
  matrix products  7.47 us (8%)
    all_to_all x2, waiting for transfers between devices, gather_rows(): return lax.all_to_all(wide, AXES, 0, 0, tiled=True)  46.7 us
    all_to_all x2, starting transfers between devices, gather_rows(): return lax.all_to_all(wide, AXES, 0, 0, tiled=True)  10 us
    gather x1, local copies, waits for them, and re-layouts, body(): jnp.take(jnp.take(mask_full, col_block, axis=0), col_block, axis=1) == 1  5.44 us
    lt x1, other arithmetic, body(): col_live = col_ids % blk < jnp.take(counts, col_block, axis=0)  5.05 us
    dot_general x1, matrix products, body(): lax.dot_general(unit_all, unit_all, (((1,), (1,)), ((), ())), preferred_e...  4.97 us
    gather x1, local copies, waits for them, and re-layouts, body(): jnp.take(mask_full, col_block, axis=0)  2.81 us
    unnamed x8, local copies, waits for them, and re-layouts  2.01 us
  transfers between devices with their start and end apart: 2, of which 2 were waited for; matrix products, arithmetic and copies ran while one was open for 12% of the time, Pallas kernels for 0%

profile of v1, /device:TPU:0, one launch (start us, length us, event | category | flops | bytes accessed | tf_op | source)
XLA Modules:
  0.0 91.5 jit_solution(1437012608915364856)
XLA Ops:
  0.0 0.0 copy-start
  0.0 0.7 copy-done
  0.7 0.0 copy-start.1
  0.8 1.0 %reshape.175 = f32[32,1,2048]{2,1,0:T(1,128)} reshape(f32[32,32,64]{2,1,0:T(8,128)S(1)} %broadcast_bitcast_fusion) | data formatting | bytes 524288
  1.8 7.3 %all-to-all-start = ((f32[32,1,2048]{2,1,0:T(1,128)}), f32[32,1,2048]{2,1,0:T(1,128)S(1)}, u32[]{:S(2)}, u32[]{:S(2)}) async-start(f32[32,1,2048]{2,1,0:T(1,128)} %reshape.175), calls=%async_computation | async-start | bytes 524288 | tf_op jit(solution)/shard_map/all_to_all | solution.py:15
  9.1 0.7 convert_element_type.41
  9.8 0.1 convert_element_type.42
  9.9 0.9 fusion.7
  10.8 0.7 pad.8
  11.5 0.9 fusion.8
  12.4 7.4 %all-to-all-done = f32[32,1,2048]{2,1,0:T(1,128)S(1)} async-done(((f32[32,1,2048]{2,1,0:T(1,128)}), f32[32,1,2048]{2,1,0:T(1,128)S(1)}, u32[]{:S(2)}, u32[]{:S(2)}) %all-to-all-start) | async-done | bytes 262176 | tf_op jit(solution)/shard_map/all_to_all | solution.py:15
  19.7 1.4 %broadcast_in_dim.61 = bf16[32,34,768]{2,1,0:T(8,128)(2,1)} broadcast(bf16[34,768]{1,0:T(8,128)(2,1)S(1)} %pad_maximum_fusion), dimensions={1,2} | broadcast | bytes 1723392 | tf_op jit(solution)/shard_map/broadcast_in_dim | solution.py:14
  21.2 2.7 %all-to-all-start.1 = ((bf16[32,34,768]{2,1,0:T(8,128)(2,1)}), bf16[32,34,768]{2,1,0:T(8,128)(2,1)S(1)}, u32[]{:S(2)}, u32[]{:S(2)}) async-start(bf16[32,34,768]{2,1,0:T(8,128)(2,1)} %broadcast_in_dim.61), calls=%async_computation.1 | async-start | bytes 3932160 | tf_op jit(solution)/shard_map/all_to_all | solution.py:15
  23.9 0.0 copy-done.1
  23.9 0.7 fusion.27
  24.6 5.1 %fusion.19 = (pred[1024]{0:T(1024)(128)(4,1)S(1)}, pred[1024]{0:T(1024)(128)(4,1)S(1)}) fusion(s32[1024]{0:T(1024)S(1)} %bitcast.37, s32[]{:T(128)} %bitcast.5, s32[]{:T(128)} %bitcast.6, s32[]{:T(128)} %bitcast.7, s32[]{:T(128)} %bitcast.8, s32[]{:T(128)} %bitcast.9, s32[]{:T(128)} %bitcast.10, s32[]{:T(128)} %bitcast.11, s32[]{:T(128)} %bitcast.12), kind=kLoop, calls=%fused_computation.46 | loop fusion | flops 34816 | bytes 6176 | tf_op jit(solution)/shard_map/lt | solution.py:62
  29.7 0.5 broadcast.264
  30.2 1.3 %reduce.4 = f32[32,2048]{1,0:T(8,128)S(1)} reduce(f32[32,1,2048]{2,1,0:T(1,128)S(1)} %all-to-all-done, f32[]{:T(128)} %broadcast.264), dimensions={1}, to_apply=%all_to_all.6.reduce_sub_computation | reduce | bytes 524292 | tf_op jit(solution)/shard_map/all_to_all | solution.py:15
  31.5 0.2 reshape.176
  31.7 0.2 copy.39
  31.9 39.3 %all-to-all-done.1 = bf16[32,34,768]{2,1,0:T(8,128)(2,1)S(1)} async-done(((bf16[32,34,768]{2,1,0:T(8,128)(2,1)}), bf16[32,34,768]{2,1,0:T(8,128)(2,1)S(1)}, u32[]{:S(2)}, u32[]{:S(2)}) %all-to-all-start.1) | async-done | bytes 1671200 | tf_op jit(solution)/shard_map/all_to_all | solution.py:15
  71.2 0.1 fusion.12
  71.2 0.1 div.50
  71.3 0.1 slice.36
  71.4 0.1 reshape.167
  71.5 2.8 %gather_fusion = s32[1024,8]{1,0:T(8,128)S(1)} fusion(s32[8,8]{1,0:T(8,128)S(1)} %bitcast.33, s32[1024]{0:T(1024)S(1)} %broadcast_clamp_fusion), kind=kCustom, calls=%fused_computation | custom fusion | bytes 69632 | tf_op jit(solution)/shard_map/jit(_take)/gather | solution.py:71
  74.4 0.2 broadcast_select_fusion
  74.6 0.2 copy.38
  74.7 5.4 %gather_fusion.1 = s32[1024,1024]{1,0:T(8,128)} fusion(s32[1024,8]{0,1:T(8,128)S(1)} %copy.38, s32[1024]{0:T(1024)S(1)} %broadcast_clamp_fusion), kind=kCustom, calls=%fused_computation.1 | custom fusion | bytes 8392704 | tf_op jit(solution)/shard_map/jit(_take)/gather | solution.py:71
  80.2 0.2 slice.39
  80.3 5.0 %fusion.3 = (f32[1024]{0:T(1024)S(1)}, pred[1024,1024]{0,1:T(8,128)(4,1)S(1)}, f32[1024,1024]{0,1:T(8,128)S(1)}) fusion(f32[1024]{0:T(1024)S(1)} %div.50, pred[1024]{0:T(1024)(128)(4,1)S(1)} %get-tuple-element.20, s32[1024,1024]{1,0:T(8,128)} %gather_fusion.1, pred[1024]{0:T(1024)(128)(4,1)S(1)} %get-tuple-element.21, bf16[1024,768]{1,0:T(8,128)(2,1)S(1)} %bitcast.35), kind=kOutput, calls=%fused_computation.11 | convolution fusion | flops 1619000320 | bytes 11020288 | tf_op jit(solution)/shard_map/dot_general | solution.py:67
  85.3 1.2 %select_reduce_fusion = f32[1024]{0:T(1024)S(1)} fusion(pred[1024,1024]{0,1:T(8,128)(4,1)S(1)} %get-tuple-element.6, f32[1024,1024]{0,1:T(8,128)S(1)} %get-tuple-element.19, f32[1024]{0:T(1024)S(1)} %get-tuple-element.5, f32[1024]{0:T(1024)S(1)} %div.50), kind=kLoop, calls=%fused_computation.4 | loop fusion | flops 5241856 | bytes 5255168 | tf_op jit(solution)/shard_map/reduce_sum | solution.py:75
  86.6 1.5 %fusion.25 = (f32[1024]{0:T(1024)S(1)}, bf16[1024,1024]{0,1:T(8,128)(2,1)S(1)}) fusion(pred[1024,1024]{0,1:T(8,128)(4,1)S(1)} %get-tuple-element.6, f32[1024]{0:T(1024)S(1)} %select_reduce_fusion, f32[1024]{0:T(1024)S(1)} %get-tuple-element.5, f32[1024,1024]{0,1:T(8,128)S(1)} %get-tuple-element.19, f32[1024]{0:T(1024)S(1)} %div.50), kind=kLoop, calls=%fused_computation.58 | loop fusion | flops 7339008 | bytes 7356416 | tf_op jit(solution)/shard_map/reduce_sum | solution.py:77
  88.1 0.5 fusion.9
  88.6 0.8 fusion.6
  89.4 0.8 fusion.29
  90.1 0.5 fusion.28
  90.6 0.1 dynamic-slice
  90.7 0.1 fusion.10
  90.8 0.7 copy.42
  (14 shorter events, 0.1 us)
Async XLA Ops:
  0.0 0.7 copy-start
  0.7 23.2 %copy-start.1 = (s32[8]{0:T(128)S(1)}, s32[8]{0:T(128)}, u32[]{:S(2)}) copy-start(s32[8]{0:T(128)} %param.8) | copy-start | bytes 100
  1.8 18.0 %all-to-all-start = ((f32[32,1,2048]{2,1,0:T(1,128)}), f32[32,1,2048]{2,1,0:T(1,128)S(1)}, u32[]{:S(2)}, u32[]{:S(2)}) async-start(f32[32,1,2048]{2,1,0:T(1,128)} %reshape.175), calls=%async_computation | async-start | bytes 524288 | tf_op jit(solution)/shard_map/all_to_all | solution.py:15
  21.2 50.0 %all-to-all-start.1 = ((bf16[32,34,768]{2,1,0:T(8,128)(2,1)}), bf16[32,34,768]{2,1,0:T(8,128)(2,1)S(1)}, u32[]{:S(2)}, u32[]{:S(2)}) async-start(bf16[32,34,768]{2,1,0:T(8,128)(2,1)} %broadcast_in_dim.61), calls=%async_computation.1 | async-start | bytes 3932160 | tf_op jit(solution)/shard_map/all_to_all | solution.py:15

commit v2 on v1

--- a/solution.py
+++ b/solution.py
@@ -16,11 +16,41 @@
     return lax.all_gather(x, AXES, axis=0, tiled=False)
 
 
+def gather_halves(x, n_dev, n_row):
+    if n_row % 2:
+        return gather_rows(x, n_dev)
+    rows = x.shape[0] + x.shape[0] % 2
+    halves = jnp.pad(x, ((0, rows - x.shape[0]), (0, 0))).reshape(2, rows // 2, x.shape[1])
+    per_row = n_dev // n_row
+    wide = jnp.broadcast_to(
+        halves[None, :, None], (n_row // 2, 2, per_row, rows // 2, x.shape[1])
+    ).reshape(n_dev, rows // 2, x.shape[1])
+    mine = lax.all_to_all(wide, AXES, 0, 0, tiled=True)
+    other = lax.ppermute(mine, "row", [(r, r ^ 1) for r in range(n_row)])
+    first = lax.axis_index("row") % 2 == 0
+    low = jnp.where(first, mine, other)
+    high = jnp.where(first, other, mine)
+    return jnp.concatenate([low, high], axis=1)[:, : x.shape[0]]
+
+
 def normalize(embed):
     values = embed.astype(jnp.float32)
     return (values * lax.rsqrt(jnp.mean(values * values, axis=1, keepdims=True) + 1e-06)).astype(
         jnp.bfloat16
     )
+
+
+def split3(x):
+    hi = lax.reduce_precision(x, exponent_bits=8, mantissa_bits=7)
+    rest = x - hi
+    mid = lax.reduce_precision(rest, exponent_bits=8, mantissa_bits=7)
+    lo = rest - mid
+    return jnp.stack([hi, mid, lo]).astype(jnp.bfloat16)
+
+
+def join3(parts):
+    parts = parts.astype(jnp.float32)
+    return (parts[0] + parts[1]) + parts[2]
 
 
 def pack_rows(flat, width):
@@ -43,9 +73,15 @@
     mask_rows, mask_n = pack_rows(block_mask.reshape(-1).astype(jnp.bfloat16), feat)
     replicate = files * files <= REPLICATE_CELLS
     if replicate:
-        got = gather_rows(jnp.concatenate([unit_own, beta_rows, mask_rows], axis=0), n_dev)
+        probe_rows, probe_n = pack_rows(split3(probes).reshape(-1), feat)
+        payload = jnp.concatenate([unit_own, beta_rows, mask_rows, probe_rows], axis=0)
+        got = gather_halves(payload, n_dev, n_row)
         unit_all = got[:, :shard].reshape(files, feat)
-        extra = got[:, shard:]
+        extra = got[:, shard : shard + beta_n + mask_n]
+        probe_parts = got[:, shard + beta_n + mask_n :].reshape(n_dev, -1)[:, : 3 * probes.size]
+        probe_parts = probe_parts.reshape(n_dev, 3, probes.shape[0], shard)
+        probes_all = jnp.transpose(join3(jnp.moveaxis(probe_parts, 1, 0)), (1, 0, 2))
+        probes_all = probes_all.reshape(probes.shape[0], files)
     else:
         unit_all = gather_rows(unit_own, n_dev).reshape(files, feat)
         extra = gather_rows(jnp.concatenate([beta_rows, mask_rows], axis=0), n_dev)
@@ -59,16 +95,17 @@
 
     col_ids = lax.iota(jnp.int32, files)
     col_block = col_ids // blk
-    col_live = col_ids % blk < jnp.take(counts, col_block, axis=0)
+    in_block = lax.iota(jnp.int32, blk)
+    col_live = (in_block[None, :] < counts[:, None]).reshape(files)
 
     if replicate:
-        probes_all = gather_rows(probes, n_dev)
-        probes_all = jnp.transpose(probes_all, (1, 0, 2)).reshape(probes.shape[0], files)
         gram = lax.dot_general(
             unit_all, unit_all, (((1,), (1,)), ((), ())), preferred_element_type=jnp.float32
         )
         scores = gram * scale_all[:, None]
-        block_ok = jnp.take(jnp.take(mask_full, col_block, axis=0), col_block, axis=1) == 1
+        block_ok = jnp.broadcast_to(
+            (mask_full == 1)[:, None, :, None], (nb, blk, nb, blk)
+        ).reshape(files, files)
         allowed = block_ok & col_live[None, :] & (col_ids[:, None] != col_ids[None, :])
         masked = jnp.where(allowed, scores, -1e30)
         row_top = jnp.max(masked, axis=1)

time: 92 us -> 69.8 us (0.76)
  waiting for transfers between devices: 46.7 us -> 2.65 us
  blocking collectives: 0 us -> 37.5 us
  starting transfers between devices: 10 us -> 0.07 us
  local copies, waits for them, and re-layouts: 15.2 us -> 9.77 us
    all_to_all x2 -> x0, waiting for transfers between devices: 46.7 us -> none  [gather_rows(): return lax.all_to_all(wide, AXES, 0, 0, tiled=True)]
    all_to_all x0 -> x1, blocking collectives: none -> 37.5 us  [gather_halves(): mine = lax.all_to_all(wide, AXES, 0, 0, tiled=True)]
    all_to_all x2 -> x0, starting transfers between devices: 10 us -> none  [gather_rows(): return lax.all_to_all(wide, AXES, 0, 0, tiled=True)]
    gather x3 -> x0, local copies, waits for them, and re-layouts: 8.93 us -> none  [the longest x1 5.44 us: body(): jnp.take(jnp.take(mask_full, col_block, axis=0), col_block, axis=1) == 1]
    lt x1, other arithmetic: 5.05 us -> 0.07 us  [body(): col_live = (in_block[None, :] < counts[:, None]).reshape(files)]
    convert_element_type x1 -> x3, local copies, waits for them, and re-layouts: 0.01 us -> 3.46 us  [the longest x2 3.36 us: join3(): parts = parts.astype(jnp.float32)]
    ppermute x0 -> x1, waiting for transfers between devices: none -> 2.65 us  [gather_halves(): other = lax.ppermute(mine, 'row', [(r, r ^ 1) for r in range(n_row)])]
    unnamed x8 -> x2, local copies, waits for them, and re-layouts: 2.01 us -> 0.01 us
  transfers between devices with their start and end apart: 2 -> 1, of which waited for: 2 -> 1; matrix products, arithmetic and copies ran while one was open for 12% -> 0% of each run, Pallas kernels for 0% -> 0%
where the time goes in v2:
time: 69.8 us; the launch traced here: 69.4 us
  blocking collectives  37.5 us (54%)
  other arithmetic  12 us (17%)
  local copies, waits for them, and re-layouts  9.77 us (14%)
  matrix products  7.24 us (10%)
  waiting for transfers between devices  2.65 us (4%)
    all_to_all x1, blocking collectives, gather_halves(): mine = lax.all_to_all(wide, AXES, 0, 0, tiled=True)  37.5 us
    dot_general x1, matrix products, body(): lax.dot_general(unit_all, unit_all, (((1,), (1,)), ((), ())), preferred_e...  4.73 us
    convert_element_type x2, local copies, waits for them, and re-layouts, join3(): parts = parts.astype(jnp.float32)  3.36 us
    reduce_sum x1, other arithmetic, body(): col_mass = jnp.sum(weights, axis=0)  2.93 us
    reduce_sum x1, other arithmetic, body(): jnp.sum(jnp.where(allowed, jnp.exp(masked - row_top[:, None]), 0.0), axis=1)  2.7 us
    ppermute x1, waiting for transfers between devices, gather_halves(): other = lax.ppermute(mine, 'row', [(r, r ^ 1) for r in range(n_row)])  2.65 us
    slice x1, local copies, waits for them, and re-layouts, body(): unit_all = got[:, :shard].reshape(files, feat)  2.02 us
    transpose x1, local copies, waits for them, and re-layouts, body(): jnp.transpose(join3(jnp.moveaxis(probe_parts, 1, 0)), (1, 0, 2))  1.54 us
  transfers between devices with their start and end apart: 1, of which 1 were waited for; matrix products, arithmetic and copies ran while one was open for 0% of the time, Pallas kernels for 0%

profile of v2, /device:TPU:0, one launch (start us, length us, event | category | flops | bytes accessed | tf_op | source)
XLA Modules:
  0.0 69.4 jit_solution(4651644225375421564)
XLA Ops:
  0.0 0.0 copy-start
  0.0 0.7 %convert_element_type.57 = bf16[2,8]{1,0:T(2,128)(2,1)S(1)} convert(s32[2,8]{1,0:T(2,128)} %param.7) | non-fusion elementwise | flops 16 | bytes 96 | tf_op jit(solution)/shard_map/convert_element_type | solution.py:73
  0.7 0.1 convert_element_type.58
  0.8 0.9 %fusion.6 = f32[32]{0:T(128)S(1)} fusion(bf16[32,768]{1,0:T(8,128)(2,1)} %param.5), kind=kLoop, calls=%fused_computation.22 | loop fusion | flops 73696 | bytes 49280 | tf_op jit(solution)/shard_map/reduce_sum | solution.py:38
  1.7 0.7 pad.8
  2.4 0.7 %fusion.12 = (bf16[1,64,32]{1,2,0:T(8,128)(2,1)S(1)}, bf16[1,64,32]{1,2,0:T(8,128)(2,1)S(1)}, bf16[1,64,32]{1,2,0:T(8,128)(2,1)S(1)}) fusion(f32[64,32]{0,1:T(8,128)} %param.9), kind=kLoop, calls=%fused_computation.37 | loop fusion | flops 14336 | bytes 20480 | tf_op jit(solution)/shard_map/stack | solution.py:48
  3.1 0.1 copy.47
  3.2 0.1 convert_element_type.59
  3.4 0.9 %fusion.7 = bf16[32,768]{1,0:T(8,128)(2,1)S(1)} fusion(bf16[32,768]{1,0:T(8,128)(2,1)} %param.5, f32[32]{0:T(128)S(1)} %add_rsqrt_fusion), kind=kLoop, calls=%fused_computation.23 | loop fusion | flops 73728 | bytes 98432 | tf_op jit(solution)/shard_map/convert_element_type | solution.py:38
  4.3 0.1 broadcast_in_dim.15
  4.4 37.5 %all_to_all.5 = bf16[32,21,768]{2,1,0:T(8,128)(2,1)S(1)} all-to-all(bf16[32,21,768]{2,1,0:T(8,128)(2,1)S(1)} %bitcast.50), channel_id=1, replica_groups=mesh['row'=4,'col'=8] {'row','col'}, dimensions={0} | all-to-all | bytes 2064384 | tf_op jit(solution)/shard_map/all_to_all | solution.py:28
  41.9 0.2 copy.48
  42.1 0.1 collective-permute-start
  42.2 0.0 copy-done
  42.2 0.1 fusion.14
  42.3 2.7 %collective-permute-done = bf16[32,21,768]{2,0,1:T(8,128)(2,1)} collective-permute-done((bf16[32,21,768]{2,0,1:T(8,128)(2,1)S(1)}, bf16[32,21,768]{2,0,1:T(8,128)(2,1)}, u32[]{:S(2)}, u32[]{:S(2)}) %collective-permute-start) | collective-permute-done | bytes 1032224 | tf_op jit(solution)/shard_map/ppermute | solution.py:29
  44.9 1.5 %broadcast_select_fusion = (bf16[32,21,768]{2,0,1:T(8,128)(2,1)S(1)}, bf16[32,21,768]{2,0,1:T(8,128)(2,1)S(1)}) fusion(bf16[32,21,768]{2,0,1:T(8,128)(2,1)} %collective-permute-done, pred[]{:T(512)S(6)} %eq.18, bf16[32,21,768]{2,1,0:T(8,128)(2,1)S(1)} %all_to_all.5), kind=kLoop, calls=%fused_computation.16 | loop fusion | flops 1032192 | bytes 4128769 | tf_op jit(solution)/shard_map/jit(_where)/select_n | solution.py:31
  46.4 0.1 slice_convert_fusion
  46.5 0.1 div.26
  46.6 0.1 reshape.96
  46.7 0.1 copy.55
  46.8 0.1 pad_maximum_fusion
  46.9 1.3 %copy.50 = f32[32,8,768]{2,1,0:T(8,128)} copy(f32[32,8,768]{2,0,1:T(8,128)S(1)} %slice_convert_fusion) | data formatting | bytes 1572864 | tf_op jit(solution)/shard_map/convert_element_type | solution.py:52
  48.3 2.0 %copy.57 = bf16[32,32,768]{2,1,0:T(8,128)(2,1)} copy(bf16[32,32,768]{2,0,1:T(8,128)(2,1)S(1)} %pad_maximum_fusion) | data formatting | bytes 3145728 | tf_op jit(solution)/shard_map/slice | solution.py:79
  50.3 2.0 %reshape.95 = f32[32,3,64,32]{3,2,1,0:T(8,128)S(1)} reshape(f32[32,8,768]{2,1,0:T(8,128)} %copy.50) | data formatting | bytes 1572864 | tf_op jit(solution)/shard_map/convert_element_type | solution.py:52
  52.3 1.2 %fusion.5 = f32[64,32,32]{2,0,1:T(8,128)} fusion(f32[3,32,64,32]{3,2,0,1:T(8,128)S(1)} %bitcast.46), kind=kLoop, calls=%fused_computation.14 | loop fusion | flops 131072 | bytes 1048576 | tf_op jit(solution)/shard_map/transpose | solution.py:83
  53.5 1.5 %copy.51 = f32[64,32,32]{0,2,1:T(8,128)S(1)} copy(f32[64,32,32]{2,0,1:T(8,128)} %fusion.5) | data formatting | bytes 524288 | tf_op jit(solution)/shard_map/transpose | solution.py:83
  55.1 0.2 copy.58
  55.3 0.3 broadcast_in_dim.16
  55.6 4.7 %fusion.1 = (f32[1024]{0:T(1024)S(1)}, f32[1024,1024]{0,1:T(8,128)S(1)}) fusion(f32[1024]{0:T(1024)S(1)} %div.26, pred[1024]{0:T(1024)(128)(4,1)S(1)} %fusion.14, pred[128,8,8,128]{3,2,1,0:T(8,128)(4,1)S(1)} %bitcast.47, bf16[1024,768]{1,0:T(8,128)(2,1)} %bitcast.52), kind=kOutput, calls=%fused_computation.7 | convolution fusion | flops 1616903168 | bytes 6824960 | tf_op jit(solution)/shard_map/dot_general | solution.py:102
  60.4 2.7 %select_reduce_fusion = f32[1024]{0:T(1024)S(1)} fusion(f32[1024,1024]{0,1:T(8,128)S(1)} %get-tuple-element.15, f32[1024]{0:T(1024)S(1)} %get-tuple-element.14, f32[1024]{0:T(1024)S(1)} %div.26, pred[1024]{0:T(1024)(128)(4,1)S(1)} %fusion.14, pred[128,8,8,128]{3,2,1,0:T(8,128)(4,1)S(1)} %bitcast.48), kind=kLoop, calls=%fused_computation.1 | loop fusion | flops 8387584 | bytes 5256192 | tf_op jit(solution)/shard_map/reduce_sum | solution.py:112
  63.1 2.9 %fusion.16 = (f32[1024]{0:T(1024)S(1)}, bf16[1024,1024]{0,1:T(8,128)(2,1)S(1)}) fusion(f32[1024]{0:T(1024)S(1)} %select_reduce_fusion, f32[1024]{0:T(1024)S(1)} %get-tuple-element.14, f32[1024,1024]{0,1:T(8,128)S(1)} %get-tuple-element.15, f32[1024]{0:T(1024)S(1)} %div.26, pred[1024]{0:T(1024)(128)(4,1)S(1)} %fusion.14, pred[128,8,8,128]{3,2,1,0:T(8,128)(4,1)S(1)} %bitcast.49), kind=kLoop, calls=%fused_computation.46 | loop fusion | flops 10484736 | bytes 7357440 | tf_op jit(solution)/shard_map/reduce_sum | solution.py:114
  66.0 0.5 fusion.8
  66.5 0.8 %fusion.4 = bf16[64,1024]{1,0:T(8,128)(2,1)S(1)} fusion(f32[64,1024]{1,0:T(8,128)S(1)} %fusion.8, bf16[1024,1024]{0,1:T(8,128)(2,1)S(1)} %get-tuple-element.6, f32[1024]{0:T(1024)S(1)} %get-tuple-element.12, f32[1024]{0:T(1024)S(1)} %get-tuple-element.13, f32[64,1024]{1,0:T(8,128)S(1)} %copy.58), kind=kOutput, calls=%fused_computation.12 | convolution fusion | flops 134610944 | bytes 2760704 | tf_op jit(solution)/shard_map/dot_general | solution.py:123
  67.3 0.8 %fusion.18 = f32[64,1024]{1,0:T(8,128)S(1)} fusion(bf16[64,1024]{1,0:T(8,128)(2,1)S(1)} %fusion.4, bf16[1024,1024]{0,1:T(8,128)(2,1)S(1)} %get-tuple-element.6), kind=kOutput, calls=%fused_computation.48 | convolution fusion | flops 134217728 | bytes 2490368 | tf_op jit(solution)/shard_map/dot_general | solution.py:123
  68.1 0.5 fusion.17
  68.6 0.1 dynamic-slice
  68.6 0.1 fusion.9
  68.7 0.7 copy.61
  (15 shorter events, 0.1 us)
Async XLA Ops:
  0.0 42.2 %copy-start = (s32[8]{0:T(128)S(1)}, s32[8]{0:T(128)}, u32[]{:S(2)}) copy-start(s32[8]{0:T(128)} %param.8) | copy-start | bytes 100
  42.1 2.8 %collective-permute-start = (bf16[32,21,768]{2,0,1:T(8,128)(2,1)S(1)}, bf16[32,21,768]{2,0,1:T(8,128)(2,1)}, u32[]{:S(2)}, u32[]{:S(2)}) collective-permute-start(bf16[32,21,768]{2,0,1:T(8,128)(2,1)S(1)} %copy.48), channel_id=1, source_target_pairs={{0,8},{8,0},{16,24},{24,16},{1,9},{9,1},{17,25},{25,17},{2,10},{10... | collective-permute-start | bytes 3096584 | tf_op jit(solution)/shard_map/ppermute | solution.py:29

commit v3 on v2

--- a/solution.py
+++ b/solution.py
@@ -73,20 +73,31 @@
     mask_rows, mask_n = pack_rows(block_mask.reshape(-1).astype(jnp.bfloat16), feat)
     replicate = files * files <= REPLICATE_CELLS
     if replicate:
-        probe_rows, probe_n = pack_rows(split3(probes).reshape(-1), feat)
-        payload = jnp.concatenate([unit_own, beta_rows, mask_rows, probe_rows], axis=0)
-        got = gather_halves(payload, n_dev, n_row)
-        unit_all = got[:, :shard].reshape(files, feat)
-        extra = got[:, shard : shard + beta_n + mask_n]
-        probe_parts = got[:, shard + beta_n + mask_n :].reshape(n_dev, -1)[:, : 3 * probes.size]
+        extra_flat = jnp.concatenate(
+            [
+                beta,
+                block_mask.reshape(-1).astype(jnp.bfloat16),
+                split3(probes).reshape(-1),
+            ]
+        )
+        lanes = -(-extra_flat.shape[0] // (shard * 128)) * 128
+        extra_cols = jnp.pad(extra_flat, (0, shard * lanes - extra_flat.shape[0])).reshape(
+            shard, lanes
+        )
+        got = gather_halves(jnp.concatenate([unit_own, extra_cols], axis=1), n_dev, n_row)
+        unit_all = got[:, :, :feat].reshape(files, feat)
+        tail = got[:, :, feat:].reshape(n_dev, shard * lanes)
+        beta_all = tail[:, :shard].reshape(files)
+        mask_got = tail[:, shard : shard + local_blocks * nb]
+        probe_parts = tail[:, shard + local_blocks * nb : shard + local_blocks * nb + 3 * probes.size]
         probe_parts = probe_parts.reshape(n_dev, 3, probes.shape[0], shard)
         probes_all = jnp.transpose(join3(jnp.moveaxis(probe_parts, 1, 0)), (1, 0, 2))
         probes_all = probes_all.reshape(probes.shape[0], files)
     else:
         unit_all = gather_rows(unit_own, n_dev).reshape(files, feat)
         extra = gather_rows(jnp.concatenate([beta_rows, mask_rows], axis=0), n_dev)
-    beta_all = extra[:, 0, :shard].reshape(files)
-    mask_got = extra[:, beta_n:, :].reshape(n_dev, -1)[:, : local_blocks * nb]
+        beta_all = extra[:, 0, :shard].reshape(files)
+        mask_got = extra[:, beta_n:, :].reshape(n_dev, -1)[:, : local_blocks * nb]
     per_row = n_dev // n_row
     mask_full = (
         mask_got.reshape(n_row, per_row, local_blocks, nb)[:, 0].reshape(nb, nb).astype(jnp.int32)

time: 69.8 us -> 64.7 us (0.927)
  local copies, waits for them, and re-layouts: 9.77 us -> 6.76 us
  blocking collectives: 37.5 us -> 34.7 us
  other arithmetic: 12 us -> 13.5 us
  waiting for transfers between devices: 2.65 us -> 1.93 us
    all_to_all x1, blocking collectives: 37.5 us -> 34.7 us  [gather_halves(): mine = lax.all_to_all(wide, AXES, 0, 0, tiled=True)]
    slice x2 -> x1, local copies, waits for them, and re-layouts: 2.02 us -> 0.08 us  [body(): mask_got = tail[:, shard:shard + local_blocks * nb]]
    select_n x1, other arithmetic: 1.47 us -> 0.14 us  [gather_halves(): low = jnp.where(first, mine, other)]
    convert_element_type x2 -> x1, local copies, waits for them, and re-layouts: 3.36 us -> 2.12 us  [join3(): parts = parts.astype(jnp.float32)]
    concatenate x1, other arithmetic: 0.14 us -> 1.31 us  [gather_halves(): return jnp.concatenate([low, high], axis=1)[:, :x.shape[0]]]
    convert_element_type x1, other arithmetic: 0.06 us -> 1.06 us  [join3(): parts = parts.astype(jnp.float32)]
    concatenate x0 -> x2, local copies, waits for them, and re-layouts: none -> 0.77 us  [the longest x1 0.76 us: body(): jnp.concatenate([beta, block_mask.reshape(-1).astype(jnp.bfloat16), split...]
    ppermute x1, waiting for transfers between devices: 2.65 us -> 1.93 us  [gather_halves(): other = lax.ppermute(mine, 'row', [(r, r ^ 1) for r in range(n_row)])]
  transfers between devices with their start and end apart: 1 -> 1, of which waited for: 1 -> 1; matrix products, arithmetic and copies ran while one was open for 0% -> 1% of each run, Pallas kernels for 0% -> 0%
where the time goes in v3:
time: 64.7 us; the launch traced here: 64.3 us
  blocking collectives  34.7 us (54%)
  other arithmetic  13.5 us (21%)
  matrix products  7.24 us (11%)
  local copies, waits for them, and re-layouts  6.76 us (10%)
  waiting for transfers between devices  1.93 us (3%)
    all_to_all x1, blocking collectives, gather_halves(): mine = lax.all_to_all(wide, AXES, 0, 0, tiled=True)  34.7 us
    dot_general x1, matrix products, body(): lax.dot_general(unit_all, unit_all, (((1,), (1,)), ((), ())), preferred_e...  4.74 us
    reduce_sum x1, other arithmetic, body(): col_mass = jnp.sum(weights, axis=0)  2.93 us
    reduce_sum x1, other arithmetic, body(): jnp.sum(jnp.where(allowed, jnp.exp(masked - row_top[:, None]), 0.0), axis=1)  2.7 us
    convert_element_type x1, local copies, waits for them, and re-layouts, join3(): parts = parts.astype(jnp.float32)  2.12 us
    ppermute x1, waiting for transfers between devices, gather_halves(): other = lax.ppermute(mine, 'row', [(r, r ^ 1) for r in range(n_row)])  1.93 us
    transpose x1, local copies, waits for them, and re-layouts, body(): jnp.transpose(join3(jnp.moveaxis(probe_parts, 1, 0)), (1, 0, 2))  1.54 us
    dot_general x2, matrix products, body(): col_part = jnp.dot(scaled, affinity, preferred_element_type=jnp.float32)  1.54 us
  transfers between devices with their start and end apart: 1, of which 1 were waited for; matrix products, arithmetic and copies ran while one was open for 1% of the time, Pallas kernels for 0%

profile of v3, /device:TPU:0, one launch (start us, length us, event | category | flops | bytes accessed | tf_op | source)
XLA Modules:
  0.0 64.3 jit_solution(3135181897170500876)
XLA Ops:
  0.0 0.7 %convert_element_type.55 = bf16[2,8]{1,0:T(2,128)(2,1)S(1)} convert(s32[2,8]{1,0:T(2,128)} %param.7) | non-fusion elementwise | flops 16 | bytes 96 | tf_op jit(solution)/shard_map/convert_element_type | solution.py:79
  0.7 0.1 convert_element_type.56
  0.8 0.9 %fusion.6 = f32[32]{0:T(128)S(1)} fusion(bf16[32,768]{1,0:T(8,128)(2,1)} %param.5), kind=kLoop, calls=%fused_computation.23 | loop fusion | flops 73696 | bytes 49280 | tf_op jit(solution)/shard_map/reduce_sum | solution.py:38
  1.7 0.7 %fusion.12 = (bf16[1,64,32]{1,2,0:T(8,128)(2,1)S(1)}, bf16[1,64,32]{1,2,0:T(8,128)(2,1)S(1)}, bf16[1,64,32]{1,2,0:T(8,128)(2,1)S(1)}) fusion(f32[64,32]{0,1:T(8,128)} %param.9), kind=kLoop, calls=%fused_computation.37 | loop fusion | flops 14336 | bytes 20480 | tf_op jit(solution)/shard_map/stack | solution.py:48
  2.4 0.1 copy.29
  2.5 0.1 convert_element_type.57
  2.6 0.8 %concatenate.15 = bf16[6192]{0:T(1024)(128)(2,1)S(1)} concatenate(bf16[32]{0:T(256)(128)(2,1)} %param.6, bf16[16]{0:T(256)(128)(2,1)S(1)} %convert_element_type.56, bf16[6144]{0:T(1024)(128)(2,1)S(1)} %convert_element_type.57), dimensions={0} | concatenate | bytes 24768 | tf_op jit(solution)/shard_map/concatenate | solution.py:76
  3.4 0.9 %fusion.7 = bf16[32,768]{1,0:T(8,128)(2,1)S(1)} fusion(bf16[32,768]{1,0:T(8,128)(2,1)} %param.5, f32[32]{0:T(128)S(1)} %add_rsqrt_fusion), kind=kLoop, calls=%fused_computation.24 | loop fusion | flops 73728 | bytes 98432 | tf_op jit(solution)/shard_map/convert_element_type | solution.py:38
  4.3 0.1 broadcast_in_dim.15
  4.4 34.7 %all_to_all.5 = bf16[32,16,1024]{2,1,0:T(8,128)(2,1)S(1)} all-to-all(bf16[32,16,1024]{2,1,0:T(8,128)(2,1)S(1)} %bitcast.51), channel_id=1, replica_groups=mesh['row'=4,'col'=8] {'row','col'}, dimensions={0} | all-to-all | bytes 2097152 | tf_op jit(solution)/shard_map/all_to_all | solution.py:28
  39.1 0.0 collective-permute-start
  39.1 0.7 %fusion.14 = pred[1024]{0:T(1024)(128)(4,1)S(1)} fusion(s32[8]{0:T(128)} %param.8), kind=kLoop, calls=%fused_computation.42 | loop fusion | flops 1024 | bytes 1056 | tf_op jit(solution)/shard_map/lt | solution.py:110
  39.9 1.9 %collective-permute-done = bf16[32,16,1024]{2,1,0:T(8,128)(2,1)S(1)} collective-permute-done((bf16[32,16,1024]{2,1,0:T(8,128)(2,1)S(1)}, bf16[32,16,1024]{2,1,0:T(8,128)(2,1)S(1)}, u32[]{:S(2)}, u32[]{:S(2)}) %collective-permute-start) | collective-permute-done | bytes 1048608 | tf_op jit(solution)/shard_map/ppermute | solution.py:29
  41.8 0.1 broadcast_select_fusion.1
  41.9 0.1 pad_maximum_fusion.1
  42.0 1.3 %pad_maximum_fusion = bf16[32,32,768]{2,1,0:T(8,128)(2,1)} fusion(bf16[32,16,1024]{2,1,0:T(8,128)(2,1)S(1)} %get-tuple-element.8, bf16[32,16,1024]{2,1,0:T(8,128)(2,1)S(1)} %get-tuple-element.7), kind=kLoop, calls=%fused_computation.8 | loop fusion | flops 3145728 | bytes 3670016 | tf_op jit(solution)/shard_map/concatenate | solution.py:33
  43.3 0.3 copy.44
  43.6 0.1 slice.40
  43.7 1.1 %slice_convert_fusion = f32[32,6144]{1,0:T(8,128)} fusion(bf16[32,8192]{1,0:T(8,128)(2,1)S(1)} %bitcast.56), kind=kLoop, calls=%fused_computation.19 | loop fusion | flops 196608 | bytes 1179648 | tf_op jit(solution)/shard_map/convert_element_type | solution.py:52
  44.8 0.1 reshape.91
  44.9 0.1 copy.34
  45.0 0.1 div.26
  45.1 2.1 %reshape.90 = f32[32,3,64,32]{3,2,1,0:T(8,128)S(1)} reshape(f32[32,6144]{1,0:T(8,128)} %slice_convert_fusion) | data formatting | bytes 1572864 | tf_op jit(solution)/shard_map/convert_element_type | solution.py:52
  47.2 1.2 %fusion.5 = f32[64,32,32]{2,0,1:T(8,128)} fusion(f32[3,32,64,32]{3,2,0,1:T(8,128)S(1)} %bitcast.47), kind=kLoop, calls=%fused_computation.14 | loop fusion | flops 131072 | bytes 1048576 | tf_op jit(solution)/shard_map/transpose | solution.py:94
  48.4 1.5 %copy.30 = f32[64,32,32]{0,2,1:T(8,128)S(1)} copy(f32[64,32,32]{2,0,1:T(8,128)} %fusion.5) | data formatting | bytes 524288 | tf_op jit(solution)/shard_map/transpose | solution.py:94
  50.0 0.2 copy.35
  50.2 0.3 broadcast_in_dim.16
  50.5 4.7 %fusion.1 = (f32[1024]{0:T(1024)S(1)}, f32[1024,1024]{0,1:T(8,128)S(1)}) fusion(f32[1024]{0:T(1024)S(1)} %div.26, pred[1024]{0:T(1024)(128)(4,1)S(1)} %fusion.14, pred[128,8,8,128]{3,2,1,0:T(8,128)(4,1)S(1)} %bitcast.48, bf16[1024,768]{1,0:T(8,128)(2,1)} %bitcast.57), kind=kOutput, calls=%fused_computation.7 | convolution fusion | flops 1616903168 | bytes 6824960 | tf_op jit(solution)/shard_map/dot_general | solution.py:113
  55.3 2.7 %select_reduce_fusion = f32[1024]{0:T(1024)S(1)} fusion(f32[1024,1024]{0,1:T(8,128)S(1)} %get-tuple-element.15, f32[1024]{0:T(1024)S(1)} %get-tuple-element.14, f32[1024]{0:T(1024)S(1)} %div.26, pred[1024]{0:T(1024)(128)(4,1)S(1)} %fusion.14, pred[128,8,8,128]{3,2,1,0:T(8,128)(4,1)S(1)} %bitcast.49), kind=kLoop, calls=%fused_computation.1 | loop fusion | flops 8387584 | bytes 5256192 | tf_op jit(solution)/shard_map/reduce_sum | solution.py:123
  58.0 2.9 %fusion.16 = (f32[1024]{0:T(1024)S(1)}, bf16[1024,1024]{0,1:T(8,128)(2,1)S(1)}) fusion(f32[1024]{0:T(1024)S(1)} %select_reduce_fusion, f32[1024]{0:T(1024)S(1)} %get-tuple-element.14, f32[1024,1024]{0,1:T(8,128)S(1)} %get-tuple-element.15, f32[1024]{0:T(1024)S(1)} %div.26, pred[1024]{0:T(1024)(128)(4,1)S(1)} %fusion.14, pred[128,8,8,128]{3,2,1,0:T(8,128)(4,1)S(1)} %bitcast.50), kind=kLoop, calls=%fused_computation.46 | loop fusion | flops 10484736 | bytes 7357440 | tf_op jit(solution)/shard_map/reduce_sum | solution.py:125
  60.9 0.5 fusion.8
  61.4 0.8 %fusion.4 = bf16[64,1024]{1,0:T(8,128)(2,1)S(1)} fusion(f32[64,1024]{1,0:T(8,128)S(1)} %fusion.8, bf16[1024,1024]{0,1:T(8,128)(2,1)S(1)} %get-tuple-element.6, f32[1024]{0:T(1024)S(1)} %get-tuple-element.12, f32[1024]{0:T(1024)S(1)} %get-tuple-element.13, f32[64,1024]{1,0:T(8,128)S(1)} %copy.35), kind=kOutput, calls=%fused_computation.12 | convolution fusion | flops 134610944 | bytes 2760704 | tf_op jit(solution)/shard_map/dot_general | solution.py:134
  62.2 0.8 %fusion.18 = f32[64,1024]{1,0:T(8,128)S(1)} fusion(bf16[64,1024]{1,0:T(8,128)(2,1)S(1)} %fusion.4, bf16[1024,1024]{0,1:T(8,128)(2,1)S(1)} %get-tuple-element.6), kind=kOutput, calls=%fused_computation.48 | convolution fusion | flops 134217728 | bytes 2490368 | tf_op jit(solution)/shard_map/dot_general | solution.py:134
  63.0 0.5 fusion.17
  63.5 0.1 dynamic-slice
  63.5 0.1 fusion.9
  63.6 0.7 %copy.38 = f32[64,32]{0,1:T(8,128)} copy(f32[64,32]{1,0:T(8,128)S(1)} %fusion.9) | data formatting | bytes 16384 | tf_op jit(solution)/shard_map/dynamic_slice | solution.py:136
  (11 shorter events, 0.1 us)
Async XLA Ops:
  39.1 2.7 %collective-permute-start = (bf16[32,16,1024]{2,1,0:T(8,128)(2,1)S(1)}, bf16[32,16,1024]{2,1,0:T(8,128)(2,1)S(1)}, u32[]{:S(2)}, u32[]{:S(2)}) collective-permute-start(bf16[32,16,1024]{2,1,0:T(8,128)(2,1)S(1)} %all_to_all.5), channel_id=1, source_target_pairs={{0,8},{8,0},{16,24},{24,16},{1,9},{9,1},{17,25},{25,17},{2,10},{10... | collective-permute-start | bytes 3145736 | tf_op jit(solution)/shard_map/ppermute | solution.py:29

commit v4 on v3

--- a/solution.py
+++ b/solution.py
@@ -1,6 +1,8 @@
 import jax
 import jax.numpy as jnp
 from jax import lax
+from jax.experimental import pallas as pl
+from jax.experimental.pallas import tpu as pltpu
 from jax.sharding import PartitionSpec as P
 
 ITERS = 2
@@ -33,6 +35,126 @@
     return jnp.concatenate([low, high], axis=1)[:, : x.shape[0]]
 
 
+def dense_kernel(n_iter, tile, mine_ref, other_ref, scale_ref, rowmask_ref, probes_ref, out_ref, unit_s, aff_s):
+    files, feat = unit_s.shape
+    half = files // 2
+    runs = half // tile
+    unit_s[0:half, :] = mine_ref[:, 0:feat]
+    unit_s[half:files, :] = other_ref[:, 0:feat]
+    col_pos = lax.broadcasted_iota(jnp.int32, (tile, files), 1)
+    row_pos = lax.broadcasted_iota(jnp.int32, (tile, files), 0)
+
+    def step(t, colsum):
+        p0 = pl.multiple_of(t * tile, tile)
+        gram = lax.dot_general(
+            unit_s[pl.ds(p0, tile), :],
+            unit_s[...],
+            (((1,), (1,)), ((), ())),
+            preferred_element_type=jnp.float32,
+        )
+        scores = gram * scale_ref[pl.ds(p0, tile), :]
+        ok = (rowmask_ref[pl.ds(t % runs, 1), :] > 0.0) & (row_pos + p0 != col_pos)
+        masked = jnp.where(ok, scores, -1e30)
+        top = jnp.max(masked, axis=1, keepdims=True)
+        e = jnp.where(ok, jnp.exp(masked - top), 0.0)
+        mass = jnp.sum(e, axis=1, keepdims=True)
+        weights = e / mass
+        aff_s[pl.ds(p0, tile), :] = weights.astype(jnp.bfloat16)
+        return colsum + jnp.sum(weights, axis=0, keepdims=True)
+
+    colsum = lax.fori_loop(0, files // tile, step, jnp.zeros((1, files), jnp.float32))
+    inv_root = lax.rsqrt((1.0 + colsum) * 0.5)
+    state = probes_ref[...]
+    for sweep in range(n_iter):
+        scaled = (state * inv_root).astype(jnp.bfloat16)
+        row_part = lax.dot_general(
+            scaled, aff_s[...], (((1,), (1,)), ((), ())), preferred_element_type=jnp.float32
+        )
+        col_part = jnp.dot(scaled, aff_s[...], preferred_element_type=jnp.float32)
+        state = (row_part + col_part) * (0.5 * inv_root)
+    out_ref[...] = state
+
+
+def dense_call(mine, other, scale, rowmask, probes_int, feat):
+    files = scale.shape[0]
+    tile = files // (2 * rowmask.shape[0])
+    vmem = pl.BlockSpec(memory_space=pltpu.VMEM)
+    return pl.pallas_call(
+        lambda *refs: dense_kernel(ITERS, tile, *refs),
+        out_shape=jax.ShapeDtypeStruct(probes_int.shape, jnp.float32),
+        in_specs=[vmem] * 5,
+        out_specs=vmem,
+        scratch_shapes=[
+            pltpu.VMEM((files, feat), jnp.bfloat16),
+            pltpu.VMEM((files, files), jnp.bfloat16),
+        ],
+        cost_estimate=pl.CostEstimate(
+            flops=2 * files * files * feat + 4 * ITERS * files * files * probes_int.shape[0],
+            transcendentals=files * files,
+            bytes_accessed=files * (feat + 256) * 2 + 8 * files * probes_int.shape[0],
+        ),
+    )(mine, other, scale, rowmask, probes_int)
+
+
+def dense_path(unit_own, beta, block_mask, counts, probes, n_dev, n_row, me):
+    shard, feat = unit_own.shape
+    files = shard * n_dev
+    half_s = shard // 2
+    half_f = files // 2
+    nb = block_mask.shape[1]
+    blk = files // nb
+    local_blocks = block_mask.shape[0]
+    n_probe = probes.shape[0]
+    per_row = n_dev // n_row
+    mask_flat = block_mask.reshape(-1).astype(jnp.bfloat16)
+    mask_cols = -(-mask_flat.shape[0] // half_s)
+    mask_part = jnp.pad(mask_flat, (0, half_s * mask_cols - mask_flat.shape[0]))
+    mask_part = jnp.tile(mask_part.reshape(half_s, mask_cols), (2, 1))
+    used = 3 * n_probe + 1 + mask_cols
+    lanes = -(-used // 128) * 128
+    payload = jnp.concatenate(
+        [
+            unit_own,
+            jnp.moveaxis(split3(probes.T), 0, 1).reshape(shard, 3 * n_probe),
+            beta[:, None],
+            mask_part,
+            jnp.zeros((shard, lanes - used), jnp.bfloat16),
+        ],
+        axis=1,
+    )
+    width = payload.shape[1]
+    halves = payload.reshape(2, half_s, width)
+    wide = jnp.broadcast_to(
+        halves[None, :, None], (n_row // 2, 2, per_row, half_s, width)
+    ).reshape(n_dev, half_s, width)
+    mine = lax.all_to_all(wide, AXES, 0, 0, tiled=True)
+    other = lax.ppermute(mine, "row", [(r, r ^ 1) for r in range(n_row)])
+    core = lax.axis_index("row") % 2
+    pos = lax.iota(jnp.int32, files)
+    file_id = (
+        (pos % half_f) // half_s * shard + (pos // half_f ^ core) * half_s + pos % half_s
+    )
+    mine2 = mine.reshape(half_f, width)
+    other2 = other.reshape(half_f, width)
+    tails = jnp.concatenate([mine2[:, feat:], other2[:, feat:]], axis=0)
+    probes_int = join3(
+        jnp.stack([tails[:, k * n_probe : (k + 1) * n_probe] for k in range(3)])
+    ).T
+    scale = (tails[:, 3 * n_probe].astype(jnp.float32) / feat)[:, None]
+    mask_got = mine[:, :, feat + 3 * n_probe + 1 : feat + used].reshape(n_dev, -1)
+    mask_got = mask_got[:, : local_blocks * nb]
+    mask_full = mask_got.reshape(n_row, per_row, local_blocks, nb)[:, 0].reshape(nb, nb)
+    col_block = file_id // blk
+    live = file_id % blk < jnp.take(counts, col_block, axis=0)
+    rowmask = jnp.where(
+        live[None, :] & (jnp.take(mask_full, col_block, axis=1) == 1), 1.0, 0.0
+    ).astype(jnp.float32)
+    state = dense_call(mine2, other2, scale, rowmask, probes_int, feat)
+    first = lax.dynamic_slice_in_dim(state, core * half_f + me * half_s, half_s, 1)
+    second = lax.dynamic_slice_in_dim(state, (1 - core) * half_f + me * half_s, half_s, 1)
+    return jnp.concatenate([first, second], axis=1)
+
+
 def normalize(embed):
     values = embed.astype(jnp.float32)
     return (values * lax.rsqrt(jnp.mean(values * values, axis=1, keepdims=True) + 1e-06)).astype(
@@ -72,27 +194,40 @@
     beta_rows, beta_n = pack_rows(beta, feat)
     mask_rows, mask_n = pack_rows(block_mask.reshape(-1).astype(jnp.bfloat16), feat)
     replicate = files * files <= REPLICATE_CELLS
+    n_probe = probes.shape[0]
+    if (
+        replicate
+        and n_row % 2 == 0
+        and shard % 2 == 0
+        and blk % shard == 0
+        and (blk // 2) % 8 == 0
+        and files % 128 == 0
+    ):
+        return dense_path(unit_own, beta, block_mask, counts, probes, n_dev, n_row, me)
     if replicate:
-        extra_flat = jnp.concatenate(
+        mask_flat = block_mask.reshape(-1).astype(jnp.bfloat16)
+        mask_cols = -(-mask_flat.shape[0] // shard)
+        mask_part = jnp.pad(mask_flat, (0, shard * mask_cols - mask_flat.shape[0]))
+        used = 3 * n_probe + 1 + mask_cols
+        lanes = -(-used // 128) * 128
+        extra_cols = jnp.concatenate(
             [
-                beta,
-                block_mask.reshape(-1).astype(jnp.bfloat16),
-                split3(probes).reshape(-1),
-            ]
-        )
-        lanes = -(-extra_flat.shape[0] // (shard * 128)) * 128
-        extra_cols = jnp.pad(extra_flat, (0, shard * lanes - extra_flat.shape[0])).reshape(
-            shard, lanes
+                jnp.moveaxis(split3(probes.T), 0, 1).reshape(shard, 3 * n_probe),
+                beta[:, None],
+                mask_part.reshape(shard, mask_cols),
+                jnp.zeros((shard, lanes - used), jnp.bfloat16),
+            ],
+            axis=1,
         )
         got = gather_halves(jnp.concatenate([unit_own, extra_cols], axis=1), n_dev, n_row)
         unit_all = got[:, :, :feat].reshape(files, feat)
-        tail = got[:, :, feat:].reshape(n_dev, shard * lanes)
-        beta_all = tail[:, :shard].reshape(files)
-        mask_got = tail[:, shard : shard + local_blocks * nb]
-        probe_parts = tail[:, shard + local_blocks * nb : shard + local_blocks * nb + 3 * probes.size]
-        probe_parts = probe_parts.reshape(n_dev, 3, probes.shape[0], shard)
-        probes_all = jnp.transpose(join3(jnp.moveaxis(probe_parts, 1, 0)), (1, 0, 2))
-        probes_all = probes_all.reshape(probes.shape[0], files)
+        tail = got[:, :, feat:].reshape(files, lanes)
+        probes_t = join3(
+            jnp.stack([tail[:, k * n_probe : (k + 1) * n_probe] for k in range(3)])
+        )
+        beta_all = tail[:, 3 * n_probe]
+        mask_got = got[:, :, feat + 3 * n_probe + 1 : feat + used].reshape(n_dev, -1)
+        mask_got = mask_got[:, : local_blocks * nb]
     else:
         unit_all = gather_rows(unit_own, n_dev).reshape(files, feat)
         extra = gather_rows(jnp.concatenate([beta_rows, mask_rows], axis=0), n_dev)
@@ -125,15 +260,15 @@
         col_mass = jnp.sum(weights, axis=0)
         inv_root = lax.rsqrt((1.0 + col_mass) * 0.5)
         affinity = weights.astype(jnp.bfloat16)
-        state = probes_all
+        state = probes_t
         for sweep in range(ITERS):
-            scaled = (state * inv_root[None, :]).astype(jnp.bfloat16)
-            row_part = lax.dot_general(
-                scaled, affinity, (((1,), (1,)), ((), ())), preferred_element_type=jnp.float32
+            scaled = (state * inv_root[:, None]).astype(jnp.bfloat16)
+            row_part = jnp.dot(affinity, scaled, preferred_element_type=jnp.float32)
+            col_part = lax.dot_general(
+                affinity, scaled, (((0,), (0,)), ((), ())), preferred_element_type=jnp.float32
             )
-            col_part = jnp.dot(scaled, affinity, preferred_element_type=jnp.float32)
-            state = (row_part + col_part) * (0.5 * inv_root)[None, :]
-        return lax.dynamic_slice_in_dim(state, me * shard, shard, 1)
+            state = (row_part + col_part) * (0.5 * inv_root)[:, None]
+        return lax.dynamic_slice_in_dim(state, me * shard, shard, 0).T
 
     own_ids = me * shard + lax.iota(jnp.int32, shard)
     own_block = own_ids // blk

time: 64.7 us -> 72.4 us (1.12)
  Pallas kernels: 0 us -> 17.8 us
  matrix products: 7.24 us -> 0 us
  other arithmetic: 13.5 us -> 8.35 us
  local copies, waits for them, and re-layouts: 6.76 us -> 10.9 us
  waiting for transfers between devices: 1.93 us -> 0.01 us
    pallas_call x0 -> x1, Pallas kernels: none -> 17.8 us  [dense_call(): pl.pallas_call(lambda *refs: dense_kernel(ITERS, tile, *refs), out_shape=...]
    dot_general x5 -> x0, matrix products: 7.24 us -> none  [the longest x1 4.74 us: body(): lax.dot_general(unit_all, unit_all, (((1,), (1,)), ((), ())), preferred_e...]
    reduce_sum x2 -> x0, other arithmetic: 5.64 us -> none  [the longest x1 2.93 us: body(): col_mass = jnp.sum(weights, axis=0)]
    lt x1, other arithmetic: 0.73 us -> 5.04 us  [dense_path(): live = file_id % blk < jnp.take(counts, col_block, axis=0)]
    gather x0 -> x3, local copies, waits for them, and re-layouts: none -> 4 us  [the longest x2 3.31 us: dense_path(): jnp.take(mask_full, col_block, axis=1) == 1]
    unnamed x1 -> x14, local copies, waits for them, and re-layouts: 0.3 us -> 2.99 us
    convert_element_type x3 -> x1, local copies, waits for them, and re-layouts: 2.3 us -> 0.09 us  [dense_path(): mask_flat = block_mask.reshape(-1).astype(jnp.bfloat16)]
    ppermute x1, waiting for transfers between devices: 1.93 us -> 0.01 us  [dense_path(): other = lax.ppermute(mine, 'row', [(r, r ^ 1) for r in range(n_row)])]
  transfers between devices with their start and end apart: 1 -> 1, of which waited for: 1 -> 0; matrix products, arithmetic and copies ran while one was open for 1% -> 15% of each run, Pallas kernels for 0% -> 0%
where the time goes in v4:
time: 72.4 us; the launch traced here: 71.9 us
  blocking collectives  34.7 us (48%)
  Pallas kernels  17.8 us (25%)
  local copies, waits for them, and re-layouts  10.9 us (15%)
  other arithmetic  8.35 us (12%)
    all_to_all x1, blocking collectives, dense_path(): mine = lax.all_to_all(wide, AXES, 0, 0, tiled=True)  34.7 us
    pallas_call x1, Pallas kernels, dense_call(): pl.pallas_call(lambda *refs: dense_kernel(ITERS, tile, *refs), out_shape=...  17.8 us
    lt x1, other arithmetic, dense_path(): live = file_id % blk < jnp.take(counts, col_block, axis=0)  5.04 us
    gather x2, local copies, waits for them, and re-layouts, dense_path(): jnp.take(mask_full, col_block, axis=1) == 1  3.31 us
    unnamed x14, local copies, waits for them, and re-layouts  2.99 us
  transfers between devices with their start and end apart: 1, of which 0 were waited for; matrix products, arithmetic and copies ran while one was open for 15% of the time, Pallas kernels for 0%

profile of v4, /device:TPU:0, one launch (start us, length us, event | category | flops | bytes accessed | tf_op | source)
XLA Modules:
  0.0 71.9 jit_solution(17920552959775569132)
XLA Ops:
  0.0 0.7 convert_element_type.26
  0.7 0.1 convert_element_type.27
  0.8 0.0 copy-start.4
  0.8 0.9 %fusion.2 = f32[32]{0:T(128)S(1)} fusion(bf16[32,768]{1,0:T(8,128)(2,1)} %param.5), kind=kLoop, calls=%fused_computation.11 | loop fusion | flops 73696 | bytes 49280 | tf_op jit(solution)/shard_map/reduce_sum | solution.py:160
  1.7 0.0 copy-start.5
  1.7 0.6 copy-done.5
  2.4 0.1 concatenate.22
  2.5 0.0 copy-done.4
  2.5 0.0 copy-start.1
  2.6 0.1 concatenate.17
  2.7 0.7 copy-done.1
  3.3 0.1 fusion.3
  3.4 0.1 tile.2
  3.5 0.1 concatenate.19
  3.6 0.1 broadcast_in_dim.40
  3.7 34.7 %all_to_all.5 = bf16[32,16,1024]{2,1,0:T(8,128)(2,1)S(1)} all-to-all(bf16[32,16,1024]{2,1,0:T(8,128)(2,1)S(1)} %bitcast.51), channel_id=1, replica_groups=mesh['row'=4,'col'=8] {'row','col'}, dimensions={0} | all-to-all | bytes 2097152 | tf_op jit(solution)/shard_map/all_to_all | solution.py:130
  38.4 0.0 copy-start
  38.4 0.0 collective-permute-start
  38.4 0.0 copy-start.3
  38.4 0.6 copy-done.3
  39.0 0.7 fusion.32
  39.7 5.0 %fusion.16 = (pred[1024]{0:T(1024)(128)(4,1)S(1)}, pred[1024]{0:T(1024)(128)(4,1)S(1)}) fusion(s32[1024]{0:T(1024)S(1)} %bitcast.59, s32[]{:T(128)} %bitcast.11, s32[]{:T(128)} %bitcast.12, s32[]{:T(128)} %bitcast.13, s32[]{:T(128)} %bitcast.14, s32[]{:T(128)} %bitcast.15, s32[]{:T(128)} %bitcast.16, s32[]{:T(128)} %bitcast.17, s32[]{:T(128)} %bitcast.18, ...), kind=kLoop, calls=%fused_computation.61 | loop fusion | flops 80896 | bytes 6180 | tf_op jit(solution)/shard_map/lt | solution.py:148
  44.8 0.1 slice.57
  44.9 0.2 copy.18
  45.1 0.1 reshape_reshape.3
  45.2 0.1 copy.19
  45.3 0.1 copy.20
  45.4 3.2 %gather_fusion = bf16[1024,8]{1,0:T(8,128)(2,1)S(1)} fusion(bf16[8,8]{0,1:T(8,128)(2,1)S(1)} %copy.20, s32[1024]{0:T(1024)S(1)} %broadcast_clamp_fusion), kind=kCustom, calls=%fused_computation | custom fusion | bytes 36864 | tf_op jit(solution)/shard_map/jit(_take)/gather | solution.py:150
  48.6 0.1 copy.21
  48.8 0.1 copy.24
  48.9 0.6 select_bitcast_fusion.refs_3_
  49.6 0.0 copy-done
  49.6 0.0 collective-permute-done
  49.6 0.0 copy-start.2
  49.6 0.1 copy.25
  49.8 0.8 %copy-done.2 = bf16[32,16,1024]{2,1,0:T(8,128)(2,1)} copy-done((bf16[32,16,1024]{2,1,0:T(8,128)(2,1)}, bf16[32,16,1024]{2,1,0:T(8,128)(2,1)S(1)}, u32[]{:S(2)}) %copy-start.2) | copy-done | bytes 1048600
  50.6 0.1 maximum_convert_fusion
  50.6 0.7 %fusion.refs_4_ = f32[64,1024]{1,0:T(8,128)} fusion(f32[3,1024,64]{1,2,0:T(8,128)S(1)} %maximum_convert_fusion), kind=kLoop, calls=%fused_computation.3 | loop fusion | flops 131072 | bytes 1048576 | tf_op jit(solution)/shard_map/transpose | solution.py:142
  51.4 1.0 %copy.22.refs_2_ = f32[1024,1]{1,0:T(8,128)} copy(f32[1024,1]{0,1:T(1,128)S(1)} %fusion.20) | data formatting | bytes 8192 | tf_op jit(solution)/shard_map/div | solution.py:143
  52.4 17.8 %shard_map.55 = f32[64,1024]{1,0:T(8,128)} custom-call(bf16[512,1024]{1,0:T(8,128)(2,1)} %bitcast.53, bf16[512,1024]{1,0:T(8,128)(2,1)} %bitcast.58, f32[1024,1]{1,0:T(8,128)} %copy.22.refs_2_, f32[8,1024]{1,0:T(8,128)} %select_bitcast_fusion.refs_3_, f32[64,1024]{1,0:T(8,128)} %fusion.refs_4_), custom_call_target="tpu_custom_call" | custom-call | flops 2147483648 | bytes 2621440 | tf_op jit(solution)/shard_map/pallas_call | solution.py:82
  70.2 0.8 %constant_dynamic-slice_fusion.1 = (f32[64,16]{1,0:T(8,128)S(1)}, f32[64,16]{1,0:T(8,128)S(1)}) fusion(f32[64,1024]{1,0:T(8,128)} %shard_map.55, s32[]{:T(128)S(6)} %select_n.175, s32[]{:T(128)S(6)} %select_n.176), kind=kLoop, calls=%fused_computation.86 | loop fusion | bytes 16392 | tf_op jit(solution)/shard_map/dynamic_slice | solution.py:153
  71.1 0.1 pad_maximum_fusion.1
  71.2 0.7 copy.23
  (11 shorter events, 0.2 us)
Async XLA Ops:
  0.8 1.7 %copy-start.4 = (f32[64,32]{0,1:T(8,128)S(1)}, f32[64,32]{0,1:T(8,128)}, u32[]{:S(2)}) copy-start(f32[64,32]{0,1:T(8,128)} %param.9) | copy-start | bytes 24580
  1.7 0.7 copy-start.5
  2.5 0.8 %copy-start.1 = (bf16[32,768]{1,0:T(8,128)(2,1)S(1)}, bf16[32,768]{1,0:T(8,128)(2,1)}, u32[]{:S(2)}) copy-start(bf16[32,768]{1,0:T(8,128)(2,1)} %param.5) | copy-start | bytes 147460
  38.4 11.2 %copy-start = (bf16[32,16,1024]{2,1,0:T(8,128)(2,1)}, bf16[32,16,1024]{2,1,0:T(8,128)(2,1)S(1)}, u32[]{:S(2)}) copy-start(bf16[32,16,1024]{2,1,0:T(8,128)(2,1)S(1)} %all_to_all.5) | copy-start | bytes 3145732
  38.4 11.2 %collective-permute-start = (bf16[32,16,1024]{2,1,0:T(8,128)(2,1)S(1)}, bf16[32,16,1024]{2,1,0:T(8,128)(2,1)S(1)}, u32[]{:S(2)}, u32[]{:S(2)}) collective-permute-start(bf16[32,16,1024]{2,1,0:T(8,128)(2,1)S(1)} %all_to_all.5), channel_id=1, source_target_pairs={{0,8},{8,0},{16,24},{24,16},{1,9},{9,1},{17,25},{25,17},{2,10},{10... | collective-permute-start | bytes 3145736 | tf_op jit(solution)/shard_map/ppermute | solution.py:131
  38.4 0.7 copy-start.3
  49.6 1.0 %copy-start.2 = (bf16[32,16,1024]{2,1,0:T(8,128)(2,1)}, bf16[32,16,1024]{2,1,0:T(8,128)(2,1)S(1)}, u32[]{:S(2)}) copy-start(bf16[32,16,1024]{2,1,0:T(8,128)(2,1)S(1)} %collective-permute-done) | copy-start | bytes 3145732

commit v5 on v4

--- a/solution.py
+++ b/solution.py
@@ -35,24 +35,26 @@
     return jnp.concatenate([low, high], axis=1)[:, : x.shape[0]]
 
 
-def dense_kernel(n_iter, tile, mine_ref, other_ref, scale_ref, rowmask_ref, probes_ref, out_ref, unit_s, aff_s):
-    files, feat = unit_s.shape
+def dense_kernel(n_iter, tile, beta_lane, mine_ref, other_ref, rowmask_ref, probes_ref, out_ref, unit_t, scale_s, aff_s):
+    feat, files = unit_t.shape
     half = files // 2
     runs = half // tile
-    unit_s[0:half, :] = mine_ref[:, 0:feat]
-    unit_s[half:files, :] = other_ref[:, 0:feat]
+    for k, ref in enumerate((mine_ref, other_ref)):
+        unit_t[:, k * half : (k + 1) * half] = (
+            ref[:, 0:feat].astype(jnp.float32).T.astype(jnp.bfloat16)
+        )
+        scale_s[k * half : (k + 1) * half, :] = (
+            ref[:, beta_lane : beta_lane + 1].astype(jnp.float32) / feat
+        )
     col_pos = lax.broadcasted_iota(jnp.int32, (tile, files), 1)
     row_pos = lax.broadcasted_iota(jnp.int32, (tile, files), 0)
 
     def step(t, colsum):
         p0 = pl.multiple_of(t * tile, tile)
-        gram = lax.dot_general(
-            unit_s[pl.ds(p0, tile), :],
-            unit_s[...],
-            (((1,), (1,)), ((), ())),
-            preferred_element_type=jnp.float32,
-        )
-        scores = gram * scale_ref[pl.ds(p0, tile), :]
+        q0 = pl.multiple_of((t % runs) * tile, tile)
+        rows = jnp.where(t < runs, mine_ref[pl.ds(q0, tile), 0:feat], other_ref[pl.ds(q0, tile), 0:feat])
+        gram = jnp.dot(rows, unit_t[...], preferred_element_type=jnp.float32)
+        scores = gram * scale_s[pl.ds(p0, tile), :]
         ok = (rowmask_ref[pl.ds(t % runs, 1), :] > 0.0) & (row_pos + p0 != col_pos)
         masked = jnp.where(ok, scores, -1e30)
         top = jnp.max(masked, axis=1, keepdims=True)
@@ -66,34 +68,34 @@
     inv_root = lax.rsqrt((1.0 + colsum) * 0.5)
     state = probes_ref[...]
     for sweep in range(n_iter):
-        scaled = (state * inv_root).astype(jnp.bfloat16)
-        row_part = lax.dot_general(
-            scaled, aff_s[...], (((1,), (1,)), ((), ())), preferred_element_type=jnp.float32
-        )
+        scaled_f = (state * inv_root).astype(jnp.bfloat16).astype(jnp.float32)
+        scaled = scaled_f.astype(jnp.bfloat16)
+        row_t = jnp.dot(aff_s[...], scaled_f.T.astype(jnp.bfloat16), preferred_element_type=jnp.float32)
         col_part = jnp.dot(scaled, aff_s[...], preferred_element_type=jnp.float32)
-        state = (row_part + col_part) * (0.5 * inv_root)
+        state = (row_t.T + col_part) * (0.5 * inv_root)
     out_ref[...] = state
 
 
-def dense_call(mine, other, scale, rowmask, probes_int, feat):
-    files = scale.shape[0]
+def dense_call(mine, other, rowmask, probes_int, feat, beta_lane):
+    files = 2 * mine.shape[0]
     tile = files // (2 * rowmask.shape[0])
     vmem = pl.BlockSpec(memory_space=pltpu.VMEM)
     return pl.pallas_call(
-        lambda *refs: dense_kernel(ITERS, tile, *refs),
+        lambda *refs: dense_kernel(ITERS, tile, beta_lane, *refs),
         out_shape=jax.ShapeDtypeStruct(probes_int.shape, jnp.float32),
-        in_specs=[vmem] * 5,
+        in_specs=[vmem] * 4,
         out_specs=vmem,
         scratch_shapes=[
-            pltpu.VMEM((files, feat), jnp.bfloat16),
+            pltpu.VMEM((feat, files), jnp.bfloat16),
+            pltpu.VMEM((files, 1), jnp.float32),
             pltpu.VMEM((files, files), jnp.bfloat16),
         ],
         cost_estimate=pl.CostEstimate(
             flops=2 * files * files * feat + 4 * ITERS * files * files * probes_int.shape[0],
             transcendentals=files * files,
-            bytes_accessed=files * (feat + 256) * 2 + 8 * files * probes_int.shape[0],
+            bytes_accessed=files * mine.shape[1] * 2 + 8 * files * probes_int.shape[0],
         ),
-    )(mine, other, scale, rowmask, probes_int)
+    )(mine, other, rowmask, probes_int)
 
 
 def dense_path(unit_own, beta, block_mask, counts, probes, n_dev, n_row, me):
@@ -131,25 +133,25 @@
     other = lax.ppermute(mine, "row", [(r, r ^ 1) for r in range(n_row)])
     core = lax.axis_index("row") % 2
     pos = lax.iota(jnp.int32, files)
-    file_id = (
-        (pos % half_f) // half_s * shard + (pos // half_f ^ core) * half_s + pos % half_s
-    )
+    run = blk // 2
+    in_run = lax.iota(jnp.int32, files) % run
+    run_dev = in_run // half_s
+    half_of = jnp.broadcast_to((lax.iota(jnp.int32, 2) ^ core)[:, None, None], (2, nb, run))
+    in_block = (run_dev % (blk // shard)) * shard + half_of.reshape(files) * half_s + in_run % half_s
+    block_counts = jnp.broadcast_to(counts[None, :, None], (2, nb, run)).reshape(files)
+    live = in_block < block_counts
     mine2 = mine.reshape(half_f, width)
     other2 = other.reshape(half_f, width)
     tails = jnp.concatenate([mine2[:, feat:], other2[:, feat:]], axis=0)
     probes_int = join3(
         jnp.stack([tails[:, k * n_probe : (k + 1) * n_probe] for k in range(3)])
     ).T
-    scale = (tails[:, 3 * n_probe].astype(jnp.float32) / feat)[:, None]
     mask_got = mine[:, :, feat + 3 * n_probe + 1 : feat + used].reshape(n_dev, -1)
     mask_got = mask_got[:, : local_blocks * nb]
     mask_full = mask_got.reshape(n_row, per_row, local_blocks, nb)[:, 0].reshape(nb, nb)
-    col_block = file_id // blk
-    live = file_id % blk < jnp.take(counts, col_block, axis=0)
-    rowmask = jnp.where(
-        live[None, :] & (jnp.take(mask_full, col_block, axis=1) == 1), 1.0, 0.0
-    ).astype(jnp.float32)
-    state = dense_call(mine2, other2, scale, rowmask, probes_int, feat)
+    block_ok = jnp.broadcast_to((mask_full == 1)[:, None, :, None], (nb, 2, nb, run))
+    rowmask = jnp.where(block_ok.reshape(nb, files) & live[None, :], 1.0, 0.0).astype(jnp.float32)
+    state = dense_call(mine2, other2, rowmask, probes_int, feat, feat + 3 * n_probe)
     first = lax.dynamic_slice_in_dim(state, core * half_f + me * half_s, half_s, 1)
     second = lax.dynamic_slice_in_dim(state, (1 - core) * half_f + me * half_s, half_s, 1)
     return jnp.concatenate([first, second], axis=1)

time: 72.4 us -> 60.3 us (0.83)
  other arithmetic: 8.35 us -> 3.3 us
  local copies, waits for them, and re-layouts: 10.9 us -> 5.93 us
  Pallas kernels: 17.8 us -> 15.5 us
    lt x1, other arithmetic: 5.04 us -> 0.02 us  [dense_path(): live = in_block < block_counts]
    gather x3 -> x0, local copies, waits for them, and re-layouts: 4 us -> none  [the longest x2 3.31 us: dense_path(): jnp.take(mask_full, col_block, axis=1) == 1]
    pallas_call x1, Pallas kernels: 17.8 us -> 15.5 us  [dense_call(): pl.pallas_call(lambda *refs: dense_kernel(ITERS, tile, beta_lane, *refs),...]
    div x1 -> x0, local copies, waits for them, and re-layouts: 1.04 us -> none  [dense_path(): scale = (tails[:, 3 * n_probe].astype(jnp.float32) / feat)[:, None]]
  transfers between devices with their start and end apart: 1 -> 1, of which waited for: 0 -> 1; matrix products, arithmetic and copies ran while one was open for 15% -> 3% of each run, Pallas kernels for 0% -> 0%
where the time goes in v5:
time: 60.3 us; the launch traced here: 60 us
  blocking collectives  34.7 us (58%)
  Pallas kernels  15.5 us (26%)
  local copies, waits for them, and re-layouts  5.93 us (10%)
  other arithmetic  3.3 us (5%)
    all_to_all x1, blocking collectives, dense_path(): mine = lax.all_to_all(wide, AXES, 0, 0, tiled=True)  34.7 us
    pallas_call x1, Pallas kernels, dense_call(): pl.pallas_call(lambda *refs: dense_kernel(ITERS, tile, beta_lane, *refs),...  15.5 us
    unnamed x14, local copies, waits for them, and re-layouts  2.91 us
  transfers between devices with their start and end apart: 1, of which 1 were waited for; matrix products, arithmetic and copies ran while one was open for 3% of the time, Pallas kernels for 0%

profile of v5, /device:TPU:0, one launch (start us, length us, event | category | flops | bytes accessed | tf_op | source)
XLA Modules:
  0.0 60.0 jit_solution(8656058123508042760)
XLA Ops:
  0.0 0.7 %convert_element_type.22 = bf16[2,8]{1,0:T(2,128)(2,1)S(1)} convert(s32[2,8]{1,0:T(2,128)} %param.7) | non-fusion elementwise | flops 16 | bytes 96 | tf_op jit(solution)/shard_map/convert_element_type | solution.py:111
  0.7 0.1 convert_element_type.23
  0.8 0.0 copy-start.3
  0.8 0.9 %fusion.2 = f32[32]{0:T(128)S(1)} fusion(bf16[32,768]{1,0:T(8,128)(2,1)} %param.5), kind=kLoop, calls=%fused_computation.11 | loop fusion | flops 73696 | bytes 49280 | tf_op jit(solution)/shard_map/reduce_sum | solution.py:162
  1.7 0.0 copy-start.4
  1.7 0.6 %copy-done.4 = bf16[32]{0:T(256)(128)(2,1)S(1)} copy-done((bf16[32]{0:T(256)(128)(2,1)S(1)}, bf16[32]{0:T(256)(128)(2,1)}, u32[]{:S(2)}) %copy-start.4) | copy-done | bytes 88
  2.4 0.1 concatenate.22
  2.5 0.0 copy-done.3
  2.5 0.0 copy-start.1
  2.6 0.1 concatenate.17
  2.7 0.7 %copy-done.1 = bf16[32,768]{1,0:T(8,128)(2,1)S(1)} copy-done((bf16[32,768]{1,0:T(8,128)(2,1)S(1)}, bf16[32,768]{1,0:T(8,128)(2,1)}, u32[]{:S(2)}) %copy-start.1) | copy-done | bytes 49176
  3.3 0.1 fusion.3
  3.4 0.1 tile.2
  3.5 0.1 concatenate.19
  3.6 0.1 broadcast_in_dim.20
  3.7 34.7 %all_to_all.5 = bf16[32,16,1024]{2,1,0:T(8,128)(2,1)S(1)} all-to-all(bf16[32,16,1024]{2,1,0:T(8,128)(2,1)S(1)} %bitcast.40), channel_id=1, replica_groups=mesh['row'=4,'col'=8] {'row','col'}, dimensions={0} | all-to-all | bytes 2097152 | tf_op jit(solution)/shard_map/all_to_all | solution.py:132
  38.4 0.0 copy-start
  38.4 0.0 collective-permute-start
  38.4 0.1 broadcast_in_dim.43
  38.5 0.0 copy-start.5
  38.5 0.1 mul.52
  38.5 0.6 %copy-done.5 = s32[8]{0:T(128)S(1)} copy-done((s32[8]{0:T(128)S(1)}, s32[8]{0:T(128)}, u32[]{:S(2)}) %copy-start.5) | copy-done | bytes 56
  39.2 0.1 broadcast_in_dim.44
  39.2 0.1 reshape.123
  39.3 0.2 slice_reduce_fusion
  39.6 0.1 reshape.124
  39.7 0.1 broadcast_in_dim.42
  39.8 0.1 reshape.122
  39.9 0.1 copy.29
  40.1 0.6 %and_select_fusion.refs_2_ = f32[8,1024]{1,0:T(8,128)} fusion(pred[8,1024]{1,0:T(8,128)(4,1)S(1)} %reshape.122, pred[1024]{0:T(1024)(128)(4,1)S(1)} %fusion.12), kind=kLoop, calls=%fused_computation.14 | loop fusion | flops 16384 | bytes 41984 | tf_op jit(solution)/shard_map/jit(_where)/select_n | solution.py:153
  40.7 0.4 collective-permute-done
  41.0 0.0 copy-start.2
  41.1 0.1 copy.30
  41.2 0.0 copy-done
  41.3 0.1 maximum_convert_fusion
  41.4 0.7 %copy-done.2 = bf16[32,16,1024]{2,1,0:T(8,128)(2,1)} copy-done((bf16[32,16,1024]{2,1,0:T(8,128)(2,1)}, bf16[32,16,1024]{2,1,0:T(8,128)(2,1)S(1)}, u32[]{:S(2)}) %copy-start.2) | copy-done | bytes 1048600
  42.1 0.7 %fusion.refs_3_ = f32[64,1024]{1,0:T(8,128)} fusion(f32[3,1024,64]{1,2,0:T(8,128)S(1)} %maximum_convert_fusion), kind=kLoop, calls=%fused_computation.2 | loop fusion | flops 131072 | bytes 1048576 | tf_op jit(solution)/shard_map/transpose | solution.py:148
  42.8 15.5 %shard_map.55 = f32[64,1024]{1,0:T(8,128)} custom-call(bf16[512,1024]{1,0:T(8,128)(2,1)} %bitcast.42, bf16[512,1024]{1,0:T(8,128)(2,1)} %bitcast.46, f32[8,1024]{1,0:T(8,128)} %and_select_fusion.refs_2_, f32[64,1024]{1,0:T(8,128)} %fusion.refs_3_), custom_call_target="tpu_custom_call" | custom-call | flops 2147483648 | bytes 2621440 | tf_op jit(solution)/shard_map/pallas_call | solution.py:83
  58.3 0.8 %constant_dynamic-slice_fusion.1 = (f32[64,16]{1,0:T(8,128)S(1)}, f32[64,16]{1,0:T(8,128)S(1)}) fusion(f32[64,1024]{1,0:T(8,128)} %shard_map.55, s32[]{:T(128)S(6)} %select_n.60, s32[]{:T(128)S(6)} %select_n.61), kind=kLoop, calls=%fused_computation.48 | loop fusion | bytes 16392 | tf_op jit(solution)/shard_map/dynamic_slice | solution.py:155
  59.2 0.1 pad_maximum_fusion.1
  59.3 0.7 %copy.25 = f32[64,32]{0,1:T(8,128)} copy(f32[64,32]{1,0:T(8,128)S(1)} %pad_maximum_fusion.1) | data formatting | bytes 16384 | tf_op jit(solution)/shard_map/concatenate | solution.py:157
  (14 shorter events, 0.2 us)
Async XLA Ops:
  0.8 1.7 %copy-start.3 = (f32[64,32]{0,1:T(8,128)S(1)}, f32[64,32]{0,1:T(8,128)}, u32[]{:S(2)}) copy-start(f32[64,32]{0,1:T(8,128)} %param.9) | copy-start | bytes 24580
  1.7 0.7 %copy-start.4 = (bf16[32]{0:T(256)(128)(2,1)S(1)}, bf16[32]{0:T(256)(128)(2,1)}, u32[]{:S(2)}) copy-start(bf16[32]{0:T(256)(128)(2,1)} %param.6) | copy-start | bytes 196
  2.5 0.8 %copy-start.1 = (bf16[32,768]{1,0:T(8,128)(2,1)S(1)}, bf16[32,768]{1,0:T(8,128)(2,1)}, u32[]{:S(2)}) copy-start(bf16[32,768]{1,0:T(8,128)(2,1)} %param.5) | copy-start | bytes 147460
  38.4 2.9 %copy-start = (bf16[32,16,1024]{2,1,0:T(8,128)(2,1)}, bf16[32,16,1024]{2,1,0:T(8,128)(2,1)S(1)}, u32[]{:S(2)}) copy-start(bf16[32,16,1024]{2,1,0:T(8,128)(2,1)S(1)} %all_to_all.5) | copy-start | bytes 3145732
  38.4 2.7 %collective-permute-start = (bf16[32,16,1024]{2,1,0:T(8,128)(2,1)S(1)}, bf16[32,16,1024]{2,1,0:T(8,128)(2,1)S(1)}, u32[]{:S(2)}, u32[]{:S(2)}) collective-permute-start(bf16[32,16,1024]{2,1,0:T(8,128)(2,1)S(1)} %all_to_all.5), channel_id=1, source_target_pairs={{0,8},{8,0},{16,24},{24,16},{1,9},{9,1},{17,25},{25,17},{2,10},{10... | collective-permute-start | bytes 3145736 | tf_op jit(solution)/shard_map/ppermute | solution.py:133
  38.5 0.7 %copy-start.5 = (s32[8]{0:T(128)S(1)}, s32[8]{0:T(128)}, u32[]{:S(2)}) copy-start(s32[8]{0:T(128)} %param.8) | copy-start | bytes 100
  41.0 1.0 %copy-start.2 = (bf16[32,16,1024]{2,1,0:T(8,128)(2,1)}, bf16[32,16,1024]{2,1,0:T(8,128)(2,1)S(1)}, u32[]{:S(2)}) copy-start(bf16[32,16,1024]{2,1,0:T(8,128)(2,1)S(1)} %collective-permute-done) | copy-start | bytes 3145732

commit v6 on v5

--- a/solution.py
+++ b/solution.py
@@ -35,11 +35,12 @@
     return jnp.concatenate([low, high], axis=1)[:, : x.shape[0]]
 
 
-def dense_kernel(n_iter, tile, beta_lane, mine_ref, other_ref, rowmask_ref, probes_ref, out_ref, unit_t, scale_s, aff_s):
+def dense_kernel(n_iter, tile, beta_lane, mine_ref, other_ref, rowmask_ref, probes_ref, out_ref, unit_t, unit_s, scale_s, aff_s):
     feat, files = unit_t.shape
     half = files // 2
     runs = half // tile
     for k, ref in enumerate((mine_ref, other_ref)):
+        unit_s[k * half : (k + 1) * half, :] = ref[:, 0:feat]
         unit_t[:, k * half : (k + 1) * half] = (
             ref[:, 0:feat].astype(jnp.float32).T.astype(jnp.bfloat16)
         )
@@ -51,16 +52,14 @@
 
     def step(t, colsum):
         p0 = pl.multiple_of(t * tile, tile)
-        q0 = pl.multiple_of((t % runs) * tile, tile)
-        rows = jnp.where(t < runs, mine_ref[pl.ds(q0, tile), 0:feat], other_ref[pl.ds(q0, tile), 0:feat])
-        gram = jnp.dot(rows, unit_t[...], preferred_element_type=jnp.float32)
+        gram = jnp.dot(unit_s[pl.ds(p0, tile), :], unit_t[...], preferred_element_type=jnp.float32)
         scores = gram * scale_s[pl.ds(p0, tile), :]
         ok = (rowmask_ref[pl.ds(t % runs, 1), :] > 0.0) & (row_pos + p0 != col_pos)
         masked = jnp.where(ok, scores, -1e30)
         top = jnp.max(masked, axis=1, keepdims=True)
-        e = jnp.where(ok, jnp.exp(masked - top), 0.0)
+        e = jnp.exp(masked - top)
         mass = jnp.sum(e, axis=1, keepdims=True)
-        weights = e / mass
+        weights = e * (1.0 / mass)
         aff_s[pl.ds(p0, tile), :] = weights.astype(jnp.bfloat16)
         return colsum + jnp.sum(weights, axis=0, keepdims=True)
 
@@ -87,6 +86,7 @@
         out_specs=vmem,
         scratch_shapes=[
             pltpu.VMEM((feat, files), jnp.bfloat16),
+            pltpu.VMEM((files, feat), jnp.bfloat16),
             pltpu.VMEM((files, 1), jnp.float32),
             pltpu.VMEM((files, files), jnp.bfloat16),
         ],

time: 60.3 us -> 60.3 us (level)
  no operation moved by 1% of the time
where the time goes in v6:
time: 60.3 us; the launch traced here: 59.9 us
  blocking collectives  34.7 us (58%)
  Pallas kernels  15.5 us (26%)
  local copies, waits for them, and re-layouts  5.93 us (10%)
  other arithmetic  3.3 us (5%)
    all_to_all x1, blocking collectives, dense_path(): mine = lax.all_to_all(wide, AXES, 0, 0, tiled=True)  34.7 us
    pallas_call x1, Pallas kernels, dense_call(): pl.pallas_call(lambda *refs: dense_kernel(ITERS, tile, beta_lane, *refs),...  15.5 us
    unnamed x14, local copies, waits for them, and re-layouts  2.91 us
  transfers between devices with their start and end apart: 1, of which 1 were waited for; matrix products, arithmetic and copies ran while one was open for 3% of the time, Pallas kernels for 0%

profile of v6, /device:TPU:0, one launch (start us, length us, event | category | flops | bytes accessed | tf_op | source)
XLA Modules:
  0.0 59.9 jit_solution(13554983556044461766)
XLA Ops:
  0.0 0.7 %convert_element_type.22 = bf16[2,8]{1,0:T(2,128)(2,1)S(1)} convert(s32[2,8]{1,0:T(2,128)} %param.7) | non-fusion elementwise | flops 16 | bytes 96 | tf_op jit(solution)/shard_map/convert_element_type | solution.py:111
  0.7 0.1 convert_element_type.23
  0.8 0.0 copy-start.3
  0.8 0.9 %fusion.2 = f32[32]{0:T(128)S(1)} fusion(bf16[32,768]{1,0:T(8,128)(2,1)} %param.5), kind=kLoop, calls=%fused_computation.11 | loop fusion | flops 73696 | bytes 49280 | tf_op jit(solution)/shard_map/reduce_sum | solution.py:162
  1.7 0.0 copy-start.4
  1.7 0.6 %copy-done.4 = bf16[32]{0:T(256)(128)(2,1)S(1)} copy-done((bf16[32]{0:T(256)(128)(2,1)S(1)}, bf16[32]{0:T(256)(128)(2,1)}, u32[]{:S(2)}) %copy-start.4) | copy-done | bytes 88
  2.4 0.1 concatenate.22
  2.5 0.0 copy-done.3
  2.5 0.0 copy-start.1
  2.6 0.1 concatenate.17
  2.7 0.7 %copy-done.1 = bf16[32,768]{1,0:T(8,128)(2,1)S(1)} copy-done((bf16[32,768]{1,0:T(8,128)(2,1)S(1)}, bf16[32,768]{1,0:T(8,128)(2,1)}, u32[]{:S(2)}) %copy-start.1) | copy-done | bytes 49176
  3.3 0.1 fusion.3
  3.4 0.1 tile.2
  3.5 0.1 concatenate.19
  3.6 0.1 broadcast_in_dim.20
  3.7 34.7 %all_to_all.5 = bf16[32,16,1024]{2,1,0:T(8,128)(2,1)S(1)} all-to-all(bf16[32,16,1024]{2,1,0:T(8,128)(2,1)S(1)} %bitcast.40), channel_id=1, replica_groups=mesh['row'=4,'col'=8] {'row','col'}, dimensions={0} | all-to-all | bytes 2097152 | tf_op jit(solution)/shard_map/all_to_all | solution.py:132
  38.4 0.0 copy-start
  38.4 0.0 collective-permute-start
  38.4 0.1 broadcast_in_dim.43
  38.5 0.0 copy-start.5
  38.5 0.1 mul.52
  38.5 0.6 %copy-done.5 = s32[8]{0:T(128)S(1)} copy-done((s32[8]{0:T(128)S(1)}, s32[8]{0:T(128)}, u32[]{:S(2)}) %copy-start.5) | copy-done | bytes 56
  39.2 0.1 broadcast_in_dim.44
  39.2 0.1 reshape.123
  39.3 0.2 slice_reduce_fusion
  39.6 0.1 reshape.124
  39.7 0.1 broadcast_in_dim.42
  39.8 0.1 reshape.122
  39.9 0.1 copy.29
  40.1 0.6 %and_select_fusion.refs_2_ = f32[8,1024]{1,0:T(8,128)} fusion(pred[8,1024]{1,0:T(8,128)(4,1)S(1)} %reshape.122, pred[1024]{0:T(1024)(128)(4,1)S(1)} %fusion.12), kind=kLoop, calls=%fused_computation.14 | loop fusion | flops 16384 | bytes 41984 | tf_op jit(solution)/shard_map/jit(_where)/select_n | solution.py:153
  40.7 0.4 collective-permute-done
  41.0 0.0 copy-start.2
  41.1 0.1 copy.30
  41.2 0.0 copy-done
  41.3 0.1 maximum_convert_fusion
  41.4 0.7 %copy-done.2 = bf16[32,16,1024]{2,1,0:T(8,128)(2,1)} copy-done((bf16[32,16,1024]{2,1,0:T(8,128)(2,1)}, bf16[32,16,1024]{2,1,0:T(8,128)(2,1)S(1)}, u32[]{:S(2)}) %copy-start.2) | copy-done | bytes 1048600
  42.1 0.7 %fusion.refs_3_ = f32[64,1024]{1,0:T(8,128)} fusion(f32[3,1024,64]{1,2,0:T(8,128)S(1)} %maximum_convert_fusion), kind=kLoop, calls=%fused_computation.2 | loop fusion | flops 131072 | bytes 1048576 | tf_op jit(solution)/shard_map/transpose | solution.py:148
  42.8 15.5 %shard_map.55 = f32[64,1024]{1,0:T(8,128)} custom-call(bf16[512,1024]{1,0:T(8,128)(2,1)} %bitcast.42, bf16[512,1024]{1,0:T(8,128)(2,1)} %bitcast.46, f32[8,1024]{1,0:T(8,128)} %and_select_fusion.refs_2_, f32[64,1024]{1,0:T(8,128)} %fusion.refs_3_), custom_call_target="tpu_custom_call" | custom-call | flops 2147483648 | bytes 2621440 | tf_op jit(solution)/shard_map/pallas_call | solution.py:82
  58.3 0.8 %constant_dynamic-slice_fusion.1 = (f32[64,16]{1,0:T(8,128)S(1)}, f32[64,16]{1,0:T(8,128)S(1)}) fusion(f32[64,1024]{1,0:T(8,128)} %shard_map.55, s32[]{:T(128)S(6)} %select_n.60, s32[]{:T(128)S(6)} %select_n.61), kind=kLoop, calls=%fused_computation.48 | loop fusion | bytes 16392 | tf_op jit(solution)/shard_map/dynamic_slice | solution.py:155
  59.1 0.1 pad_maximum_fusion.1
  59.2 0.7 %copy.25 = f32[64,32]{0,1:T(8,128)} copy(f32[64,32]{1,0:T(8,128)S(1)} %pad_maximum_fusion.1) | data formatting | bytes 16384 | tf_op jit(solution)/shard_map/concatenate | solution.py:157
  (14 shorter events, 0.2 us)
Async XLA Ops:
  0.8 1.7 %copy-start.3 = (f32[64,32]{0,1:T(8,128)S(1)}, f32[64,32]{0,1:T(8,128)}, u32[]{:S(2)}) copy-start(f32[64,32]{0,1:T(8,128)} %param.9) | copy-start | bytes 24580
  1.7 0.7 %copy-start.4 = (bf16[32]{0:T(256)(128)(2,1)S(1)}, bf16[32]{0:T(256)(128)(2,1)}, u32[]{:S(2)}) copy-start(bf16[32]{0:T(256)(128)(2,1)} %param.6) | copy-start | bytes 196
  2.5 0.8 %copy-start.1 = (bf16[32,768]{1,0:T(8,128)(2,1)S(1)}, bf16[32,768]{1,0:T(8,128)(2,1)}, u32[]{:S(2)}) copy-start(bf16[32,768]{1,0:T(8,128)(2,1)} %param.5) | copy-start | bytes 147460
  38.4 2.9 %copy-start = (bf16[32,16,1024]{2,1,0:T(8,128)(2,1)}, bf16[32,16,1024]{2,1,0:T(8,128)(2,1)S(1)}, u32[]{:S(2)}) copy-start(bf16[32,16,1024]{2,1,0:T(8,128)(2,1)S(1)} %all_to_all.5) | copy-start | bytes 3145732
  38.4 2.7 %collective-permute-start = (bf16[32,16,1024]{2,1,0:T(8,128)(2,1)S(1)}, bf16[32,16,1024]{2,1,0:T(8,128)(2,1)S(1)}, u32[]{:S(2)}, u32[]{:S(2)}) collective-permute-start(bf16[32,16,1024]{2,1,0:T(8,128)(2,1)S(1)} %all_to_all.5), channel_id=1, source_target_pairs={{0,8},{8,0},{16,24},{24,16},{1,9},{9,1},{17,25},{25,17},{2,10},{10... | collective-permute-start | bytes 3145736 | tf_op jit(solution)/shard_map/ppermute | solution.py:133
  38.5 0.7 %copy-start.5 = (s32[8]{0:T(128)S(1)}, s32[8]{0:T(128)}, u32[]{:S(2)}) copy-start(s32[8]{0:T(128)} %param.8) | copy-start | bytes 100
  41.0 1.0 %copy-start.2 = (bf16[32,16,1024]{2,1,0:T(8,128)(2,1)}, bf16[32,16,1024]{2,1,0:T(8,128)(2,1)S(1)}, u32[]{:S(2)}) copy-start(bf16[32,16,1024]{2,1,0:T(8,128)(2,1)S(1)} %collective-permute-done) | copy-start | bytes 3145732

commit v7 on v6

--- a/solution.py
+++ b/solution.py
@@ -47,6 +47,8 @@
         scale_s[k * half : (k + 1) * half, :] = (
             ref[:, beta_lane : beta_lane + 1].astype(jnp.float32) / feat
         )
+    per_tile = rowmask_ref.shape[1]
+    run = tile // per_tile
     col_pos = lax.broadcasted_iota(jnp.int32, (tile, files), 1)
     row_pos = lax.broadcasted_iota(jnp.int32, (tile, files), 0)
 
@@ -54,7 +56,9 @@
         p0 = pl.multiple_of(t * tile, tile)
         gram = jnp.dot(unit_s[pl.ds(p0, tile), :], unit_t[...], preferred_element_type=jnp.float32)
         scores = gram * scale_s[pl.ds(p0, tile), :]
-        ok = (rowmask_ref[pl.ds(t % runs, 1), :] > 0.0) & (row_pos + p0 != col_pos)
+        runs_here = rowmask_ref[t % runs]
+        block_row = jnp.broadcast_to(runs_here[:, None, :], (per_tile, run, files)).reshape(tile, files)
+        ok = (block_row > 0.0) & (row_pos + p0 != col_pos)
         masked = jnp.where(ok, scores, -1e30)
         top = jnp.max(masked, axis=1, keepdims=True)
         e = jnp.exp(masked - top)
@@ -77,7 +81,11 @@
 
 def dense_call(mine, other, rowmask, probes_int, feat, beta_lane):
     files = 2 * mine.shape[0]
-    tile = files // (2 * rowmask.shape[0])
+    run = files // (2 * rowmask.shape[0])
+    tile = run
+    while tile * 2 <= min(256, files // 2) and (files // 2) % (tile * 2) == 0:
+        tile *= 2
+    rowmask = rowmask.reshape(-1, tile // run, files)
     vmem = pl.BlockSpec(memory_space=pltpu.VMEM)
     return pl.pallas_call(
         lambda *refs: dense_kernel(ITERS, tile, beta_lane, *refs),

time: 60.3 us -> 54.2 us (0.90)
  Pallas kernels: 15.5 us -> 9.35 us
    pallas_call x1, Pallas kernels: 15.5 us -> 9.35 us  [dense_call(): pl.pallas_call(lambda *refs: dense_kernel(ITERS, tile, beta_lane, *refs),...]
where the time goes in v7:
time: 54.2 us; the launch traced here: 53.8 us
  blocking collectives  34.7 us (64%)
  Pallas kernels  9.35 us (17%)
  local copies, waits for them, and re-layouts  5.92 us (11%)
  other arithmetic  3.3 us (6%)
    all_to_all x1, blocking collectives, dense_path(): mine = lax.all_to_all(wide, AXES, 0, 0, tiled=True)  34.7 us
    pallas_call x1, Pallas kernels, dense_call(): pl.pallas_call(lambda *refs: dense_kernel(ITERS, tile, beta_lane, *refs),...  9.35 us
    unnamed x14, local copies, waits for them, and re-layouts  2.91 us
  transfers between devices with their start and end apart: 1, of which 1 were waited for; matrix products, arithmetic and copies ran while one was open for 3% of the time, Pallas kernels for 0%

profile of v7, /device:TPU:0, one launch (start us, length us, event | category | flops | bytes accessed | tf_op | source)
XLA Modules:
  0.0 53.8 jit_solution(661134249317240666)
XLA Ops:
  0.0 0.7 %convert_element_type.22 = bf16[2,8]{1,0:T(2,128)(2,1)S(1)} convert(s32[2,8]{1,0:T(2,128)} %param.7) | non-fusion elementwise | flops 16 | bytes 96 | tf_op jit(solution)/shard_map/convert_element_type | solution.py:119
  0.7 0.1 convert_element_type.23
  0.8 0.0 copy-start.3
  0.8 0.9 %fusion.2 = f32[32]{0:T(128)S(1)} fusion(bf16[32,768]{1,0:T(8,128)(2,1)} %param.5), kind=kLoop, calls=%fused_computation.11 | loop fusion | flops 73696 | bytes 49280 | tf_op jit(solution)/shard_map/reduce_sum | solution.py:170
  1.7 0.0 copy-start.4
  1.7 0.6 %copy-done.4 = bf16[32]{0:T(256)(128)(2,1)S(1)} copy-done((bf16[32]{0:T(256)(128)(2,1)S(1)}, bf16[32]{0:T(256)(128)(2,1)}, u32[]{:S(2)}) %copy-start.4) | copy-done | bytes 88
  2.4 0.1 concatenate.22
  2.5 0.0 copy-done.3
  2.5 0.0 copy-start.1
  2.6 0.1 concatenate.17
  2.7 0.7 %copy-done.1 = bf16[32,768]{1,0:T(8,128)(2,1)S(1)} copy-done((bf16[32,768]{1,0:T(8,128)(2,1)S(1)}, bf16[32,768]{1,0:T(8,128)(2,1)}, u32[]{:S(2)}) %copy-start.1) | copy-done | bytes 49176
  3.3 0.1 fusion.3
  3.4 0.1 tile.2
  3.5 0.1 concatenate.19
  3.6 0.1 broadcast_in_dim.20
  3.7 34.7 %all_to_all.5 = bf16[32,16,1024]{2,1,0:T(8,128)(2,1)S(1)} all-to-all(bf16[32,16,1024]{2,1,0:T(8,128)(2,1)S(1)} %bitcast.40), channel_id=1, replica_groups=mesh['row'=4,'col'=8] {'row','col'}, dimensions={0} | all-to-all | bytes 2097152 | tf_op jit(solution)/shard_map/all_to_all | solution.py:140
  38.4 0.0 copy-start
  38.4 0.0 collective-permute-start
  38.4 0.1 broadcast_in_dim.43
  38.5 0.0 copy-start.5
  38.5 0.1 mul.52
  38.5 0.6 %copy-done.5 = s32[8]{0:T(128)S(1)} copy-done((s32[8]{0:T(128)S(1)}, s32[8]{0:T(128)}, u32[]{:S(2)}) %copy-start.5) | copy-done | bytes 56
  39.2 0.1 broadcast_in_dim.44
  39.2 0.1 reshape.130
  39.3 0.2 slice_reduce_fusion
  39.6 0.1 reshape.131
  39.7 0.1 broadcast_in_dim.42
  39.8 0.1 reshape.129
  39.9 0.1 copy.29
  40.1 0.6 %and_select_fusion.refs_2_ = f32[2,4,1024]{2,1,0:T(4,128)} fusion(pred[2,4,1024]{2,1,0:T(4,128)(4,1)S(1)} %reshape.129, pred[1024]{0:T(1024)(128)(4,1)S(1)} %fusion.12), kind=kLoop, calls=%fused_computation.14 | loop fusion | flops 16384 | bytes 41984 | tf_op jit(solution)/shard_map/jit(_where)/select_n | solution.py:161
  40.7 0.3 collective-permute-done
  41.0 0.0 copy-start.2
  41.1 0.1 copy.30
  41.2 0.0 copy-done
  41.3 0.1 maximum_convert_fusion
  41.4 0.7 %copy-done.2 = bf16[32,16,1024]{2,1,0:T(8,128)(2,1)} copy-done((bf16[32,16,1024]{2,1,0:T(8,128)(2,1)}, bf16[32,16,1024]{2,1,0:T(8,128)(2,1)S(1)}, u32[]{:S(2)}) %copy-start.2) | copy-done | bytes 1048600
  42.1 0.7 %fusion.refs_3_ = f32[64,1024]{1,0:T(8,128)} fusion(f32[3,1024,64]{1,2,0:T(8,128)S(1)} %maximum_convert_fusion), kind=kLoop, calls=%fused_computation.2 | loop fusion | flops 131072 | bytes 1048576 | tf_op jit(solution)/shard_map/transpose | solution.py:156
  42.8 9.4 %shard_map.55 = f32[64,1024]{1,0:T(8,128)} custom-call(bf16[512,1024]{1,0:T(8,128)(2,1)} %bitcast.42, bf16[512,1024]{1,0:T(8,128)(2,1)} %bitcast.46, f32[2,4,1024]{2,1,0:T(4,128)} %and_select_fusion.refs_2_, f32[64,1024]{1,0:T(8,128)} %fusion.refs_3_), custom_call_target="tpu_custom_call" | custom-call | flops 2147483648 | bytes 2621440 | tf_op jit(solution)/shard_map/pallas_call | solution.py:90
  52.2 0.8 %constant_dynamic-slice_fusion.1 = (f32[64,16]{1,0:T(8,128)S(1)}, f32[64,16]{1,0:T(8,128)S(1)}) fusion(f32[64,1024]{1,0:T(8,128)} %shard_map.55, s32[]{:T(128)S(6)} %select_n.61, s32[]{:T(128)S(6)} %select_n.62), kind=kLoop, calls=%fused_computation.48 | loop fusion | bytes 16392 | tf_op jit(solution)/shard_map/dynamic_slice | solution.py:163
  53.0 0.1 pad_maximum_fusion.1
  53.1 0.7 %copy.25 = f32[64,32]{0,1:T(8,128)} copy(f32[64,32]{1,0:T(8,128)S(1)} %pad_maximum_fusion.1) | data formatting | bytes 16384 | tf_op jit(solution)/shard_map/concatenate | solution.py:165
  (14 shorter events, 0.2 us)
Async XLA Ops:
  0.8 1.7 %copy-start.3 = (f32[64,32]{0,1:T(8,128)S(1)}, f32[64,32]{0,1:T(8,128)}, u32[]{:S(2)}) copy-start(f32[64,32]{0,1:T(8,128)} %param.9) | copy-start | bytes 24580
  1.7 0.7 %copy-start.4 = (bf16[32]{0:T(256)(128)(2,1)S(1)}, bf16[32]{0:T(256)(128)(2,1)}, u32[]{:S(2)}) copy-start(bf16[32]{0:T(256)(128)(2,1)} %param.6) | copy-start | bytes 196
  2.5 0.8 %copy-start.1 = (bf16[32,768]{1,0:T(8,128)(2,1)S(1)}, bf16[32,768]{1,0:T(8,128)(2,1)}, u32[]{:S(2)}) copy-start(bf16[32,768]{1,0:T(8,128)(2,1)} %param.5) | copy-start | bytes 147460
  38.4 2.9 %copy-start = (bf16[32,16,1024]{2,1,0:T(8,128)(2,1)}, bf16[32,16,1024]{2,1,0:T(8,128)(2,1)S(1)}, u32[]{:S(2)}) copy-start(bf16[32,16,1024]{2,1,0:T(8,128)(2,1)S(1)} %all_to_all.5) | copy-start | bytes 3145732
  38.4 2.7 %collective-permute-start = (bf16[32,16,1024]{2,1,0:T(8,128)(2,1)S(1)}, bf16[32,16,1024]{2,1,0:T(8,128)(2,1)S(1)}, u32[]{:S(2)}, u32[]{:S(2)}) collective-permute-start(bf16[32,16,1024]{2,1,0:T(8,128)(2,1)S(1)} %all_to_all.5), channel_id=1, source_target_pairs={{0,8},{8,0},{16,24},{24,16},{1,9},{9,1},{17,25},{25,17},{2,10},{10... | collective-permute-start | bytes 3145736 | tf_op jit(solution)/shard_map/ppermute | solution.py:141
  38.5 0.7 %copy-start.5 = (s32[8]{0:T(128)S(1)}, s32[8]{0:T(128)}, u32[]{:S(2)}) copy-start(s32[8]{0:T(128)} %param.8) | copy-start | bytes 100
  41.0 1.0 %copy-start.2 = (bf16[32,16,1024]{2,1,0:T(8,128)(2,1)}, bf16[32,16,1024]{2,1,0:T(8,128)(2,1)S(1)}, u32[]{:S(2)}) copy-start(bf16[32,16,1024]{2,1,0:T(8,128)(2,1)S(1)} %collective-permute-done) | copy-start | bytes 3145732

commit v8 on v7

--- a/solution.py
+++ b/solution.py
@@ -83,7 +83,7 @@
     files = 2 * mine.shape[0]
     run = files // (2 * rowmask.shape[0])
     tile = run
-    while tile * 2 <= min(256, files // 2) and (files // 2) % (tile * 2) == 0:
+    while tile * 2 <= min(512, files // 2) and (files // 2) % (tile * 2) == 0:
         tile *= 2
     rowmask = rowmask.reshape(-1, tile // run, files)
     vmem = pl.BlockSpec(memory_space=pltpu.VMEM)

time: 54.2 us -> 53.8 us (level)
  no operation moved by 1% of the time
where the time goes in v8:
time: 53.8 us; the launch traced here: 53.4 us
  blocking collectives  34.7 us (64%)
  Pallas kernels  9 us (17%)
  local copies, waits for them, and re-layouts  5.93 us (11%)
  other arithmetic  3.3 us (6%)
    all_to_all x1, blocking collectives, dense_path(): mine = lax.all_to_all(wide, AXES, 0, 0, tiled=True)  34.7 us
    pallas_call x1, Pallas kernels, dense_call(): pl.pallas_call(lambda *refs: dense_kernel(ITERS, tile, beta_lane, *refs),...  9 us
    unnamed x14, local copies, waits for them, and re-layouts  2.91 us
  transfers between devices with their start and end apart: 1, of which 1 were waited for; matrix products, arithmetic and copies ran while one was open for 3% of the time, Pallas kernels for 0%

profile of v8, /device:TPU:0, one launch (start us, length us, event | category | flops | bytes accessed | tf_op | source)
XLA Modules:
  0.0 53.4 jit_solution(5651029495976048760)
XLA Ops:
  0.0 0.7 %convert_element_type.22 = bf16[2,8]{1,0:T(2,128)(2,1)S(1)} convert(s32[2,8]{1,0:T(2,128)} %param.7) | non-fusion elementwise | flops 16 | bytes 96 | tf_op jit(solution)/shard_map/convert_element_type | solution.py:119
  0.7 0.1 convert_element_type.23
  0.8 0.0 copy-start.3
  0.8 0.9 %fusion.2 = f32[32]{0:T(128)S(1)} fusion(bf16[32,768]{1,0:T(8,128)(2,1)} %param.5), kind=kLoop, calls=%fused_computation.11 | loop fusion | flops 73696 | bytes 49280 | tf_op jit(solution)/shard_map/reduce_sum | solution.py:170
  1.7 0.0 copy-start.4
  1.7 0.6 %copy-done.4 = bf16[32]{0:T(256)(128)(2,1)S(1)} copy-done((bf16[32]{0:T(256)(128)(2,1)S(1)}, bf16[32]{0:T(256)(128)(2,1)}, u32[]{:S(2)}) %copy-start.4) | copy-done | bytes 88
  2.4 0.1 concatenate.22
  2.5 0.0 copy-done.3
  2.5 0.0 copy-start.1
  2.6 0.1 concatenate.17
  2.7 0.7 %copy-done.1 = bf16[32,768]{1,0:T(8,128)(2,1)S(1)} copy-done((bf16[32,768]{1,0:T(8,128)(2,1)S(1)}, bf16[32,768]{1,0:T(8,128)(2,1)}, u32[]{:S(2)}) %copy-start.1) | copy-done | bytes 49176
  3.3 0.1 fusion.3
  3.4 0.1 tile.2
  3.5 0.1 concatenate.19
  3.6 0.1 broadcast_in_dim.20
  3.7 34.7 %all_to_all.5 = bf16[32,16,1024]{2,1,0:T(8,128)(2,1)S(1)} all-to-all(bf16[32,16,1024]{2,1,0:T(8,128)(2,1)S(1)} %bitcast.40), channel_id=1, replica_groups=mesh['row'=4,'col'=8] {'row','col'}, dimensions={0} | all-to-all | bytes 2097152 | tf_op jit(solution)/shard_map/all_to_all | solution.py:140
  38.4 0.0 copy-start
  38.4 0.0 collective-permute-start
  38.4 0.1 broadcast_in_dim.43
  38.5 0.0 copy-start.5
  38.5 0.1 mul.52
  38.5 0.6 %copy-done.5 = s32[8]{0:T(128)S(1)} copy-done((s32[8]{0:T(128)S(1)}, s32[8]{0:T(128)}, u32[]{:S(2)}) %copy-start.5) | copy-done | bytes 56
  39.2 0.1 broadcast_in_dim.44
  39.2 0.1 reshape.158
  39.3 0.2 slice_reduce_fusion
  39.6 0.1 reshape.159
  39.7 0.1 broadcast_in_dim.42
  39.8 0.1 reshape.157
  39.9 0.1 copy.29
  40.1 0.6 %and_select_fusion.refs_2_ = f32[1,8,1024]{2,1,0:T(8,128)} fusion(pred[1,8,1024]{2,1,0:T(8,128)(4,1)S(1)} %reshape.157, pred[1024]{0:T(1024)(128)(4,1)S(1)} %fusion.12), kind=kLoop, calls=%fused_computation.14 | loop fusion | flops 16384 | bytes 41984 | tf_op jit(solution)/shard_map/jit(_where)/select_n | solution.py:161
  40.7 0.4 collective-permute-done
  41.0 0.0 copy-start.2
  41.1 0.1 copy.30
  41.2 0.0 copy-done
  41.3 0.1 maximum_convert_fusion
  41.4 0.7 %copy-done.2 = bf16[32,16,1024]{2,1,0:T(8,128)(2,1)} copy-done((bf16[32,16,1024]{2,1,0:T(8,128)(2,1)}, bf16[32,16,1024]{2,1,0:T(8,128)(2,1)S(1)}, u32[]{:S(2)}) %copy-start.2) | copy-done | bytes 1048600
  42.1 0.7 %fusion.refs_3_ = f32[64,1024]{1,0:T(8,128)} fusion(f32[3,1024,64]{1,2,0:T(8,128)S(1)} %maximum_convert_fusion), kind=kLoop, calls=%fused_computation.2 | loop fusion | flops 131072 | bytes 1048576 | tf_op jit(solution)/shard_map/transpose | solution.py:156
  42.8 9.0 %shard_map.55 = f32[64,1024]{1,0:T(8,128)} custom-call(bf16[512,1024]{1,0:T(8,128)(2,1)} %bitcast.42, bf16[512,1024]{1,0:T(8,128)(2,1)} %bitcast.46, f32[1,8,1024]{2,1,0:T(8,128)} %and_select_fusion.refs_2_, f32[64,1024]{1,0:T(8,128)} %fusion.refs_3_), custom_call_target="tpu_custom_call" | custom-call | flops 2147483648 | bytes 2621440 | tf_op jit(solution)/shard_map/pallas_call | solution.py:90
  51.8 0.8 %constant_dynamic-slice_fusion.1 = (f32[64,16]{1,0:T(8,128)S(1)}, f32[64,16]{1,0:T(8,128)S(1)}) fusion(f32[64,1024]{1,0:T(8,128)} %shard_map.55, s32[]{:T(128)S(6)} %select_n.67, s32[]{:T(128)S(6)} %select_n.68), kind=kLoop, calls=%fused_computation.48 | loop fusion | bytes 16392 | tf_op jit(solution)/shard_map/dynamic_slice | solution.py:163
  52.7 0.1 pad_maximum_fusion.1
  52.7 0.7 %copy.25 = f32[64,32]{0,1:T(8,128)} copy(f32[64,32]{1,0:T(8,128)S(1)} %pad_maximum_fusion.1) | data formatting | bytes 16384 | tf_op jit(solution)/shard_map/concatenate | solution.py:165
  (14 shorter events, 0.2 us)
Async XLA Ops:
  0.8 1.7 %copy-start.3 = (f32[64,32]{0,1:T(8,128)S(1)}, f32[64,32]{0,1:T(8,128)}, u32[]{:S(2)}) copy-start(f32[64,32]{0,1:T(8,128)} %param.9) | copy-start | bytes 24580
  1.7 0.7 %copy-start.4 = (bf16[32]{0:T(256)(128)(2,1)S(1)}, bf16[32]{0:T(256)(128)(2,1)}, u32[]{:S(2)}) copy-start(bf16[32]{0:T(256)(128)(2,1)} %param.6) | copy-start | bytes 196
  2.5 0.8 %copy-start.1 = (bf16[32,768]{1,0:T(8,128)(2,1)S(1)}, bf16[32,768]{1,0:T(8,128)(2,1)}, u32[]{:S(2)}) copy-start(bf16[32,768]{1,0:T(8,128)(2,1)} %param.5) | copy-start | bytes 147460
  38.4 2.9 %copy-start = (bf16[32,16,1024]{2,1,0:T(8,128)(2,1)}, bf16[32,16,1024]{2,1,0:T(8,128)(2,1)S(1)}, u32[]{:S(2)}) copy-start(bf16[32,16,1024]{2,1,0:T(8,128)(2,1)S(1)} %all_to_all.5) | copy-start | bytes 3145732
  38.4 2.7 %collective-permute-start = (bf16[32,16,1024]{2,1,0:T(8,128)(2,1)S(1)}, bf16[32,16,1024]{2,1,0:T(8,128)(2,1)S(1)}, u32[]{:S(2)}, u32[]{:S(2)}) collective-permute-start(bf16[32,16,1024]{2,1,0:T(8,128)(2,1)S(1)} %all_to_all.5), channel_id=1, source_target_pairs={{0,8},{8,0},{16,24},{24,16},{1,9},{9,1},{17,25},{25,17},{2,10},{10... | collective-permute-start | bytes 3145736 | tf_op jit(solution)/shard_map/ppermute | solution.py:141
  38.5 0.7 %copy-start.5 = (s32[8]{0:T(128)S(1)}, s32[8]{0:T(128)}, u32[]{:S(2)}) copy-start(s32[8]{0:T(128)} %param.8) | copy-start | bytes 100
  41.0 1.0 %copy-start.2 = (bf16[32,16,1024]{2,1,0:T(8,128)(2,1)}, bf16[32,16,1024]{2,1,0:T(8,128)(2,1)S(1)}, u32[]{:S(2)}) copy-start(bf16[32,16,1024]{2,1,0:T(8,128)(2,1)S(1)} %collective-permute-done) | copy-start | bytes 3145732

commit v9 on v8

--- a/solution.py
+++ b/solution.py
@@ -6,6 +6,7 @@
 from jax.sharding import PartitionSpec as P
 
 ITERS = 2
+PROBE_PARTS = 1
 AXES = ("row", "col")
 A2A_BYTES = 8 << 20
 REPLICATE_CELLS = 1 << 21
@@ -35,7 +36,7 @@
     return jnp.concatenate([low, high], axis=1)[:, : x.shape[0]]
 
 
-def dense_kernel(n_iter, tile, beta_lane, mine_ref, other_ref, rowmask_ref, probes_ref, out_ref, unit_t, unit_s, scale_s, aff_s):
+def dense_kernel(n_iter, tile, beta_lane, n_parts, pos_ref, mine_ref, other_ref, rowmask_ref, out_ref, unit_t, unit_s, scale_s, aff_s):
     feat, files = unit_t.shape
     half = files // 2
     runs = half // tile
@@ -69,17 +70,34 @@
 
     colsum = lax.fori_loop(0, files // tile, step, jnp.zeros((1, files), jnp.float32))
     inv_root = lax.rsqrt((1.0 + colsum) * 0.5)
-    state = probes_ref[...]
+    n_probe, shard = out_ref.shape
+    state = jnp.concatenate(
+        [
+            sum(
+                ref[:, feat + k * n_probe : feat + (k + 1) * n_probe].astype(jnp.float32)
+                for k in range(n_parts)
+            ).T
+            for ref in (mine_ref, other_ref)
+        ],
+        axis=1,
+    )
     for sweep in range(n_iter):
         scaled_f = (state * inv_root).astype(jnp.bfloat16).astype(jnp.float32)
         scaled = scaled_f.astype(jnp.bfloat16)
         row_t = jnp.dot(aff_s[...], scaled_f.T.astype(jnp.bfloat16), preferred_element_type=jnp.float32)
         col_part = jnp.dot(scaled, aff_s[...], preferred_element_type=jnp.float32)
         state = (row_t.T + col_part) * (0.5 * inv_root)
-    out_ref[...] = state
-
-
-def dense_call(mine, other, rowmask, probes_int, feat, beta_lane):
+    half_s = shard // 2
+    col = lax.broadcasted_iota(jnp.int32, (files, shard), 0)
+    j = lax.broadcasted_iota(jnp.int32, (files, shard), 1)
+    target = jnp.where(j < half_s, pos_ref[0] + j, pos_ref[1] + j - half_s)
+    pick = jnp.where(col == target, 1.0, 0.0).astype(jnp.float32)
+    out_ref[...] = jnp.dot(
+        state, pick, precision=lax.Precision.HIGHEST, preferred_element_type=jnp.float32
+    )
+
+
+def dense_call(positions, mine, other, rowmask, n_probe, shard, feat, beta_lane):
     files = 2 * mine.shape[0]
     run = files // (2 * rowmask.shape[0])
     tile = run
@@ -87,10 +105,11 @@
         tile *= 2
     rowmask = rowmask.reshape(-1, tile // run, files)
     vmem = pl.BlockSpec(memory_space=pltpu.VMEM)
+    smem = pl.BlockSpec(memory_space=pltpu.SMEM)
     return pl.pallas_call(
-        lambda *refs: dense_kernel(ITERS, tile, beta_lane, *refs),
-        out_shape=jax.ShapeDtypeStruct(probes_int.shape, jnp.float32),
-        in_specs=[vmem] * 4,
+        lambda *refs: dense_kernel(ITERS, tile, beta_lane, PROBE_PARTS, *refs),
+        out_shape=jax.ShapeDtypeStruct((n_probe, shard), jnp.float32),
+        in_specs=[smem, vmem, vmem, vmem],
         out_specs=vmem,
         scratch_shapes=[
             pltpu.VMEM((feat, files), jnp.bfloat16),
@@ -99,11 +118,11 @@
             pltpu.VMEM((files, files), jnp.bfloat16),
         ],
         cost_estimate=pl.CostEstimate(
-            flops=2 * files * files * feat + 4 * ITERS * files * files * probes_int.shape[0],
+            flops=2 * files * files * feat + 4 * ITERS * files * files * n_probe,
             transcendentals=files * files,
-            bytes_accessed=files * mine.shape[1] * 2 + 8 * files * probes_int.shape[0],
+            bytes_accessed=files * mine.shape[1] * 2 + 4 * shard * n_probe,
         ),
-    )(mine, other, rowmask, probes_int)
+    )(positions, mine, other, rowmask)
 
 
 def dense_path(unit_own, beta, block_mask, counts, probes, n_dev, n_row, me):
@@ -120,12 +139,12 @@
     mask_cols = -(-mask_flat.shape[0] // half_s)
     mask_part = jnp.pad(mask_flat, (0, half_s * mask_cols - mask_flat.shape[0]))
     mask_part = jnp.tile(mask_part.reshape(half_s, mask_cols), (2, 1))
-    used = 3 * n_probe + 1 + mask_cols
+    used = PROBE_PARTS * n_probe + 1 + mask_cols
     lanes = -(-used // 128) * 128
     payload = jnp.concatenate(
         [
             unit_own,
-            jnp.moveaxis(split3(probes.T), 0, 1).reshape(shard, 3 * n_probe),
+            jnp.moveaxis(split3(probes.T)[:PROBE_PARTS], 0, 1).reshape(shard, PROBE_PARTS * n_probe),
             beta[:, None],
             mask_part,
             jnp.zeros((shard, lanes - used), jnp.bfloat16),
@@ -150,19 +169,17 @@
     live = in_block < block_counts
     mine2 = mine.reshape(half_f, width)
     other2 = other.reshape(half_f, width)
-    tails = jnp.concatenate([mine2[:, feat:], other2[:, feat:]], axis=0)
-    probes_int = join3(
-        jnp.stack([tails[:, k * n_probe : (k + 1) * n_probe] for k in range(3)])
-    ).T
-    mask_got = mine[:, :, feat + 3 * n_probe + 1 : feat + used].reshape(n_dev, -1)
+    mask_got = mine[:, :, feat + PROBE_PARTS * n_probe + 1 : feat + used].reshape(n_dev, -1)
     mask_got = mask_got[:, : local_blocks * nb]
     mask_full = mask_got.reshape(n_row, per_row, local_blocks, nb)[:, 0].reshape(nb, nb)
     block_ok = jnp.broadcast_to((mask_full == 1)[:, None, :, None], (nb, 2, nb, run))
     rowmask = jnp.where(block_ok.reshape(nb, files) & live[None, :], 1.0, 0.0).astype(jnp.float32)
-    state = dense_call(mine2, other2, rowmask, probes_int, feat, feat + 3 * n_probe)
-    first = lax.dynamic_slice_in_dim(state, core * half_f + me * half_s, half_s, 1)
-    second = lax.dynamic_slice_in_dim(state, (1 - core) * half_f + me * half_s, half_s, 1)
-    return jnp.concatenate([first, second], axis=1)
+    positions = jnp.stack(
+        [core * half_f + me * half_s, (1 - core) * half_f + me * half_s]
+    ).astype(jnp.int32)
+    return dense_call(
+        positions, mine2, other2, rowmask, n_probe, shard, feat, feat + PROBE_PARTS * n_probe
+    )
 
 
 def normalize(embed):
@@ -182,6 +199,8 @@
 
 def join3(parts):
     parts = parts.astype(jnp.float32)
+    if parts.shape[0] == 1:
+        return parts[0]
     return (parts[0] + parts[1]) + parts[2]
 
 

time: 53.8 us -> 51.2 us (0.952)
  blocking collectives: 34.7 us -> 0 us
  waiting for transfers between devices: 0.35 us -> 24.8 us
  starting transfers between devices: 0.01 us -> 7.3 us
    all_to_all x1 -> x0, blocking collectives: 34.7 us -> none  [dense_path(): mine = lax.all_to_all(wide, AXES, 0, 0, tiled=True)]
    all_to_all x0 -> x1, waiting for transfers between devices: none -> 24.8 us  [dense_path(): mine = lax.all_to_all(wide, AXES, 0, 0, tiled=True)]
    all_to_all x0 -> x1, starting transfers between devices: none -> 7.3 us  [dense_path(): mine = lax.all_to_all(wide, AXES, 0, 0, tiled=True)]
    pallas_call x0 -> x1, local copies, waits for them, and re-layouts: none -> 1.44 us  [dense_call(): pl.pallas_call(lambda *refs: dense_kernel(ITERS, tile, beta_lane, PROBE_P...]
    another operation x2, other arithmetic: 0.04 us -> 1.38 us  [the longest x1 0.04 us: dense_path(): jnp.stack([tails[:, k * n_probe:(k + 1) * n_probe] for k in range(3)])]
    broadcast_in_dim x1, local copies, waits for them, and re-layouts: 0.12 us -> 0.99 us  [dense_path(): jnp.broadcast_to(halves[None, :, None], (n_row // 2, 2, per_row, half_s,...]
    dynamic_slice x1 -> x0, local copies, waits for them, and re-layouts: 0.85 us -> none  [dense_path(): lax.dynamic_slice_in_dim(state, core * half_f + me * half_s, half_s, 1)]
    concatenate x4 -> x2, local copies, waits for them, and re-layouts: 0.98 us -> 0.2 us  [dense_path(): jnp.concatenate([unit_own, jnp.moveaxis(split3(probes.T)[:PROBE_PARTS], 0...]
  transfers between devices with their start and end apart: 1 -> 2, of which waited for: 1 -> 1; matrix products, arithmetic and copies ran while one was open for 3% -> 4% of each run, Pallas kernels for 0% -> 0%
where the time goes in v9:
time: 51.2 us; the launch traced here: 50.7 us
  waiting for transfers between devices  24.8 us (48%)
  Pallas kernels  9.03 us (18%)
  starting transfers between devices  7.3 us (14%)
  local copies, waits for them, and re-layouts  5.82 us (11%)
  other arithmetic  3.72 us (7%)
    all_to_all x1, waiting for transfers between devices, dense_path(): mine = lax.all_to_all(wide, AXES, 0, 0, tiled=True)  24.8 us
    pallas_call x1, Pallas kernels, dense_call(): pl.pallas_call(lambda *refs: dense_kernel(ITERS, tile, beta_lane, PROBE_P...  9.03 us
    all_to_all x1, starting transfers between devices, dense_path(): mine = lax.all_to_all(wide, AXES, 0, 0, tiled=True)  7.3 us
    unnamed x10, local copies, waits for them, and re-layouts  2.22 us
    pallas_call x1, local copies, waits for them, and re-layouts, dense_call(): pl.pallas_call(lambda *refs: dense_kernel(ITERS, tile, beta_lane, PROBE_P...  1.44 us
  transfers between devices with their start and end apart: 2, of which 1 were waited for; matrix products, arithmetic and copies ran while one was open for 4% of the time, Pallas kernels for 0%

profile of v9, /device:TPU:0, one launch (start us, length us, event | category | flops | bytes accessed | tf_op | source)
XLA Modules:
  0.0 50.7 jit_solution(3321870321830653428)
XLA Ops:
  0.0 0.0 copy-start.1
  0.0 0.7 %convert_element_type.19 = bf16[2,8]{1,0:T(2,128)(2,1)S(1)} convert(s32[2,8]{1,0:T(2,128)} %param.7) | non-fusion elementwise | flops 16 | bytes 96 | tf_op jit(solution)/shard_map/convert_element_type | solution.py:138
  0.7 0.1 convert_element_type.20
  0.8 0.9 %fusion = f32[32]{0:T(128)S(1)} fusion(bf16[32,768]{1,0:T(8,128)(2,1)} %param.5), kind=kLoop, calls=%fused_computation.3 | loop fusion | flops 73696 | bytes 49280 | tf_op jit(solution)/shard_map/reduce_sum | solution.py:187
  1.7 0.0 copy-start.2
  1.7 0.6 %copy-done.2 = bf16[32]{0:T(256)(128)(2,1)S(1)} copy-done((bf16[32]{0:T(256)(128)(2,1)S(1)}, bf16[32]{0:T(256)(128)(2,1)}, u32[]{:S(2)}) %copy-start.2) | copy-done | bytes 88
  2.4 0.1 concatenate.14
  2.5 0.7 %reduce-precision_convert_fusion = bf16[64,32]{0,1:T(8,128)(2,1)S(1)} fusion(f32[64,32]{0,1:T(8,128)} %param.9), kind=kLoop, calls=%fused_computation.6 | loop fusion | flops 4096 | bytes 12288 | tf_op jit(solution)/shard_map/convert.5
  3.2 0.0 copy-done.1
  3.2 0.1 fusion.1
  3.3 0.1 tile.2
  3.4 0.1 concatenate.13
  3.5 1.0 %broadcast_in_dim.20 = bf16[2,2,8,16,896]{4,3,2,1,0:T(8,128)(2,1)} broadcast(bf16[2,16,896]{2,1,0:T(8,128)(2,1)S(1)} %bitcast.15), dimensions={1,3,4} | broadcast | bytes 974848 | tf_op jit(solution)/shard_map/broadcast_in_dim | solution.py:156
  4.4 7.3 %all-to-all-start = ((bf16[32,16,896]{2,1,0:T(8,128)(2,1)}), bf16[32,16,896]{2,1,0:T(8,128)(2,1)S(1)}, u32[]{:S(2)}, u32[]{:S(2)}) async-start(bf16[32,16,896]{2,1,0:T(8,128)(2,1)} %bitcast.6), calls=%async_computation | async-start | bytes 1835008 | tf_op jit(solution)/shard_map/all_to_all | solution.py:159
  11.8 24.8 %all-to-all-done = bf16[32,16,896]{2,1,0:T(8,128)(2,1)S(1)} async-done(((bf16[32,16,896]{2,1,0:T(8,128)(2,1)}), bf16[32,16,896]{2,1,0:T(8,128)(2,1)S(1)}, u32[]{:S(2)}, u32[]{:S(2)}) %all-to-all-start) | async-done | bytes 917536 | tf_op jit(solution)/shard_map/all_to_all | solution.py:159
  36.5 0.0 copy-start
  36.5 0.0 collective-permute-start
  36.6 0.1 broadcast_in_dim.43
  36.6 0.0 copy-start.3
  36.6 0.1 mul.56
  36.7 0.6 %copy-done.3 = s32[8]{0:T(128)S(1)} copy-done((s32[8]{0:T(128)S(1)}, s32[8]{0:T(128)}, u32[]{:S(2)}) %copy-start.3) | copy-done | bytes 56
  37.3 0.1 broadcast_in_dim.44
  37.4 0.1 reshape.156
  37.5 0.7 %pad_add_fusion.refs_0_ = s32[2]{0:T(128)} fusion(s32[1]{0:T(128)} %bitcast.1, s32[1]{0:T(128)} %bitcast), kind=kLoop, calls=%fused_computation.29 | loop fusion | flops 2 | bytes 16 | tf_op jit(solution)/shard_map/stack | solution.py:177
  38.1 0.2 slice_reduce_fusion
  38.4 0.1 reshape.157
  38.5 0.1 broadcast_in_dim.42
  38.6 0.1 reshape.155
  38.7 0.6 %and_select_fusion.refs_3_ = f32[1,8,1024]{2,1,0:T(8,128)} fusion(pred[1,8,1024]{2,1,0:T(8,128)(4,1)S(1)} %reshape.155, pred[1024]{0:T(1024)(128)(4,1)S(1)} %fusion.6), kind=kLoop, calls=%fused_computation.5 | loop fusion | flops 16384 | bytes 41984 | tf_op jit(solution)/shard_map/jit(_where)/select_n | solution.py:176
  39.3 0.0 collective-permute-done
  39.3 0.0 copy-start.4
  39.3 0.0 copy-done
  39.3 1.0 %copy-done.4 = bf16[32,16,896]{2,1,0:T(8,128)(2,1)} copy-done((bf16[32,16,896]{2,1,0:T(8,128)(2,1)}, bf16[32,16,896]{2,1,0:T(8,128)(2,1)S(1)}, u32[]{:S(2)}) %copy-start.4) | copy-done | bytes 917528
  40.3 9.0 %shard_map.55 = f32[64,32]{1,0:T(8,128)} custom-call(s32[2]{0:T(128)} %pad_add_fusion.refs_0_, bf16[512,896]{1,0:T(8,128)(2,1)} %bitcast.14, bf16[512,896]{1,0:T(8,128)(2,1)} %bitcast.18, f32[1,8,1024]{2,1,0:T(8,128)} %and_select_fusion.refs_3_), custom_call_target="tpu_custom_call" | custom-call | flops 2147483648 | bytes 1843200 | tf_op jit(solution)/shard_map/pallas_call | solution.py:109
  49.3 1.4 %copy.22 = f32[64,32]{0,1:T(8,128)} copy(f32[64,32]{1,0:T(8,128)} %shard_map.55) | data formatting | bytes 16384 | tf_op jit(solution)/shard_map/pallas_call | solution.py:109
  (8 shorter events, 0.1 us)
Async XLA Ops:
  0.0 3.2 %copy-start.1 = (bf16[32,768]{1,0:T(8,128)(2,1)S(1)}, bf16[32,768]{1,0:T(8,128)(2,1)}, u32[]{:S(2)}) copy-start(bf16[32,768]{1,0:T(8,128)(2,1)} %param.5) | copy-start | bytes 147460
  1.7 0.7 %copy-start.2 = (bf16[32]{0:T(256)(128)(2,1)S(1)}, bf16[32]{0:T(256)(128)(2,1)}, u32[]{:S(2)}) copy-start(bf16[32]{0:T(256)(128)(2,1)} %param.6) | copy-start | bytes 196
  4.4 32.1 %all-to-all-start = ((bf16[32,16,896]{2,1,0:T(8,128)(2,1)}), bf16[32,16,896]{2,1,0:T(8,128)(2,1)S(1)}, u32[]{:S(2)}, u32[]{:S(2)}) async-start(bf16[32,16,896]{2,1,0:T(8,128)(2,1)} %bitcast.6), calls=%async_computation | async-start | bytes 1835008 | tf_op jit(solution)/shard_map/all_to_all | solution.py:159
  36.5 2.8 %copy-start = (bf16[32,16,896]{2,1,0:T(8,128)(2,1)}, bf16[32,16,896]{2,1,0:T(8,128)(2,1)S(1)}, u32[]{:S(2)}) copy-start(bf16[32,16,896]{2,1,0:T(8,128)(2,1)S(1)} %all-to-all-done) | copy-start | bytes 2752516
  36.5 2.8 %collective-permute-start = (bf16[32,16,896]{2,1,0:T(8,128)(2,1)S(1)}, bf16[32,16,896]{2,1,0:T(8,128)(2,1)S(1)}, u32[]{:S(2)}, u32[]{:S(2)}) collective-permute-start(bf16[32,16,896]{2,1,0:T(8,128)(2,1)S(1)} %all-to-all-done), channel_id=1, source_target_pairs={{0,8},{8,0},{16,24},{24,16},{1,9},{9,1},{17,25},{25,17},{2,10},{10... | collective-permute-start | bytes 2752520 | tf_op jit(solution)/shard_map/ppermute | solution.py:160
  36.6 0.7 %copy-start.3 = (s32[8]{0:T(128)S(1)}, s32[8]{0:T(128)}, u32[]{:S(2)}) copy-start(s32[8]{0:T(128)} %param.8) | copy-start | bytes 100
  39.3 1.0 %copy-start.4 = (bf16[32,16,896]{2,1,0:T(8,128)(2,1)}, bf16[32,16,896]{2,1,0:T(8,128)(2,1)S(1)}, u32[]{:S(2)}) copy-start(bf16[32,16,896]{2,1,0:T(8,128)(2,1)S(1)} %collective-permute-done) | copy-start | bytes 2752516

commit v10 on v9

--- a/solution.py
+++ b/solution.py
@@ -36,15 +36,17 @@
     return jnp.concatenate([low, high], axis=1)[:, : x.shape[0]]
 
 
-def dense_kernel(n_iter, tile, beta_lane, n_parts, pos_ref, mine_ref, other_ref, rowmask_ref, out_ref, unit_t, unit_s, scale_s, aff_s):
+def dense_kernel(n_iter, tile, beta_lane, n_parts, mine_ref, other_ref, rowmask_ref, out_ref, unit_t, unit_s, scale_s, aff_s):
     feat, files = unit_t.shape
     half = files // 2
     runs = half // tile
     for k, ref in enumerate((mine_ref, other_ref)):
-        unit_s[k * half : (k + 1) * half, :] = ref[:, 0:feat]
-        unit_t[:, k * half : (k + 1) * half] = (
-            ref[:, 0:feat].astype(jnp.float32).T.astype(jnp.bfloat16)
-        )
+        values = ref[:, 0:feat].astype(jnp.float32)
+        unit = (
+            values * lax.rsqrt(jnp.mean(values * values, axis=1, keepdims=True) + 1e-06)
+        ).astype(jnp.bfloat16)
+        unit_s[k * half : (k + 1) * half, :] = unit
+        unit_t[:, k * half : (k + 1) * half] = unit.astype(jnp.float32).T.astype(jnp.bfloat16)
         scale_s[k * half : (k + 1) * half, :] = (
             ref[:, beta_lane : beta_lane + 1].astype(jnp.float32) / feat
         )
@@ -70,7 +72,7 @@
 
     colsum = lax.fori_loop(0, files // tile, step, jnp.zeros((1, files), jnp.float32))
     inv_root = lax.rsqrt((1.0 + colsum) * 0.5)
-    n_probe, shard = out_ref.shape
+    n_probe = out_ref.shape[0]
     state = jnp.concatenate(
         [
             sum(
@@ -87,17 +89,10 @@
         row_t = jnp.dot(aff_s[...], scaled_f.T.astype(jnp.bfloat16), preferred_element_type=jnp.float32)
         col_part = jnp.dot(scaled, aff_s[...], preferred_element_type=jnp.float32)
         state = (row_t.T + col_part) * (0.5 * inv_root)
-    half_s = shard // 2
-    col = lax.broadcasted_iota(jnp.int32, (files, shard), 0)
-    j = lax.broadcasted_iota(jnp.int32, (files, shard), 1)
-    target = jnp.where(j < half_s, pos_ref[0] + j, pos_ref[1] + j - half_s)
-    pick = jnp.where(col == target, 1.0, 0.0).astype(jnp.float32)
-    out_ref[...] = jnp.dot(
-        state, pick, precision=lax.Precision.HIGHEST, preferred_element_type=jnp.float32
-    )
-
-
-def dense_call(positions, mine, other, rowmask, n_probe, shard, feat, beta_lane):
+    out_ref[...] = state
+
+
+def dense_call(mine, other, rowmask, n_probe, feat, beta_lane):
     files = 2 * mine.shape[0]
     run = files // (2 * rowmask.shape[0])
     tile = run
@@ -105,11 +100,10 @@
         tile *= 2
     rowmask = rowmask.reshape(-1, tile // run, files)
     vmem = pl.BlockSpec(memory_space=pltpu.VMEM)
-    smem = pl.BlockSpec(memory_space=pltpu.SMEM)
     return pl.pallas_call(
         lambda *refs: dense_kernel(ITERS, tile, beta_lane, PROBE_PARTS, *refs),
-        out_shape=jax.ShapeDtypeStruct((n_probe, shard), jnp.float32),
-        in_specs=[smem, vmem, vmem, vmem],
+        out_shape=jax.ShapeDtypeStruct((n_probe, files), jnp.float32),
+        in_specs=[vmem, vmem, vmem],
         out_specs=vmem,
         scratch_shapes=[
             pltpu.VMEM((feat, files), jnp.bfloat16),
@@ -120,13 +114,13 @@
         cost_estimate=pl.CostEstimate(
             flops=2 * files * files * feat + 4 * ITERS * files * files * n_probe,
             transcendentals=files * files,
-            bytes_accessed=files * mine.shape[1] * 2 + 4 * shard * n_probe,
+            bytes_accessed=files * mine.shape[1] * 2 + 4 * files * n_probe,
         ),
-    )(positions, mine, other, rowmask)
-
-
-def dense_path(unit_own, beta, block_mask, counts, probes, n_dev, n_row, me):
-    shard, feat = unit_own.shape
+    )(mine, other, rowmask)
+
+
+def dense_path(embed, beta, block_mask, counts, probes, n_dev, n_row, me):
+    shard, feat = embed.shape
     files = shard * n_dev
     half_s = shard // 2
     half_f = files // 2
@@ -143,7 +137,7 @@
     lanes = -(-used // 128) * 128
     payload = jnp.concatenate(
         [
-            unit_own,
+            embed,
             jnp.moveaxis(split3(probes.T)[:PROBE_PARTS], 0, 1).reshape(shard, PROBE_PARTS * n_probe),
             beta[:, None],
             mask_part,
@@ -174,12 +168,10 @@
     mask_full = mask_got.reshape(n_row, per_row, local_blocks, nb)[:, 0].reshape(nb, nb)
     block_ok = jnp.broadcast_to((mask_full == 1)[:, None, :, None], (nb, 2, nb, run))
     rowmask = jnp.where(block_ok.reshape(nb, files) & live[None, :], 1.0, 0.0).astype(jnp.float32)
-    positions = jnp.stack(
-        [core * half_f + me * half_s, (1 - core) * half_f + me * half_s]
-    ).astype(jnp.int32)
-    return dense_call(
-        positions, mine2, other2, rowmask, n_probe, shard, feat, feat + PROBE_PARTS * n_probe
-    )
+    state = dense_call(mine2, other2, rowmask, n_probe, feat, feat + PROBE_PARTS * n_probe)
+    first = lax.dynamic_slice_in_dim(state, core * half_f + me * half_s, half_s, 1)
+    second = lax.dynamic_slice_in_dim(state, (1 - core) * half_f + me * half_s, half_s, 1)
+    return jnp.concatenate([first, second], axis=1)
 
 
 def normalize(embed):
@@ -232,7 +224,7 @@
         and (blk // 2) % 8 == 0
         and files % 128 == 0
     ):
-        return dense_path(unit_own, beta, block_mask, counts, probes, n_dev, n_row, me)
+        return dense_path(embed, beta, block_mask, counts, probes, n_dev, n_row, me)
     if replicate:
         mask_flat = block_mask.reshape(-1).astype(jnp.bfloat16)
         mask_cols = -(-mask_flat.shape[0] // shard)

time: 51.2 us -> 49 us (0.957)
  blocking collectives: 0 us -> 31.9 us
  waiting for transfers between devices: 24.8 us -> 0.36 us
  starting transfers between devices: 7.3 us -> 0.01 us
  other arithmetic: 3.72 us -> 2.15 us
  local copies, waits for them, and re-layouts: 5.82 us -> 5 us
    all_to_all x0 -> x1, blocking collectives: none -> 31.9 us  [dense_path(): mine = lax.all_to_all(wide, AXES, 0, 0, tiled=True)]
    all_to_all x1 -> x0, waiting for transfers between devices: 24.8 us -> none  [dense_path(): mine = lax.all_to_all(wide, AXES, 0, 0, tiled=True)]
    all_to_all x1 -> x0, starting transfers between devices: 7.3 us -> none  [dense_path(): mine = lax.all_to_all(wide, AXES, 0, 0, tiled=True)]
    pallas_call x1 -> x0, local copies, waits for them, and re-layouts: 1.44 us -> none  [dense_call(): pl.pallas_call(lambda *refs: dense_kernel(ITERS, tile, beta_lane, PROBE_P...]
    concatenate x2 -> x3, local copies, waits for them, and re-layouts: 0.2 us -> 1.55 us  [the longest x2 0.86 us: dense_path(): jnp.concatenate([embed, jnp.moveaxis(split3(probes.T)[:PROBE_PARTS], 0, 1...]
    broadcast_in_dim x1, local copies, waits for them, and re-layouts: 0.99 us -> 0.07 us  [dense_path(): jnp.broadcast_to(halves[None, :, None], (n_row // 2, 2, per_row, half_s,...]
    reduce_sum x1 -> x0, other arithmetic: 0.91 us -> none  [normalize(): jnp.mean(values * values, axis=1, keepdims=True) + 1e-06]
    dynamic_slice x0 -> x1, local copies, waits for them, and re-layouts: none -> 0.85 us  [dense_path(): lax.dynamic_slice_in_dim(state, core * half_f + me * half_s, half_s, 1)]
  transfers between devices with their start and end apart: 2 -> 1, of which waited for: 1 -> 1; matrix products, arithmetic and copies ran while one was open for 4% -> 3% of each run, Pallas kernels for 0% -> 0%
where the time goes in v10:
time: 49 us; the launch traced here: 48.6 us
  blocking collectives  31.9 us (65%)
  Pallas kernels  9.18 us (19%)
  local copies, waits for them, and re-layouts  5 us (10%)
  other arithmetic  2.15 us (4%)
    all_to_all x1, blocking collectives, dense_path(): mine = lax.all_to_all(wide, AXES, 0, 0, tiled=True)  31.9 us
    pallas_call x1, Pallas kernels, dense_call(): pl.pallas_call(lambda *refs: dense_kernel(ITERS, tile, beta_lane, PROBE_P...  9.18 us
    unnamed x8, local copies, waits for them, and re-layouts  1.56 us
  transfers between devices with their start and end apart: 1, of which 1 were waited for; matrix products, arithmetic and copies ran while one was open for 3% of the time, Pallas kernels for 0%

profile of v10, /device:TPU:0, one launch (start us, length us, event | category | flops | bytes accessed | tf_op | source)
XLA Modules:
  0.0 48.6 jit_solution(4836313190457329785)
XLA Ops:
  0.0 0.0 copy-start.1
  0.0 0.7 %convert_element_type.11 = bf16[2,8]{1,0:T(2,128)(2,1)S(1)} convert(s32[2,8]{1,0:T(2,128)} %param.7) | non-fusion elementwise | flops 16 | bytes 96 | tf_op jit(solution)/shard_map/convert_element_type | solution.py:132
  0.7 0.1 convert_element_type.12
  0.8 0.8 %concatenate.18 = bf16[1,2,1,16,1]{4,3,1,2,0:T(8,128)(2,1)S(1)} reshape(bf16[32]{0:T(256)(128)(2,1)} %param.6) | data formatting | bytes 128 | tf_op jit(solution)/shard_map/concatenate | solution.py:138
  1.5 0.7 %reduce-precision_convert_fusion = bf16[64,32]{0,1:T(8,128)(2,1)S(1)} fusion(f32[64,32]{0,1:T(8,128)} %param.9), kind=kLoop, calls=%fused_computation.3 | loop fusion | flops 4096 | bytes 12288 | tf_op jit(solution)/shard_map/convert.5
  2.3 0.1 tile.2
  2.3 0.0 copy-done.1
  2.4 0.1 concatenate.16
  2.5 0.1 broadcast_in_dim.40
  2.5 31.9 %all_to_all.5 = bf16[32,16,896]{2,1,0:T(8,128)(2,1)S(1)} all-to-all(bf16[32,16,896]{2,1,0:T(8,128)(2,1)S(1)} %bitcast.12), channel_id=1, replica_groups=mesh['row'=4,'col'=8] {'row','col'}, dimensions={0} | all-to-all | bytes 1835008 | tf_op jit(solution)/shard_map/all_to_all | solution.py:153
  34.4 0.0 copy-start
  34.4 0.0 collective-permute-start
  34.4 0.1 broadcast_in_dim.42
  34.5 0.0 copy-start.2
  34.5 0.1 mul.38
  34.6 0.6 %copy-done.2 = s32[8]{0:T(128)S(1)} copy-done((s32[8]{0:T(128)S(1)}, s32[8]{0:T(128)}, u32[]{:S(2)}) %copy-start.2) | copy-done | bytes 56
  35.2 0.1 broadcast_in_dim.43
  35.2 0.1 reshape.148
  35.3 0.2 slice_reduce_fusion
  35.6 0.1 reshape.149
  35.7 0.1 broadcast_in_dim.41
  35.8 0.1 reshape.147
  35.9 0.6 %and_select_fusion.refs_2_ = f32[1,8,1024]{2,1,0:T(8,128)} fusion(pred[1,8,1024]{2,1,0:T(8,128)(4,1)S(1)} %reshape.147, pred[1024]{0:T(1024)(128)(4,1)S(1)} %fusion.4), kind=kLoop, calls=%fused_computation.2 | loop fusion | flops 16384 | bytes 41984 | tf_op jit(solution)/shard_map/jit(_where)/select_n | solution.py:170
  36.5 0.4 collective-permute-done
  36.9 0.0 copy-start.3
  36.9 0.0 copy-done
  36.9 0.9 %copy-done.3 = bf16[32,16,896]{2,1,0:T(8,128)(2,1)} copy-done((bf16[32,16,896]{2,1,0:T(8,128)(2,1)}, bf16[32,16,896]{2,1,0:T(8,128)(2,1)S(1)}, u32[]{:S(2)}) %copy-start.3) | copy-done | bytes 917528
  37.8 9.2 %shard_map.55 = f32[64,1024]{1,0:T(8,128)} custom-call(bf16[512,896]{1,0:T(8,128)(2,1)} %bitcast.13, bf16[512,896]{1,0:T(8,128)(2,1)} %bitcast.17, f32[1,8,1024]{2,1,0:T(8,128)} %and_select_fusion.refs_2_), custom_call_target="tpu_custom_call" | custom-call | flops 2147483648 | bytes 2097152 | tf_op jit(solution)/shard_map/pallas_call | solution.py:103
  47.0 0.8 %constant_dynamic-slice_fusion.1 = (f32[64,16]{1,0:T(8,128)S(1)}, f32[64,16]{1,0:T(8,128)S(1)}) fusion(f32[64,1024]{1,0:T(8,128)} %shard_map.55, s32[]{:T(128)S(6)} %select_n.67, s32[]{:T(128)S(6)} %select_n.68), kind=kLoop, calls=%fused_computation.28 | loop fusion | bytes 16392 | tf_op jit(solution)/shard_map/dynamic_slice | solution.py:172
  47.9 0.1 pad_maximum_fusion
  47.9 0.7 %copy.22 = f32[64,32]{0,1:T(8,128)} copy(f32[64,32]{1,0:T(8,128)S(1)} %pad_maximum_fusion) | data formatting | bytes 16384 | tf_op jit(solution)/shard_map/concatenate | solution.py:174
  (7 shorter events, 0.1 us)
Async XLA Ops:
  0.0 2.4 %copy-start.1 = (bf16[32,768]{1,0:T(8,128)(2,1)S(1)}, bf16[32,768]{1,0:T(8,128)(2,1)}, u32[]{:S(2)}) copy-start(bf16[32,768]{1,0:T(8,128)(2,1)} %param.5) | copy-start | bytes 147460
  34.4 2.5 %copy-start = (bf16[32,16,896]{2,1,0:T(8,128)(2,1)}, bf16[32,16,896]{2,1,0:T(8,128)(2,1)S(1)}, u32[]{:S(2)}) copy-start(bf16[32,16,896]{2,1,0:T(8,128)(2,1)S(1)} %all_to_all.5) | copy-start | bytes 2752516
  34.4 2.5 %collective-permute-start = (bf16[32,16,896]{2,1,0:T(8,128)(2,1)S(1)}, bf16[32,16,896]{2,1,0:T(8,128)(2,1)S(1)}, u32[]{:S(2)}, u32[]{:S(2)}) collective-permute-start(bf16[32,16,896]{2,1,0:T(8,128)(2,1)S(1)} %all_to_all.5), channel_id=1, source_target_pairs={{0,8},{8,0},{16,24},{24,16},{1,9},{9,1},{17,25},{25,17},{2,10},{10... | collective-permute-start | bytes 2752520 | tf_op jit(solution)/shard_map/ppermute | solution.py:154
  34.5 0.7 %copy-start.2 = (s32[8]{0:T(128)S(1)}, s32[8]{0:T(128)}, u32[]{:S(2)}) copy-start(s32[8]{0:T(128)} %param.8) | copy-start | bytes 100
  36.9 0.9 %copy-start.3 = (bf16[32,16,896]{2,1,0:T(8,128)(2,1)}, bf16[32,16,896]{2,1,0:T(8,128)(2,1)S(1)}, u32[]{:S(2)}) copy-start(bf16[32,16,896]{2,1,0:T(8,128)(2,1)S(1)} %collective-permute-done) | copy-start | bytes 2752516

commit v11 on v10

--- a/solution.py
+++ b/solution.py
@@ -135,15 +135,15 @@
     mask_part = jnp.tile(mask_part.reshape(half_s, mask_cols), (2, 1))
     used = PROBE_PARTS * n_probe + 1 + mask_cols
     lanes = -(-used // 128) * 128
-    payload = jnp.concatenate(
-        [
-            embed,
-            jnp.moveaxis(split3(probes.T)[:PROBE_PARTS], 0, 1).reshape(shard, PROBE_PARTS * n_probe),
-            beta[:, None],
-            mask_part,
-            jnp.zeros((shard, lanes - used), jnp.bfloat16),
-        ],
-        axis=1,
+    width = feat + lanes
+    pieces = [
+        (embed, 0),
+        (split3(probes.T)[:PROBE_PARTS].transpose(1, 0, 2).reshape(shard, PROBE_PARTS * n_probe), feat),
+        (beta[:, None], feat + PROBE_PARTS * n_probe),
+        (mask_part, feat + PROBE_PARTS * n_probe + 1),
+    ]
+    payload = sum(
+        jnp.pad(piece, ((0, 0), (start, width - start - piece.shape[1]))) for piece, start in pieces
     )
     width = payload.shape[1]
     halves = payload.reshape(2, half_s, width)

time: 49 us -> 49 us (level)
    concatenate x2 -> x0, local copies, waits for them, and re-layouts: 0.86 us -> none  [dense_path(): jnp.concatenate([embed, jnp.moveaxis(split3(probes.T)[:PROBE_PARTS], 0, 1...]
    broadcast_in_dim x1, local copies, waits for them, and re-layouts: 0.01 us -> 0.76 us  [dense_path(): beta[:, None]]
where the time goes in v11:
time: 49 us; the launch traced here: 48.6 us
  blocking collectives  31.9 us (65%)
  Pallas kernels  9.2 us (19%)
  local copies, waits for them, and re-layouts  4.93 us (10%)
  other arithmetic  2.22 us (5%)
    all_to_all x1, blocking collectives, dense_path(): mine = lax.all_to_all(wide, AXES, 0, 0, tiled=True)  31.9 us
    pallas_call x1, Pallas kernels, dense_call(): pl.pallas_call(lambda *refs: dense_kernel(ITERS, tile, beta_lane, PROBE_P...  9.2 us
    unnamed x8, local copies, waits for them, and re-layouts  1.56 us
  transfers between devices with their start and end apart: 1, of which 1 were waited for; matrix products, arithmetic and copies ran while one was open for 3% of the time, Pallas kernels for 0%

profile of v11, /device:TPU:0, one launch (start us, length us, event | category | flops | bytes accessed | tf_op | source)
XLA Modules:
  0.0 48.6 jit_solution(15672021861311042560)
XLA Ops:
  0.0 0.0 copy-start.1
  0.0 0.7 %convert_element_type.19 = bf16[2,8]{1,0:T(2,128)(2,1)S(1)} convert(s32[2,8]{1,0:T(2,128)} %param.7) | non-fusion elementwise | flops 16 | bytes 96 | tf_op jit(solution)/shard_map/convert_element_type | solution.py:132
  0.7 0.1 convert_element_type.20
  0.8 0.1 tile.10
  0.9 0.8 %copy.24 = bf16[32,1]{1,0:T(8,128)(2,1)S(1)} copy(bf16[32,1]{0,1:T(2,128)(2,1)} %bitcast.14) | data formatting | bytes 128 | tf_op jit(solution)/shard_map/broadcast_in_dim | solution.py:142
  1.6 0.7 %fusion = bf16[32,64]{1,0:T(8,128)(2,1)S(1)} fusion(f32[64,32]{0,1:T(8,128)} %param.9), kind=kLoop, calls=%fused_computation.5 | loop fusion | flops 4096 | bytes 12288 | tf_op jit(solution)/shard_map/reshape;transpose | solution.py:141
  2.4 0.0 copy-done.1
  2.4 0.1 pad_add_fusion
  2.4 0.1 broadcast_in_dim.39
  2.5 31.9 %all_to_all.5 = bf16[32,16,896]{2,1,0:T(8,128)(2,1)S(1)} all-to-all(bf16[32,16,896]{2,1,0:T(8,128)(2,1)S(1)} %bitcast.11), channel_id=1, replica_groups=mesh['row'=4,'col'=8] {'row','col'}, dimensions={0} | all-to-all | bytes 1835008 | tf_op jit(solution)/shard_map/all_to_all | solution.py:153
  34.4 0.0 copy-start
  34.4 0.0 collective-permute-start
  34.4 0.1 broadcast_in_dim.41
  34.5 0.0 copy-start.2
  34.5 0.1 mul.38
  34.6 0.6 %copy-done.2 = s32[8]{0:T(128)S(1)} copy-done((s32[8]{0:T(128)S(1)}, s32[8]{0:T(128)}, u32[]{:S(2)}) %copy-start.2) | copy-done | bytes 56
  35.2 0.1 broadcast_in_dim.42
  35.2 0.1 reshape.142
  35.3 0.2 slice_reduce_fusion
  35.6 0.1 reshape.143
  35.7 0.1 broadcast_in_dim.40
  35.8 0.1 reshape.141
  35.9 0.6 %and_select_fusion.refs_2_ = f32[1,8,1024]{2,1,0:T(8,128)} fusion(pred[1,8,1024]{2,1,0:T(8,128)(4,1)S(1)} %reshape.141, pred[1024]{0:T(1024)(128)(4,1)S(1)} %fusion.5), kind=kLoop, calls=%fused_computation.3 | loop fusion | flops 16384 | bytes 41984 | tf_op jit(solution)/shard_map/jit(_where)/select_n | solution.py:170
  36.5 0.4 collective-permute-done
  36.9 0.0 copy-start.3
  36.9 0.0 copy-done
  36.9 0.9 %copy-done.3 = bf16[32,16,896]{2,1,0:T(8,128)(2,1)} copy-done((bf16[32,16,896]{2,1,0:T(8,128)(2,1)}, bf16[32,16,896]{2,1,0:T(8,128)(2,1)S(1)}, u32[]{:S(2)}) %copy-start.3) | copy-done | bytes 917528
  37.8 9.2 %shard_map.55 = f32[64,1024]{1,0:T(8,128)} custom-call(bf16[512,896]{1,0:T(8,128)(2,1)} %bitcast.12, bf16[512,896]{1,0:T(8,128)(2,1)} %bitcast.15, f32[1,8,1024]{2,1,0:T(8,128)} %and_select_fusion.refs_2_), custom_call_target="tpu_custom_call" | custom-call | flops 2147483648 | bytes 2097152 | tf_op jit(solution)/shard_map/pallas_call | solution.py:103
  47.0 0.8 %constant_dynamic-slice_fusion.1 = (f32[64,16]{1,0:T(8,128)S(1)}, f32[64,16]{1,0:T(8,128)S(1)}) fusion(f32[64,1024]{1,0:T(8,128)} %shard_map.55, s32[]{:T(128)S(6)} %select_n.67, s32[]{:T(128)S(6)} %select_n.68), kind=kLoop, calls=%fused_computation.30 | loop fusion | bytes 16392 | tf_op jit(solution)/shard_map/dynamic_slice | solution.py:172
  47.9 0.1 pad_maximum_fusion
  48.0 0.7 %copy.29 = f32[64,32]{0,1:T(8,128)} copy(f32[64,32]{1,0:T(8,128)S(1)} %pad_maximum_fusion) | data formatting | bytes 16384 | tf_op jit(solution)/shard_map/concatenate | solution.py:174
  (7 shorter events, 0.1 us)
Async XLA Ops:
  0.0 2.4 %copy-start.1 = (bf16[32,768]{1,0:T(8,128)(2,1)S(1)}, bf16[32,768]{1,0:T(8,128)(2,1)}, u32[]{:S(2)}) copy-start(bf16[32,768]{1,0:T(8,128)(2,1)} %param.5) | copy-start | bytes 147460
  34.4 2.5 %copy-start = (bf16[32,16,896]{2,1,0:T(8,128)(2,1)}, bf16[32,16,896]{2,1,0:T(8,128)(2,1)S(1)}, u32[]{:S(2)}) copy-start(bf16[32,16,896]{2,1,0:T(8,128)(2,1)S(1)} %all_to_all.5) | copy-start | bytes 2752516
  34.4 2.5 %collective-permute-start = (bf16[32,16,896]{2,1,0:T(8,128)(2,1)S(1)}, bf16[32,16,896]{2,1,0:T(8,128)(2,1)S(1)}, u32[]{:S(2)}, u32[]{:S(2)}) collective-permute-start(bf16[32,16,896]{2,1,0:T(8,128)(2,1)S(1)} %all_to_all.5), channel_id=1, source_target_pairs={{0,8},{8,0},{16,24},{24,16},{1,9},{9,1},{17,25},{25,17},{2,10},{10... | collective-permute-start | bytes 2752520 | tf_op jit(solution)/shard_map/ppermute | solution.py:154
  34.5 0.7 %copy-start.2 = (s32[8]{0:T(128)S(1)}, s32[8]{0:T(128)}, u32[]{:S(2)}) copy-start(s32[8]{0:T(128)} %param.8) | copy-start | bytes 100
  36.9 0.9 %copy-start.3 = (bf16[32,16,896]{2,1,0:T(8,128)(2,1)}, bf16[32,16,896]{2,1,0:T(8,128)(2,1)S(1)}, u32[]{:S(2)}) copy-start(bf16[32,16,896]{2,1,0:T(8,128)(2,1)S(1)} %collective-permute-done) | copy-start | bytes 2752516

commit v12 on v10

--- a/solution.py
+++ b/solution.py
@@ -72,7 +72,7 @@
 
     colsum = lax.fori_loop(0, files // tile, step, jnp.zeros((1, files), jnp.float32))
     inv_root = lax.rsqrt((1.0 + colsum) * 0.5)
-    n_probe = out_ref.shape[0]
+    n_probe = out_ref.shape[1]
     state = jnp.concatenate(
         [
             sum(
@@ -88,8 +88,10 @@
         scaled = scaled_f.astype(jnp.bfloat16)
         row_t = jnp.dot(aff_s[...], scaled_f.T.astype(jnp.bfloat16), preferred_element_type=jnp.float32)
         col_part = jnp.dot(scaled, aff_s[...], preferred_element_type=jnp.float32)
-        state = (row_t.T + col_part) * (0.5 * inv_root)
-    out_ref[...] = state
+        if sweep + 1 < n_iter:
+            state = (row_t.T + col_part) * (0.5 * inv_root)
+        else:
+            out_ref[...] = (row_t + col_part.T) * (0.5 * inv_root).T
 
 
 def dense_call(mine, other, rowmask, n_probe, feat, beta_lane):
@@ -102,7 +104,7 @@
     vmem = pl.BlockSpec(memory_space=pltpu.VMEM)
     return pl.pallas_call(
         lambda *refs: dense_kernel(ITERS, tile, beta_lane, PROBE_PARTS, *refs),
-        out_shape=jax.ShapeDtypeStruct((n_probe, files), jnp.float32),
+        out_shape=jax.ShapeDtypeStruct((files, n_probe), jnp.float32),
         in_specs=[vmem, vmem, vmem],
         out_specs=vmem,
         scratch_shapes=[
@@ -135,15 +137,16 @@
     mask_part = jnp.tile(mask_part.reshape(half_s, mask_cols), (2, 1))
     used = PROBE_PARTS * n_probe + 1 + mask_cols
     lanes = -(-used // 128) * 128
+    extras = jnp.concatenate(
+        [
+            split3(probes)[:PROBE_PARTS].astype(jnp.float32).reshape(PROBE_PARTS * n_probe, shard),
+            beta[None, :].astype(jnp.float32),
+            mask_part.T.astype(jnp.float32),
+        ],
+        axis=0,
+    )
     payload = jnp.concatenate(
-        [
-            embed,
-            jnp.moveaxis(split3(probes.T)[:PROBE_PARTS], 0, 1).reshape(shard, PROBE_PARTS * n_probe),
-            beta[:, None],
-            mask_part,
-            jnp.zeros((shard, lanes - used), jnp.bfloat16),
-        ],
-        axis=1,
+        [embed, jnp.pad(extras.T.astype(jnp.bfloat16), ((0, 0), (0, lanes - used)))], axis=1
     )
     width = payload.shape[1]
     halves = payload.reshape(2, half_s, width)
@@ -168,10 +171,10 @@
     mask_full = mask_got.reshape(n_row, per_row, local_blocks, nb)[:, 0].reshape(nb, nb)
     block_ok = jnp.broadcast_to((mask_full == 1)[:, None, :, None], (nb, 2, nb, run))
     rowmask = jnp.where(block_ok.reshape(nb, files) & live[None, :], 1.0, 0.0).astype(jnp.float32)
-    state = dense_call(mine2, other2, rowmask, n_probe, feat, feat + PROBE_PARTS * n_probe)
-    first = lax.dynamic_slice_in_dim(state, core * half_f + me * half_s, half_s, 1)
-    second = lax.dynamic_slice_in_dim(state, (1 - core) * half_f + me * half_s, half_s, 1)
-    return jnp.concatenate([first, second], axis=1)
+    state_t = dense_call(mine2, other2, rowmask, n_probe, feat, feat + PROBE_PARTS * n_probe)
+    first = lax.dynamic_slice_in_dim(state_t, core * half_f + me * half_s, half_s, 0)
+    second = lax.dynamic_slice_in_dim(state_t, (1 - core) * half_f + me * half_s, half_s, 0)
+    return jnp.concatenate([first, second], axis=0).T
 
 
 def normalize(embed):

time: 49 us -> 47.8 us (0.976)
  local copies, waits for them, and re-layouts: 5 us -> 4.12 us
    concatenate x3 -> x0, local copies, waits for them, and re-layouts: 1.55 us -> none  [the longest x2 0.86 us: dense_path(): jnp.concatenate([embed, jnp.moveaxis(split3(probes.T)[:PROBE_PARTS], 0, 1...]
    convert_element_type x1 -> x3, local copies, waits for them, and re-layouts: 0.09 us -> 0.94 us  [the longest x1 0.76 us: dense_path(): beta[None, :].astype(jnp.float32)]
    another operation x1 -> x0, other arithmetic: 0.73 us -> none
    transpose x0 -> x1, other arithmetic: none -> 0.61 us  [dense_path(): return jnp.concatenate([first, second], axis=0).T]
    unnamed x8 -> x10, local copies, waits for them, and re-layouts: 1.56 us -> 1.58 us
where the time goes in v12:
time: 47.8 us; the launch traced here: 47.6 us
  blocking collectives  31.9 us (67%)
  Pallas kernels  9.09 us (19%)
  local copies, waits for them, and re-layouts  4.12 us (9%)
  other arithmetic  2.06 us (4%)
    all_to_all x1, blocking collectives, dense_path(): mine = lax.all_to_all(wide, AXES, 0, 0, tiled=True)  31.9 us
    pallas_call x1, Pallas kernels, dense_call(): pl.pallas_call(lambda *refs: dense_kernel(ITERS, tile, beta_lane, PROBE_P...  9.09 us
    unnamed x10, local copies, waits for them, and re-layouts  1.58 us
  transfers between devices with their start and end apart: 1, of which 1 were waited for; matrix products, arithmetic and copies ran while one was open for 3% of the time, Pallas kernels for 0%

profile of v12, /device:TPU:0, one launch (start us, length us, event | category | flops | bytes accessed | tf_op | source)
XLA Modules:
  0.0 47.6 jit_solution(1791072220103706373)
XLA Ops:
  0.0 0.0 copy-start.2
  0.0 0.0 copy-start.1
  0.0 0.7 %convert_element_type.37 = bf16[2,8]{1,0:T(2,128)(2,1)S(1)} convert(s32[2,8]{1,0:T(2,128)} %param.7) | non-fusion elementwise | flops 16 | bytes 96 | tf_op jit(solution)/shard_map/convert_element_type | solution.py:134
  0.7 0.1 convert_element_type.38
  0.8 0.1 convert_element_type.41
  0.9 0.8 %copy.18 = bf16[1,32]{0,1:T(8,128)(2,1)S(1)} copy(bf16[1,32]{1,0:T(2,128)(2,1)} %bitcast.16) | data formatting | bytes 128 | tf_op jit(solution)/shard_map/convert_element_type | solution.py:143
  1.6 0.0 copy-done.2
  1.7 0.1 maximum_bitcast_fusion.1
  1.7 0.0 copy-done.1
  1.8 0.1 broadcast_in_dim.17
  1.8 31.9 %all_to_all.5 = bf16[32,16,896]{2,1,0:T(8,128)(2,1)S(1)} all-to-all(bf16[32,16,896]{2,1,0:T(8,128)(2,1)S(1)} %bitcast.13), channel_id=1, replica_groups=mesh['row'=4,'col'=8] {'row','col'}, dimensions={0} | all-to-all | bytes 1835008 | tf_op jit(solution)/shard_map/all_to_all | solution.py:156
  33.7 0.0 copy-start
  33.7 0.0 collective-permute-start
  33.7 0.1 broadcast_in_dim.38
  33.8 0.0 copy-start.3
  33.8 0.1 mul.38
  33.9 0.6 %copy-done.3 = s32[8]{0:T(128)S(1)} copy-done((s32[8]{0:T(128)S(1)}, s32[8]{0:T(128)}, u32[]{:S(2)}) %copy-start.3) | copy-done | bytes 56
  34.5 0.1 broadcast_in_dim.39
  34.5 0.1 reshape.165
  34.6 0.2 slice_reduce_fusion
  34.9 0.1 reshape.166
  35.0 0.1 broadcast_in_dim.18
  35.1 0.1 reshape.164
  35.2 0.6 %and_select_fusion.refs_2_ = f32[1,8,1024]{2,1,0:T(8,128)} fusion(pred[1,8,1024]{2,1,0:T(8,128)(4,1)S(1)} %reshape.164, pred[1024]{0:T(1024)(128)(4,1)S(1)} %fusion.6), kind=kLoop, calls=%fused_computation.4 | loop fusion | flops 16384 | bytes 41984 | tf_op jit(solution)/shard_map/jit(_where)/select_n | solution.py:173
  35.8 0.4 collective-permute-done
  36.2 0.0 copy-start.4
  36.2 0.0 copy-done
  36.2 1.0 %copy-done.4 = bf16[32,16,896]{2,1,0:T(8,128)(2,1)} copy-done((bf16[32,16,896]{2,1,0:T(8,128)(2,1)}, bf16[32,16,896]{2,1,0:T(8,128)(2,1)S(1)}, u32[]{:S(2)}) %copy-start.4) | copy-done | bytes 917528
  37.1 9.1 %shard_map.55 = f32[1024,64]{1,0:T(8,128)} custom-call(bf16[512,896]{1,0:T(8,128)(2,1)} %bitcast.14, bf16[512,896]{1,0:T(8,128)(2,1)} %bitcast.17, f32[1,8,1024]{2,1,0:T(8,128)} %and_select_fusion.refs_2_), custom_call_target="tpu_custom_call" | custom-call | flops 2147483648 | bytes 2097152 | tf_op jit(solution)/shard_map/pallas_call | solution.py:105
  46.2 0.7 %constant_dynamic-slice_fusion.1 = (f32[16,64]{1,0:T(8,128)S(1)}, f32[16,64]{1,0:T(8,128)S(1)}) fusion(f32[1024,64]{1,0:T(8,128)} %shard_map.55, s32[]{:T(128)S(6)} %select_n.67, s32[]{:T(128)S(6)} %select_n.68), kind=kLoop, calls=%fused_computation.32 | loop fusion | bytes 16392 | tf_op jit(solution)/shard_map/dynamic_slice | solution.py:175
  46.9 0.6 %maximum_bitcast_fusion = f32[64,32]{0,1:T(8,128)} fusion(f32[16,64]{1,0:T(8,128)S(1)} %get-tuple-element.6, f32[16,64]{1,0:T(8,128)S(1)} %get-tuple-element.5), kind=kLoop, calls=%fused_computation.5 | loop fusion | flops 2048 | bytes 16384 | tf_op jit(solution)/shard_map/transpose | solution.py:177
  (9 shorter events, 0.1 us)
Async XLA Ops:
  0.0 1.6 %copy-start.2 = (f32[64,32]{0,1:T(8,128)S(1)}, f32[64,32]{0,1:T(8,128)}, u32[]{:S(2)}) copy-start(f32[64,32]{0,1:T(8,128)} %param.9) | copy-start | bytes 24580
  0.0 1.7 %copy-start.1 = (bf16[32,768]{1,0:T(8,128)(2,1)S(1)}, bf16[32,768]{1,0:T(8,128)(2,1)}, u32[]{:S(2)}) copy-start(bf16[32,768]{1,0:T(8,128)(2,1)} %param.5) | copy-start | bytes 147460
  33.7 2.5 %copy-start = (bf16[32,16,896]{2,1,0:T(8,128)(2,1)}, bf16[32,16,896]{2,1,0:T(8,128)(2,1)S(1)}, u32[]{:S(2)}) copy-start(bf16[32,16,896]{2,1,0:T(8,128)(2,1)S(1)} %all_to_all.5) | copy-start | bytes 2752516
  33.7 2.5 %collective-permute-start = (bf16[32,16,896]{2,1,0:T(8,128)(2,1)S(1)}, bf16[32,16,896]{2,1,0:T(8,128)(2,1)S(1)}, u32[]{:S(2)}, u32[]{:S(2)}) collective-permute-start(bf16[32,16,896]{2,1,0:T(8,128)(2,1)S(1)} %all_to_all.5), channel_id=1, source_target_pairs={{0,8},{8,0},{16,24},{24,16},{1,9},{9,1},{17,25},{25,17},{2,10},{10... | collective-permute-start | bytes 2752520 | tf_op jit(solution)/shard_map/ppermute | solution.py:157
  33.8 0.7 %copy-start.3 = (s32[8]{0:T(128)S(1)}, s32[8]{0:T(128)}, u32[]{:S(2)}) copy-start(s32[8]{0:T(128)} %param.8) | copy-start | bytes 100
  36.2 1.0 %copy-start.4 = (bf16[32,16,896]{2,1,0:T(8,128)(2,1)}, bf16[32,16,896]{2,1,0:T(8,128)(2,1)S(1)}, u32[]{:S(2)}) copy-start(bf16[32,16,896]{2,1,0:T(8,128)(2,1)S(1)} %collective-permute-done) | copy-start | bytes 2752516

commit v13 on v12

--- a/solution.py
+++ b/solution.py
@@ -36,11 +36,15 @@
     return jnp.concatenate([low, high], axis=1)[:, : x.shape[0]]
 
 
-def dense_kernel(n_iter, tile, beta_lane, n_parts, mine_ref, other_ref, rowmask_ref, out_ref, unit_t, unit_s, scale_s, aff_s):
+def dense_kernel(n_iter, tile, beta_lane, n_parts, mine_ref, other_hbm, rowmask_ref, out_ref, unit_t, unit_s, scale_s, aff_s, other_ref, copy_sem):
     feat, files = unit_t.shape
     half = files // 2
     runs = half // tile
+    fetch = pltpu.make_async_copy(other_hbm, other_ref, copy_sem)
+    fetch.start()
     for k, ref in enumerate((mine_ref, other_ref)):
+        if k == 1:
+            fetch.wait()
         values = ref[:, 0:feat].astype(jnp.float32)
         unit = (
             values * lax.rsqrt(jnp.mean(values * values, axis=1, keepdims=True) + 1e-06)
@@ -105,13 +109,15 @@
     return pl.pallas_call(
         lambda *refs: dense_kernel(ITERS, tile, beta_lane, PROBE_PARTS, *refs),
         out_shape=jax.ShapeDtypeStruct((files, n_probe), jnp.float32),
-        in_specs=[vmem, vmem, vmem],
+        in_specs=[vmem, pl.BlockSpec(memory_space=pl.ANY), vmem],
         out_specs=vmem,
         scratch_shapes=[
             pltpu.VMEM((feat, files), jnp.bfloat16),
             pltpu.VMEM((files, feat), jnp.bfloat16),
             pltpu.VMEM((files, 1), jnp.float32),
             pltpu.VMEM((files, files), jnp.bfloat16),
+            pltpu.VMEM(other.shape, other.dtype),
+            pltpu.SemaphoreType.DMA(()),
         ],
         cost_estimate=pl.CostEstimate(
             flops=2 * files * files * feat + 4 * ITERS * files * files * n_probe,

time: 47.8 us -> 48.4 us (1.013)
  no operation moved by 1% of the time
where the time goes in v13:
time: 48.4 us; the launch traced here: 48 us
  blocking collectives  31.9 us (66%)
  Pallas kernels  9.56 us (20%)
  local copies, waits for them, and re-layouts  4.13 us (9%)
  other arithmetic  2.06 us (4%)
    all_to_all x1, blocking collectives, dense_path(): mine = lax.all_to_all(wide, AXES, 0, 0, tiled=True)  31.9 us
    pallas_call x1, Pallas kernels, dense_call(): pl.pallas_call(lambda *refs: dense_kernel(ITERS, tile, beta_lane, PROBE_P...  9.56 us
    unnamed x10, local copies, waits for them, and re-layouts  1.58 us
  transfers between devices with their start and end apart: 1, of which 1 were waited for; matrix products, arithmetic and copies ran while one was open for 3% of the time, Pallas kernels for 0%

profile of v13, /device:TPU:0, one launch (start us, length us, event | category | flops | bytes accessed | tf_op | source)
XLA Modules:
  0.0 48.0 jit_solution(5281617256550933772)
XLA Ops:
  0.0 0.0 copy-start.2
  0.0 0.0 copy-start.1
  0.0 0.7 %convert_element_type.37 = bf16[2,8]{1,0:T(2,128)(2,1)S(1)} convert(s32[2,8]{1,0:T(2,128)} %param.7) | non-fusion elementwise | flops 16 | bytes 96 | tf_op jit(solution)/shard_map/convert_element_type | solution.py:140
  0.7 0.1 convert_element_type.38
  0.8 0.1 convert_element_type.41
  0.9 0.8 %copy.18 = bf16[1,32]{0,1:T(8,128)(2,1)S(1)} copy(bf16[1,32]{1,0:T(2,128)(2,1)} %bitcast.16) | data formatting | bytes 128 | tf_op jit(solution)/shard_map/convert_element_type | solution.py:149
  1.6 0.0 copy-done.2
  1.7 0.1 maximum_bitcast_fusion.1
  1.7 0.0 copy-done.1
  1.8 0.1 broadcast_in_dim.17
  1.8 31.9 %all_to_all.5 = bf16[32,16,896]{2,1,0:T(8,128)(2,1)S(1)} all-to-all(bf16[32,16,896]{2,1,0:T(8,128)(2,1)S(1)} %bitcast.13), channel_id=1, replica_groups=mesh['row'=4,'col'=8] {'row','col'}, dimensions={0} | all-to-all | bytes 1835008 | tf_op jit(solution)/shard_map/all_to_all | solution.py:162
  33.7 0.0 copy-start
  33.7 0.0 collective-permute-start
  33.7 0.1 broadcast_in_dim.38
  33.8 0.0 copy-start.3
  33.8 0.1 mul.38
  33.9 0.6 %copy-done.3 = s32[8]{0:T(128)S(1)} copy-done((s32[8]{0:T(128)S(1)}, s32[8]{0:T(128)}, u32[]{:S(2)}) %copy-start.3) | copy-done | bytes 56
  34.5 0.1 broadcast_in_dim.39
  34.5 0.1 reshape.165
  34.6 0.2 slice_reduce_fusion
  34.9 0.1 reshape.166
  35.0 0.1 broadcast_in_dim.18
  35.1 0.1 reshape.164
  35.2 0.6 %and_select_fusion.refs_2_ = f32[1,8,1024]{2,1,0:T(8,128)} fusion(pred[1,8,1024]{2,1,0:T(8,128)(4,1)S(1)} %reshape.164, pred[1024]{0:T(1024)(128)(4,1)S(1)} %fusion.6), kind=kLoop, calls=%fused_computation.4 | loop fusion | flops 16384 | bytes 41984 | tf_op jit(solution)/shard_map/jit(_where)/select_n | solution.py:179
  35.8 0.4 collective-permute-done
  36.2 0.0 copy-start.4
  36.2 0.0 copy-done
  36.2 1.0 %copy-done.4 = bf16[32,16,896]{2,1,0:T(8,128)(2,1)} copy-done((bf16[32,16,896]{2,1,0:T(8,128)(2,1)}, bf16[32,16,896]{2,1,0:T(8,128)(2,1)S(1)}, u32[]{:S(2)}) %copy-start.4) | copy-done | bytes 917528
  37.1 9.6 %shard_map.55 = f32[1024,64]{1,0:T(8,128)} custom-call(bf16[512,896]{1,0:T(8,128)(2,1)} %bitcast.14, bf16[512,896]{1,0:T(8,128)(2,1)} %bitcast.17, f32[1,8,1024]{2,1,0:T(8,128)} %and_select_fusion.refs_2_), custom_call_target="tpu_custom_call" | custom-call | flops 2147483648 | bytes 2097152 | tf_op jit(solution)/shard_map/pallas_call | solution.py:109
  46.7 0.7 %constant_dynamic-slice_fusion.1 = (f32[16,64]{1,0:T(8,128)S(1)}, f32[16,64]{1,0:T(8,128)S(1)}) fusion(f32[1024,64]{1,0:T(8,128)} %shard_map.55, s32[]{:T(128)S(6)} %select_n.67, s32[]{:T(128)S(6)} %select_n.68), kind=kLoop, calls=%fused_computation.32 | loop fusion | bytes 16392 | tf_op jit(solution)/shard_map/dynamic_slice | solution.py:181
  47.4 0.6 %maximum_bitcast_fusion = f32[64,32]{0,1:T(8,128)} fusion(f32[16,64]{1,0:T(8,128)S(1)} %get-tuple-element.6, f32[16,64]{1,0:T(8,128)S(1)} %get-tuple-element.5), kind=kLoop, calls=%fused_computation.5 | loop fusion | flops 2048 | bytes 16384 | tf_op jit(solution)/shard_map/transpose | solution.py:183
  (9 shorter events, 0.1 us)
Async XLA Ops:
  0.0 1.6 %copy-start.2 = (f32[64,32]{0,1:T(8,128)S(1)}, f32[64,32]{0,1:T(8,128)}, u32[]{:S(2)}) copy-start(f32[64,32]{0,1:T(8,128)} %param.9) | copy-start | bytes 24580
  0.0 1.7 %copy-start.1 = (bf16[32,768]{1,0:T(8,128)(2,1)S(1)}, bf16[32,768]{1,0:T(8,128)(2,1)}, u32[]{:S(2)}) copy-start(bf16[32,768]{1,0:T(8,128)(2,1)} %param.5) | copy-start | bytes 147460
  33.7 2.5 %copy-start = (bf16[32,16,896]{2,1,0:T(8,128)(2,1)}, bf16[32,16,896]{2,1,0:T(8,128)(2,1)S(1)}, u32[]{:S(2)}) copy-start(bf16[32,16,896]{2,1,0:T(8,128)(2,1)S(1)} %all_to_all.5) | copy-start | bytes 2752516
  33.7 2.5 %collective-permute-start = (bf16[32,16,896]{2,1,0:T(8,128)(2,1)S(1)}, bf16[32,16,896]{2,1,0:T(8,128)(2,1)S(1)}, u32[]{:S(2)}, u32[]{:S(2)}) collective-permute-start(bf16[32,16,896]{2,1,0:T(8,128)(2,1)S(1)} %all_to_all.5), channel_id=1, source_target_pairs={{0,8},{8,0},{16,24},{24,16},{1,9},{9,1},{17,25},{25,17},{2,10},{10... | collective-permute-start | bytes 2752520 | tf_op jit(solution)/shard_map/ppermute | solution.py:163
  33.8 0.7 %copy-start.3 = (s32[8]{0:T(128)S(1)}, s32[8]{0:T(128)}, u32[]{:S(2)}) copy-start(s32[8]{0:T(128)} %param.8) | copy-start | bytes 100
  36.2 1.0 %copy-start.4 = (bf16[32,16,896]{2,1,0:T(8,128)(2,1)}, bf16[32,16,896]{2,1,0:T(8,128)(2,1)S(1)}, u32[]{:S(2)}) copy-start(bf16[32,16,896]{2,1,0:T(8,128)(2,1)S(1)} %collective-permute-done) | copy-start | bytes 2752516

commit v14 on v12

--- a/solution.py
+++ b/solution.py
@@ -36,7 +36,7 @@
     return jnp.concatenate([low, high], axis=1)[:, : x.shape[0]]
 
 
-def dense_kernel(n_iter, tile, beta_lane, n_parts, mine_ref, other_ref, rowmask_ref, out_ref, unit_t, unit_s, scale_s, aff_s):
+def dense_kernel(n_iter, tile, beta_lane, n_parts, mine_ref, other_ref, rowmask_ref, out_ref, unit_t, unit_s, scale_s, aff_s, state_s):
     feat, files = unit_t.shape
     half = files // 2
     runs = half // tile
@@ -91,10 +91,17 @@
         if sweep + 1 < n_iter:
             state = (row_t.T + col_part) * (0.5 * inv_root)
         else:
-            out_ref[...] = (row_t + col_part.T) * (0.5 * inv_root).T
-
-
-def dense_call(mine, other, rowmask, n_probe, feat, beta_lane):
+            state_s[...] = (row_t + col_part.T) * (0.5 * inv_root).T
+    shard = out_ref.shape[0]
+    half_s = shard // 2
+    core = lax.axis_index("row") % 2
+    me = lax.axis_index("row") * lax.axis_size("col") + lax.axis_index("col")
+    for k, h in enumerate((core, 1 - core)):
+        start = pl.multiple_of(h * half + me * half_s, half_s)
+        out_ref[k * half_s : (k + 1) * half_s, :] = state_s[pl.ds(start, half_s), :]
+
+
+def dense_call(mine, other, rowmask, n_probe, shard, feat, beta_lane):
     files = 2 * mine.shape[0]
     run = files // (2 * rowmask.shape[0])
     tile = run
@@ -104,7 +111,7 @@
     vmem = pl.BlockSpec(memory_space=pltpu.VMEM)
     return pl.pallas_call(
         lambda *refs: dense_kernel(ITERS, tile, beta_lane, PROBE_PARTS, *refs),
-        out_shape=jax.ShapeDtypeStruct((files, n_probe), jnp.float32),
+        out_shape=jax.ShapeDtypeStruct((shard, n_probe), jnp.float32),
         in_specs=[vmem, vmem, vmem],
         out_specs=vmem,
         scratch_shapes=[
@@ -112,6 +119,7 @@
             pltpu.VMEM((files, feat), jnp.bfloat16),
             pltpu.VMEM((files, 1), jnp.float32),
             pltpu.VMEM((files, files), jnp.bfloat16),
+            pltpu.VMEM((files, n_probe), jnp.float32),
         ],
         cost_estimate=pl.CostEstimate(
             flops=2 * files * files * feat + 4 * ITERS * files * files * n_probe,
@@ -171,10 +179,8 @@
     mask_full = mask_got.reshape(n_row, per_row, local_blocks, nb)[:, 0].reshape(nb, nb)
     block_ok = jnp.broadcast_to((mask_full == 1)[:, None, :, None], (nb, 2, nb, run))
     rowmask = jnp.where(block_ok.reshape(nb, files) & live[None, :], 1.0, 0.0).astype(jnp.float32)
-    state_t = dense_call(mine2, other2, rowmask, n_probe, feat, feat + PROBE_PARTS * n_probe)
-    first = lax.dynamic_slice_in_dim(state_t, core * half_f + me * half_s, half_s, 0)
-    second = lax.dynamic_slice_in_dim(state_t, (1 - core) * half_f + me * half_s, half_s, 0)
-    return jnp.concatenate([first, second], axis=0).T
+    own_t = dense_call(mine2, other2, rowmask, n_probe, shard, feat, feat + PROBE_PARTS * n_probe)
+    return own_t.T
 
 
 def normalize(embed):

time: 47.8 us -> 46.2 us (0.967)
  local copies, waits for them, and re-layouts: 4.12 us -> 3.39 us
  other arithmetic: 2.06 us -> 1.44 us
    dynamic_slice x1 -> x0, local copies, waits for them, and re-layouts: 0.72 us -> none  [dense_path(): lax.dynamic_slice_in_dim(state_t, core * half_f + me * half_s, half_s, 0)]
    transpose x1 -> x0, other arithmetic: 0.61 us -> none  [dense_path(): return jnp.concatenate([first, second], axis=0).T]
where the time goes in v14:
time: 46.2 us; the launch traced here: 46 us
  blocking collectives  31.9 us (69%)
  Pallas kernels  8.86 us (19%)
  local copies, waits for them, and re-layouts  3.39 us (7%)
  other arithmetic  1.44 us (3%)
    all_to_all x1, blocking collectives, dense_path(): mine = lax.all_to_all(wide, AXES, 0, 0, tiled=True)  31.9 us
    pallas_call x1, Pallas kernels, dense_call(): pl.pallas_call(lambda *refs: dense_kernel(ITERS, tile, beta_lane, PROBE_P...  8.86 us
    unnamed x10, local copies, waits for them, and re-layouts  1.57 us
  transfers between devices with their start and end apart: 1, of which 1 were waited for; matrix products, arithmetic and copies ran while one was open for 3% of the time, Pallas kernels for 0%

profile of v14, /device:TPU:0, one launch (start us, length us, event | category | flops | bytes accessed | tf_op | source)
XLA Modules:
  0.0 46.0 jit_solution(14393279269591886422)
XLA Ops:
  0.0 0.0 copy-start.2
  0.0 0.0 copy-start.1
  0.0 0.7 %convert_element_type.37 = bf16[2,8]{1,0:T(2,128)(2,1)S(1)} convert(s32[2,8]{1,0:T(2,128)} %param.7) | non-fusion elementwise | flops 16 | bytes 96 | tf_op jit(solution)/shard_map/convert_element_type | solution.py:142
  0.7 0.1 convert_element_type.38
  0.8 0.1 convert_element_type.41
  0.9 0.8 %copy.18 = bf16[1,32]{0,1:T(8,128)(2,1)S(1)} copy(bf16[1,32]{1,0:T(2,128)(2,1)} %bitcast.15) | data formatting | bytes 128 | tf_op jit(solution)/shard_map/convert_element_type | solution.py:151
  1.6 0.0 copy-done.2
  1.7 0.1 maximum_bitcast_fusion
  1.7 0.0 copy-done.1
  1.8 0.1 broadcast_in_dim.17
  1.8 31.9 %all_to_all.5 = bf16[32,16,896]{2,1,0:T(8,128)(2,1)S(1)} all-to-all(bf16[32,16,896]{2,1,0:T(8,128)(2,1)S(1)} %bitcast.12), channel_id=1, replica_groups=mesh['row'=4,'col'=8] {'row','col'}, dimensions={0} | all-to-all | bytes 1835008 | tf_op jit(solution)/shard_map/all_to_all | solution.py:164
  33.7 0.0 copy-start
  33.7 0.0 collective-permute-start
  33.7 0.1 broadcast_in_dim.38
  33.8 0.0 copy-start.3
  33.8 0.1 mul.25
  33.9 0.6 %copy-done.3 = s32[8]{0:T(128)S(1)} copy-done((s32[8]{0:T(128)S(1)}, s32[8]{0:T(128)}, u32[]{:S(2)}) %copy-start.3) | copy-done | bytes 56
  34.5 0.1 broadcast_in_dim.39
  34.5 0.1 reshape.165
  34.6 0.2 slice_reduce_fusion
  34.9 0.1 reshape.166
  35.0 0.1 broadcast_in_dim.18
  35.1 0.1 reshape.164
  35.2 0.6 %and_select_fusion.refs_2_ = f32[1,8,1024]{2,1,0:T(8,128)} fusion(pred[1,8,1024]{2,1,0:T(8,128)(4,1)S(1)} %reshape.164, pred[1024]{0:T(1024)(128)(4,1)S(1)} %fusion.6), kind=kLoop, calls=%fused_computation.4 | loop fusion | flops 16384 | bytes 41984 | tf_op jit(solution)/shard_map/jit(_where)/select_n | solution.py:181
  35.8 0.4 collective-permute-done
  36.2 0.0 copy-start.4
  36.2 0.0 copy-done
  36.2 0.9 %copy-done.4 = bf16[32,16,896]{2,1,0:T(8,128)(2,1)} copy-done((bf16[32,16,896]{2,1,0:T(8,128)(2,1)}, bf16[32,16,896]{2,1,0:T(8,128)(2,1)S(1)}, u32[]{:S(2)}) %copy-start.4) | copy-done | bytes 917528
  37.1 8.9 %shard_map.55 = f32[32,64]{1,0:T(8,128)} custom-call(bf16[512,896]{1,0:T(8,128)(2,1)} %bitcast.13, bf16[512,896]{1,0:T(8,128)(2,1)} %bitcast.16, f32[1,8,1024]{2,1,0:T(8,128)} %and_select_fusion.refs_2_), custom_call_target="tpu_custom_call" | custom-call | flops 2147483648 | bytes 2097152 | tf_op jit(solution)/shard_map/pallas_call | solution.py:112
  (9 shorter events, 0.1 us)
Async XLA Ops:
  0.0 1.6 %copy-start.2 = (f32[64,32]{0,1:T(8,128)S(1)}, f32[64,32]{0,1:T(8,128)}, u32[]{:S(2)}) copy-start(f32[64,32]{0,1:T(8,128)} %param.9) | copy-start | bytes 24580
  0.0 1.7 %copy-start.1 = (bf16[32,768]{1,0:T(8,128)(2,1)S(1)}, bf16[32,768]{1,0:T(8,128)(2,1)}, u32[]{:S(2)}) copy-start(bf16[32,768]{1,0:T(8,128)(2,1)} %param.5) | copy-start | bytes 147460
  33.7 2.5 %copy-start = (bf16[32,16,896]{2,1,0:T(8,128)(2,1)}, bf16[32,16,896]{2,1,0:T(8,128)(2,1)S(1)}, u32[]{:S(2)}) copy-start(bf16[32,16,896]{2,1,0:T(8,128)(2,1)S(1)} %all_to_all.5) | copy-start | bytes 2752516
  33.7 2.5 %collective-permute-start = (bf16[32,16,896]{2,1,0:T(8,128)(2,1)S(1)}, bf16[32,16,896]{2,1,0:T(8,128)(2,1)S(1)}, u32[]{:S(2)}, u32[]{:S(2)}) collective-permute-start(bf16[32,16,896]{2,1,0:T(8,128)(2,1)S(1)} %all_to_all.5), channel_id=1, source_target_pairs={{0,8},{8,0},{16,24},{24,16},{1,9},{9,1},{17,25},{25,17},{2,10},{10... | collective-permute-start | bytes 2752520 | tf_op jit(solution)/shard_map/ppermute | solution.py:165
  33.8 0.7 %copy-start.3 = (s32[8]{0:T(128)S(1)}, s32[8]{0:T(128)}, u32[]{:S(2)}) copy-start(s32[8]{0:T(128)} %param.8) | copy-start | bytes 100
  36.2 0.9 %copy-start.4 = (bf16[32,16,896]{2,1,0:T(8,128)(2,1)}, bf16[32,16,896]{2,1,0:T(8,128)(2,1)S(1)}, u32[]{:S(2)}) copy-start(bf16[32,16,896]{2,1,0:T(8,128)(2,1)S(1)} %collective-permute-done) | copy-start | bytes 2752516

commit v15 on v14

--- a/solution.py
+++ b/solution.py
@@ -139,7 +139,7 @@
     local_blocks = block_mask.shape[0]
     n_probe = probes.shape[0]
     per_row = n_dev // n_row
-    mask_flat = block_mask.reshape(-1).astype(jnp.bfloat16)
+    mask_flat = block_mask.reshape(-1).astype(jnp.float32)
     mask_cols = -(-mask_flat.shape[0] // half_s)
     mask_part = jnp.pad(mask_flat, (0, half_s * mask_cols - mask_flat.shape[0]))
     mask_part = jnp.tile(mask_part.reshape(half_s, mask_cols), (2, 1))
@@ -149,7 +149,7 @@
         [
             split3(probes)[:PROBE_PARTS].astype(jnp.float32).reshape(PROBE_PARTS * n_probe, shard),
             beta[None, :].astype(jnp.float32),
-            mask_part.T.astype(jnp.float32),
+            mask_part.T,
         ],
         axis=0,
     )

time: 46.2 us -> 46.2 us (level)
    another operation x0 -> x1, other arithmetic: none -> 0.7 us
    convert_element_type x1 -> x0, other arithmetic: 0.7 us -> none  [dense_path(): mask_flat = block_mask.reshape(-1).astype(jnp.bfloat16)]
where the time goes in v15:
time: 46.2 us; the launch traced here: 46 us
  blocking collectives  31.9 us (69%)
  Pallas kernels  8.86 us (19%)
  local copies, waits for them, and re-layouts  3.39 us (7%)
  other arithmetic  1.44 us (3%)
    all_to_all x1, blocking collectives, dense_path(): mine = lax.all_to_all(wide, AXES, 0, 0, tiled=True)  31.9 us
    pallas_call x1, Pallas kernels, dense_call(): pl.pallas_call(lambda *refs: dense_kernel(ITERS, tile, beta_lane, PROBE_P...  8.86 us
    unnamed x10, local copies, waits for them, and re-layouts  1.57 us
  transfers between devices with their start and end apart: 1, of which 1 were waited for; matrix products, arithmetic and copies ran while one was open for 3% of the time, Pallas kernels for 0%

profile of v15, /device:TPU:0, one launch (start us, length us, event | category | flops | bytes accessed | tf_op | source)
XLA Modules:
  0.0 46.0 jit_solution(14393279269591886422)
XLA Ops:
  0.0 0.0 copy-start.2
  0.0 0.0 copy-start.1
  0.0 0.7 %convert_convert_fusion = bf16[2,8]{1,0:T(2,128)(2,1)S(1)} fusion(s32[2,8]{1,0:T(2,128)} %param.7), kind=kLoop, calls=%fused_computation.29 | loop fusion | flops 32 | bytes 96 | tf_op jit(solution)/shard_map/convert.12
  0.7 0.1 reshape.151
  0.8 0.1 tile.9
  0.9 0.8 %copy.18 = bf16[1,32]{0,1:T(8,128)(2,1)S(1)} copy(bf16[1,32]{1,0:T(2,128)(2,1)} %bitcast.15) | data formatting | bytes 128 | tf_op jit(solution)/shard_map/convert_element_type | solution.py:151
  1.6 0.0 copy-done.2
  1.7 0.1 maximum_bitcast_fusion
  1.7 0.0 copy-done.1
  1.8 0.1 broadcast_in_dim.17
  1.8 31.9 %all_to_all.5 = bf16[32,16,896]{2,1,0:T(8,128)(2,1)S(1)} all-to-all(bf16[32,16,896]{2,1,0:T(8,128)(2,1)S(1)} %bitcast.12), channel_id=1, replica_groups=mesh['row'=4,'col'=8] {'row','col'}, dimensions={0} | all-to-all | bytes 1835008 | tf_op jit(solution)/shard_map/all_to_all | solution.py:164
  33.7 0.0 copy-start
  33.7 0.0 collective-permute-start
  33.7 0.1 broadcast_in_dim.38
  33.8 0.0 copy-start.3
  33.8 0.1 mul.25
  33.9 0.6 %copy-done.3 = s32[8]{0:T(128)S(1)} copy-done((s32[8]{0:T(128)S(1)}, s32[8]{0:T(128)}, u32[]{:S(2)}) %copy-start.3) | copy-done | bytes 56
  34.5 0.1 broadcast_in_dim.39
  34.5 0.1 reshape.150
  34.6 0.2 slice_reduce_fusion
  34.9 0.1 reshape.152
  35.0 0.1 broadcast_in_dim.18
  35.1 0.1 reshape.149
  35.2 0.6 %and_select_fusion.refs_2_ = f32[1,8,1024]{2,1,0:T(8,128)} fusion(pred[1,8,1024]{2,1,0:T(8,128)(4,1)S(1)} %reshape.149, pred[1024]{0:T(1024)(128)(4,1)S(1)} %fusion.6), kind=kLoop, calls=%fused_computation.4 | loop fusion | flops 16384 | bytes 41984 | tf_op jit(solution)/shard_map/jit(_where)/select_n | solution.py:181
  35.8 0.4 collective-permute-done
  36.2 0.0 copy-start.4
  36.2 0.0 copy-done
  36.2 0.9 %copy-done.4 = bf16[32,16,896]{2,1,0:T(8,128)(2,1)} copy-done((bf16[32,16,896]{2,1,0:T(8,128)(2,1)}, bf16[32,16,896]{2,1,0:T(8,128)(2,1)S(1)}, u32[]{:S(2)}) %copy-start.4) | copy-done | bytes 917528
  37.1 8.9 %shard_map.55 = f32[32,64]{1,0:T(8,128)} custom-call(bf16[512,896]{1,0:T(8,128)(2,1)} %bitcast.13, bf16[512,896]{1,0:T(8,128)(2,1)} %bitcast.16, f32[1,8,1024]{2,1,0:T(8,128)} %and_select_fusion.refs_2_), custom_call_target="tpu_custom_call" | custom-call | flops 2147483648 | bytes 2097152 | tf_op jit(solution)/shard_map/pallas_call | solution.py:112
  (9 shorter events, 0.1 us)
Async XLA Ops:
  0.0 1.6 %copy-start.2 = (f32[64,32]{0,1:T(8,128)S(1)}, f32[64,32]{0,1:T(8,128)}, u32[]{:S(2)}) copy-start(f32[64,32]{0,1:T(8,128)} %param.9) | copy-start | bytes 24580
  0.0 1.7 %copy-start.1 = (bf16[32,768]{1,0:T(8,128)(2,1)S(1)}, bf16[32,768]{1,0:T(8,128)(2,1)}, u32[]{:S(2)}) copy-start(bf16[32,768]{1,0:T(8,128)(2,1)} %param.5) | copy-start | bytes 147460
  33.7 2.5 %copy-start = (bf16[32,16,896]{2,1,0:T(8,128)(2,1)}, bf16[32,16,896]{2,1,0:T(8,128)(2,1)S(1)}, u32[]{:S(2)}) copy-start(bf16[32,16,896]{2,1,0:T(8,128)(2,1)S(1)} %all_to_all.5) | copy-start | bytes 2752516
  33.7 2.5 %collective-permute-start = (bf16[32,16,896]{2,1,0:T(8,128)(2,1)S(1)}, bf16[32,16,896]{2,1,0:T(8,128)(2,1)S(1)}, u32[]{:S(2)}, u32[]{:S(2)}) collective-permute-start(bf16[32,16,896]{2,1,0:T(8,128)(2,1)S(1)} %all_to_all.5), channel_id=1, source_target_pairs={{0,8},{8,0},{16,24},{24,16},{1,9},{9,1},{17,25},{25,17},{2,10},{10... | collective-permute-start | bytes 2752520 | tf_op jit(solution)/shard_map/ppermute | solution.py:165
  33.8 0.7 %copy-start.3 = (s32[8]{0:T(128)S(1)}, s32[8]{0:T(128)}, u32[]{:S(2)}) copy-start(s32[8]{0:T(128)} %param.8) | copy-start | bytes 100
  36.2 0.9 %copy-start.4 = (bf16[32,16,896]{2,1,0:T(8,128)(2,1)}, bf16[32,16,896]{2,1,0:T(8,128)(2,1)S(1)}, u32[]{:S(2)}) copy-start(bf16[32,16,896]{2,1,0:T(8,128)(2,1)S(1)} %collective-permute-done) | copy-start | bytes 2752516

commit v16 on v15

--- a/solution.py
+++ b/solution.py
@@ -36,7 +36,7 @@
     return jnp.concatenate([low, high], axis=1)[:, : x.shape[0]]
 
 
-def dense_kernel(n_iter, tile, beta_lane, n_parts, mine_ref, other_ref, rowmask_ref, out_ref, unit_t, unit_s, scale_s, aff_s, state_s):
+def dense_kernel(n_iter, tile, beta_lane, n_parts, mine_ref, other_ref, rowmask_ref, out_ref, unit_t, unit_s, scale_s, aff_s, state_s, aff_t):
     feat, files = unit_t.shape
     half = files // 2
     runs = half // tile
@@ -68,9 +68,11 @@
         mass = jnp.sum(e, axis=1, keepdims=True)
         weights = e * (1.0 / mass)
         aff_s[pl.ds(p0, tile), :] = weights.astype(jnp.bfloat16)
-        return colsum + jnp.sum(weights, axis=0, keepdims=True)
-
-    colsum = lax.fori_loop(0, files // tile, step, jnp.zeros((1, files), jnp.float32))
+        weights_t = weights.T
+        aff_t[:, pl.ds(p0, tile)] = weights_t.astype(jnp.bfloat16)
+        return colsum + jnp.sum(weights_t, axis=1, keepdims=True)
+
+    colsum = lax.fori_loop(0, files // tile, step, jnp.zeros((files, 1), jnp.float32))
     inv_root = lax.rsqrt((1.0 + colsum) * 0.5)
     n_probe = out_ref.shape[1]
     state = jnp.concatenate(
@@ -78,20 +80,17 @@
             sum(
                 ref[:, feat + k * n_probe : feat + (k + 1) * n_probe].astype(jnp.float32)
                 for k in range(n_parts)
-            ).T
+            )
             for ref in (mine_ref, other_ref)
         ],
-        axis=1,
+        axis=0,
     )
     for sweep in range(n_iter):
-        scaled_f = (state * inv_root).astype(jnp.bfloat16).astype(jnp.float32)
-        scaled = scaled_f.astype(jnp.bfloat16)
-        row_t = jnp.dot(aff_s[...], scaled_f.T.astype(jnp.bfloat16), preferred_element_type=jnp.float32)
-        col_part = jnp.dot(scaled, aff_s[...], preferred_element_type=jnp.float32)
-        if sweep + 1 < n_iter:
-            state = (row_t.T + col_part) * (0.5 * inv_root)
-        else:
-            state_s[...] = (row_t + col_part.T) * (0.5 * inv_root).T
+        scaled = (state * inv_root).astype(jnp.bfloat16)
+        row_part = jnp.dot(aff_s[...], scaled, preferred_element_type=jnp.float32)
+        col_part = jnp.dot(aff_t[...], scaled, preferred_element_type=jnp.float32)
+        state = (row_part + col_part) * (0.5 * inv_root)
+    state_s[...] = state
     shard = out_ref.shape[0]
     half_s = shard // 2
     core = lax.axis_index("row") % 2
@@ -120,6 +119,7 @@
             pltpu.VMEM((files, 1), jnp.float32),
             pltpu.VMEM((files, files), jnp.bfloat16),
             pltpu.VMEM((files, n_probe), jnp.float32),
+            pltpu.VMEM((files, files), jnp.bfloat16),
         ],
         cost_estimate=pl.CostEstimate(
             flops=2 * files * files * feat + 4 * ITERS * files * files * n_probe,

time: 46.2 us -> 49.6 us (1.074)
  Pallas kernels: 8.86 us -> 12.2 us
    pallas_call x1, Pallas kernels: 8.86 us -> 12.2 us  [dense_call(): pl.pallas_call(lambda *refs: dense_kernel(ITERS, tile, beta_lane, PROBE_P...]
where the time goes in v16:
time: 49.6 us; the launch traced here: 49.4 us
  blocking collectives  31.9 us (64%)
  Pallas kernels  12.2 us (25%)
  local copies, waits for them, and re-layouts  3.39 us (7%)
  other arithmetic  1.44 us (3%)
    all_to_all x1, blocking collectives, dense_path(): mine = lax.all_to_all(wide, AXES, 0, 0, tiled=True)  31.9 us
    pallas_call x1, Pallas kernels, dense_call(): pl.pallas_call(lambda *refs: dense_kernel(ITERS, tile, beta_lane, PROBE_P...  12.2 us
    unnamed x10, local copies, waits for them, and re-layouts  1.57 us
  transfers between devices with their start and end apart: 1, of which 1 were waited for; matrix products, arithmetic and copies ran while one was open for 3% of the time, Pallas kernels for 0%

profile of v16, /device:TPU:0, one launch (start us, length us, event | category | flops | bytes accessed | tf_op | source)
XLA Modules:
  0.0 49.4 jit_solution(4094736253400000976)
XLA Ops:
  0.0 0.0 copy-start.2
  0.0 0.0 copy-start.1
  0.0 0.7 %convert_convert_fusion = bf16[2,8]{1,0:T(2,128)(2,1)S(1)} fusion(s32[2,8]{1,0:T(2,128)} %param.7), kind=kLoop, calls=%fused_computation.29 | loop fusion | flops 32 | bytes 96 | tf_op jit(solution)/shard_map/convert.12
  0.7 0.1 reshape.151
  0.8 0.1 tile.9
  0.9 0.8 %copy.18 = bf16[1,32]{0,1:T(8,128)(2,1)S(1)} copy(bf16[1,32]{1,0:T(2,128)(2,1)} %bitcast.15) | data formatting | bytes 128 | tf_op jit(solution)/shard_map/convert_element_type | solution.py:151
  1.6 0.0 copy-done.2
  1.7 0.1 maximum_bitcast_fusion
  1.7 0.0 copy-done.1
  1.8 0.1 broadcast_in_dim.17
  1.8 31.9 %all_to_all.5 = bf16[32,16,896]{2,1,0:T(8,128)(2,1)S(1)} all-to-all(bf16[32,16,896]{2,1,0:T(8,128)(2,1)S(1)} %bitcast.12), channel_id=1, replica_groups=mesh['row'=4,'col'=8] {'row','col'}, dimensions={0} | all-to-all | bytes 1835008 | tf_op jit(solution)/shard_map/all_to_all | solution.py:164
  33.7 0.0 copy-start
  33.7 0.0 collective-permute-start
  33.7 0.1 broadcast_in_dim.38
  33.8 0.0 copy-start.3
  33.8 0.1 mul.25
  33.9 0.6 %copy-done.3 = s32[8]{0:T(128)S(1)} copy-done((s32[8]{0:T(128)S(1)}, s32[8]{0:T(128)}, u32[]{:S(2)}) %copy-start.3) | copy-done | bytes 56
  34.5 0.1 broadcast_in_dim.39
  34.5 0.1 reshape.150
  34.6 0.2 slice_reduce_fusion
  34.9 0.1 reshape.152
  35.0 0.1 broadcast_in_dim.18
  35.1 0.1 reshape.149
  35.2 0.6 %and_select_fusion.refs_2_ = f32[1,8,1024]{2,1,0:T(8,128)} fusion(pred[1,8,1024]{2,1,0:T(8,128)(4,1)S(1)} %reshape.149, pred[1024]{0:T(1024)(128)(4,1)S(1)} %fusion.6), kind=kLoop, calls=%fused_computation.4 | loop fusion | flops 16384 | bytes 41984 | tf_op jit(solution)/shard_map/jit(_where)/select_n | solution.py:181
  35.8 0.4 collective-permute-done
  36.2 0.0 copy-start.4
  36.2 0.0 copy-done
  36.2 0.9 %copy-done.4 = bf16[32,16,896]{2,1,0:T(8,128)(2,1)} copy-done((bf16[32,16,896]{2,1,0:T(8,128)(2,1)}, bf16[32,16,896]{2,1,0:T(8,128)(2,1)S(1)}, u32[]{:S(2)}) %copy-start.4) | copy-done | bytes 917528
  37.1 12.2 %shard_map.55 = f32[32,64]{1,0:T(8,128)} custom-call(bf16[512,896]{1,0:T(8,128)(2,1)} %bitcast.13, bf16[512,896]{1,0:T(8,128)(2,1)} %bitcast.16, f32[1,8,1024]{2,1,0:T(8,128)} %and_select_fusion.refs_2_), custom_call_target="tpu_custom_call" | custom-call | flops 2147483648 | bytes 2097152 | tf_op jit(solution)/shard_map/pallas_call | solution.py:111
  (9 shorter events, 0.1 us)
Async XLA Ops:
  0.0 1.6 %copy-start.2 = (f32[64,32]{0,1:T(8,128)S(1)}, f32[64,32]{0,1:T(8,128)}, u32[]{:S(2)}) copy-start(f32[64,32]{0,1:T(8,128)} %param.9) | copy-start | bytes 24580
  0.0 1.7 %copy-start.1 = (bf16[32,768]{1,0:T(8,128)(2,1)S(1)}, bf16[32,768]{1,0:T(8,128)(2,1)}, u32[]{:S(2)}) copy-start(bf16[32,768]{1,0:T(8,128)(2,1)} %param.5) | copy-start | bytes 147460
  33.7 2.5 %copy-start = (bf16[32,16,896]{2,1,0:T(8,128)(2,1)}, bf16[32,16,896]{2,1,0:T(8,128)(2,1)S(1)}, u32[]{:S(2)}) copy-start(bf16[32,16,896]{2,1,0:T(8,128)(2,1)S(1)} %all_to_all.5) | copy-start | bytes 2752516
  33.7 2.5 %collective-permute-start = (bf16[32,16,896]{2,1,0:T(8,128)(2,1)S(1)}, bf16[32,16,896]{2,1,0:T(8,128)(2,1)S(1)}, u32[]{:S(2)}, u32[]{:S(2)}) collective-permute-start(bf16[32,16,896]{2,1,0:T(8,128)(2,1)S(1)} %all_to_all.5), channel_id=1, source_target_pairs={{0,8},{8,0},{16,24},{24,16},{1,9},{9,1},{17,25},{25,17},{2,10},{10... | collective-permute-start | bytes 2752520 | tf_op jit(solution)/shard_map/ppermute | solution.py:165
  33.8 0.7 %copy-start.3 = (s32[8]{0:T(128)S(1)}, s32[8]{0:T(128)}, u32[]{:S(2)}) copy-start(s32[8]{0:T(128)} %param.8) | copy-start | bytes 100
  36.2 0.9 %copy-start.4 = (bf16[32,16,896]{2,1,0:T(8,128)(2,1)}, bf16[32,16,896]{2,1,0:T(8,128)(2,1)S(1)}, u32[]{:S(2)}) copy-start(bf16[32,16,896]{2,1,0:T(8,128)(2,1)S(1)} %collective-permute-done) | copy-start | bytes 2752516

commit v17 on v15

--- a/solution.py
+++ b/solution.py
@@ -46,7 +46,7 @@
             values * lax.rsqrt(jnp.mean(values * values, axis=1, keepdims=True) + 1e-06)
         ).astype(jnp.bfloat16)
         unit_s[k * half : (k + 1) * half, :] = unit
-        unit_t[:, k * half : (k + 1) * half] = unit.astype(jnp.float32).T.astype(jnp.bfloat16)
+        unit_t[:, k * half : (k + 1) * half] = unit.T
         scale_s[k * half : (k + 1) * half, :] = (
             ref[:, beta_lane : beta_lane + 1].astype(jnp.float32) / feat
         )

time: 46.2 us -> 46.3 us (level)
  no operation moved by 1% of the time
where the time goes in v17:
time: 46.3 us; the launch traced here: 46.1 us
  blocking collectives  31.9 us (69%)
  Pallas kernels  8.94 us (19%)
  local copies, waits for them, and re-layouts  3.39 us (7%)
  other arithmetic  1.44 us (3%)
    all_to_all x1, blocking collectives, dense_path(): mine = lax.all_to_all(wide, AXES, 0, 0, tiled=True)  31.9 us
    pallas_call x1, Pallas kernels, dense_call(): pl.pallas_call(lambda *refs: dense_kernel(ITERS, tile, beta_lane, PROBE_P...  8.94 us
    unnamed x10, local copies, waits for them, and re-layouts  1.57 us
  transfers between devices with their start and end apart: 1, of which 1 were waited for; matrix products, arithmetic and copies ran while one was open for 3% of the time, Pallas kernels for 0%

profile of v17, /device:TPU:0, one launch (start us, length us, event | category | flops | bytes accessed | tf_op | source)
XLA Modules:
  0.0 46.1 jit_solution(7638236369525349046)
XLA Ops:
  0.0 0.0 copy-start.2
  0.0 0.0 copy-start.1
  0.0 0.7 %convert_convert_fusion = bf16[2,8]{1,0:T(2,128)(2,1)S(1)} fusion(s32[2,8]{1,0:T(2,128)} %param.7), kind=kLoop, calls=%fused_computation.29 | loop fusion | flops 32 | bytes 96 | tf_op jit(solution)/shard_map/convert.12
  0.7 0.1 reshape.151
  0.8 0.1 tile.9
  0.9 0.8 %copy.18 = bf16[1,32]{0,1:T(8,128)(2,1)S(1)} copy(bf16[1,32]{1,0:T(2,128)(2,1)} %bitcast.15) | data formatting | bytes 128 | tf_op jit(solution)/shard_map/convert_element_type | solution.py:151
  1.6 0.0 copy-done.2
  1.7 0.1 maximum_bitcast_fusion
  1.7 0.0 copy-done.1
  1.8 0.1 broadcast_in_dim.17
  1.8 31.9 %all_to_all.5 = bf16[32,16,896]{2,1,0:T(8,128)(2,1)S(1)} all-to-all(bf16[32,16,896]{2,1,0:T(8,128)(2,1)S(1)} %bitcast.12), channel_id=1, replica_groups=mesh['row'=4,'col'=8] {'row','col'}, dimensions={0} | all-to-all | bytes 1835008 | tf_op jit(solution)/shard_map/all_to_all | solution.py:164
  33.7 0.0 copy-start
  33.7 0.0 collective-permute-start
  33.7 0.1 broadcast_in_dim.38
  33.8 0.0 copy-start.3
  33.8 0.1 mul.25
  33.9 0.6 %copy-done.3 = s32[8]{0:T(128)S(1)} copy-done((s32[8]{0:T(128)S(1)}, s32[8]{0:T(128)}, u32[]{:S(2)}) %copy-start.3) | copy-done | bytes 56
  34.5 0.1 broadcast_in_dim.39
  34.5 0.1 reshape.150
  34.6 0.2 slice_reduce_fusion
  34.9 0.1 reshape.152
  35.0 0.1 broadcast_in_dim.18
  35.1 0.1 reshape.149
  35.2 0.6 %and_select_fusion.refs_2_ = f32[1,8,1024]{2,1,0:T(8,128)} fusion(pred[1,8,1024]{2,1,0:T(8,128)(4,1)S(1)} %reshape.149, pred[1024]{0:T(1024)(128)(4,1)S(1)} %fusion.6), kind=kLoop, calls=%fused_computation.4 | loop fusion | flops 16384 | bytes 41984 | tf_op jit(solution)/shard_map/jit(_where)/select_n | solution.py:181
  35.8 0.4 collective-permute-done
  36.2 0.0 copy-start.4
  36.2 0.0 copy-done
  36.2 0.9 %copy-done.4 = bf16[32,16,896]{2,1,0:T(8,128)(2,1)} copy-done((bf16[32,16,896]{2,1,0:T(8,128)(2,1)}, bf16[32,16,896]{2,1,0:T(8,128)(2,1)S(1)}, u32[]{:S(2)}) %copy-start.4) | copy-done | bytes 917528
  37.1 8.9 %shard_map.55 = f32[32,64]{1,0:T(8,128)} custom-call(bf16[512,896]{1,0:T(8,128)(2,1)} %bitcast.13, bf16[512,896]{1,0:T(8,128)(2,1)} %bitcast.16, f32[1,8,1024]{2,1,0:T(8,128)} %and_select_fusion.refs_2_), custom_call_target="tpu_custom_call" | custom-call | flops 2147483648 | bytes 2097152 | tf_op jit(solution)/shard_map/pallas_call | solution.py:112
  (9 shorter events, 0.1 us)
Async XLA Ops:
  0.0 1.6 %copy-start.2 = (f32[64,32]{0,1:T(8,128)S(1)}, f32[64,32]{0,1:T(8,128)}, u32[]{:S(2)}) copy-start(f32[64,32]{0,1:T(8,128)} %param.9) | copy-start | bytes 24580
  0.0 1.7 %copy-start.1 = (bf16[32,768]{1,0:T(8,128)(2,1)S(1)}, bf16[32,768]{1,0:T(8,128)(2,1)}, u32[]{:S(2)}) copy-start(bf16[32,768]{1,0:T(8,128)(2,1)} %param.5) | copy-start | bytes 147460
  33.7 2.5 %copy-start = (bf16[32,16,896]{2,1,0:T(8,128)(2,1)}, bf16[32,16,896]{2,1,0:T(8,128)(2,1)S(1)}, u32[]{:S(2)}) copy-start(bf16[32,16,896]{2,1,0:T(8,128)(2,1)S(1)} %all_to_all.5) | copy-start | bytes 2752516
  33.7 2.5 %collective-permute-start = (bf16[32,16,896]{2,1,0:T(8,128)(2,1)S(1)}, bf16[32,16,896]{2,1,0:T(8,128)(2,1)S(1)}, u32[]{:S(2)}, u32[]{:S(2)}) collective-permute-start(bf16[32,16,896]{2,1,0:T(8,128)(2,1)S(1)} %all_to_all.5), channel_id=1, source_target_pairs={{0,8},{8,0},{16,24},{24,16},{1,9},{9,1},{17,25},{25,17},{2,10},{10... | collective-permute-start | bytes 2752520 | tf_op jit(solution)/shard_map/ppermute | solution.py:165
  33.8 0.7 %copy-start.3 = (s32[8]{0:T(128)S(1)}, s32[8]{0:T(128)}, u32[]{:S(2)}) copy-start(s32[8]{0:T(128)} %param.8) | copy-start | bytes 100
  36.2 0.9 %copy-start.4 = (bf16[32,16,896]{2,1,0:T(8,128)(2,1)}, bf16[32,16,896]{2,1,0:T(8,128)(2,1)S(1)}, u32[]{:S(2)}) copy-start(bf16[32,16,896]{2,1,0:T(8,128)(2,1)S(1)} %collective-permute-done) | copy-start | bytes 2752516

commit v18 on v15

--- a/solution.py
+++ b/solution.py
@@ -39,7 +39,7 @@
 def dense_kernel(n_iter, tile, beta_lane, n_parts, mine_ref, other_ref, rowmask_ref, out_ref, unit_t, unit_s, scale_s, aff_s, state_s):
     feat, files = unit_t.shape
     half = files // 2
-    runs = half // tile
+    runs = max(half // tile, 1)
     for k, ref in enumerate((mine_ref, other_ref)):
         values = ref[:, 0:feat].astype(jnp.float32)
         unit = (
@@ -105,8 +105,10 @@
     files = 2 * mine.shape[0]
     run = files // (2 * rowmask.shape[0])
     tile = run
-    while tile * 2 <= min(512, files // 2) and (files // 2) % (tile * 2) == 0:
+    while tile * 2 <= min(1024, files) and files % (tile * 2) == 0:
         tile *= 2
+    if tile > files // 2:
+        rowmask = jnp.tile(rowmask, (tile // (files // 2), 1))
     rowmask = rowmask.reshape(-1, tile // run, files)
     vmem = pl.BlockSpec(memory_space=pltpu.VMEM)
     return pl.pallas_call(

time: 46.2 us -> 46.8 us (1.013)
  blocking collectives: 31.9 us -> 0 us
  waiting for transfers between devices: 0.36 us -> 25.1 us
  starting transfers between devices: 0.01 us -> 7.3 us
  local copies, waits for them, and re-layouts: 3.39 us -> 4.93 us
  other arithmetic: 1.44 us -> 0.83 us
  Pallas kernels: 8.86 us -> 8.25 us
    all_to_all x1 -> x0, blocking collectives: 31.9 us -> none  [dense_path(): mine = lax.all_to_all(wide, AXES, 0, 0, tiled=True)]
    all_to_all x0 -> x1, waiting for transfers between devices: none -> 23.9 us  [dense_path(): mine = lax.all_to_all(wide, AXES, 0, 0, tiled=True)]
    all_to_all x0 -> x1, starting transfers between devices: none -> 7.3 us  [dense_path(): mine = lax.all_to_all(wide, AXES, 0, 0, tiled=True)]
    broadcast_in_dim x1, local copies, waits for them, and re-layouts: 0.07 us -> 1.01 us  [dense_path(): jnp.broadcast_to(halves[None, :, None], (n_row // 2, 2, per_row, half_s,...]
    ppermute x1, waiting for transfers between devices: 0.36 us -> 1.24 us  [dense_path(): other = lax.ppermute(mine, 'row', [(r, r ^ 1) for r in range(n_row)])]
    another operation x1 -> x2, local copies, waits for them, and re-layouts: 0.09 us -> 0.71 us  [the longest x1 0.62 us: dense_call(): rowmask = jnp.tile(rowmask, (tile // (files // 2), 1))]
    pallas_call x1, Pallas kernels: 8.86 us -> 8.25 us  [dense_call(): pl.pallas_call(lambda *refs: dense_kernel(ITERS, tile, beta_lane, PROBE_P...]
    select_n x1, other arithmetic: 0.61 us -> 0.01 us  [dense_path(): jnp.where(block_ok.reshape(nb, files) & live[None, :], 1.0, 0.0)]
  transfers between devices with their start and end apart: 1 -> 2, of which waited for: 1 -> 2; matrix products, arithmetic and copies ran while one was open for 3% -> 3% of each run, Pallas kernels for 0% -> 0%
where the time goes in v18:
time: 46.8 us; the launch traced here: 46.5 us
  waiting for transfers between devices  25.1 us (54%)
  Pallas kernels  8.25 us (18%)
  starting transfers between devices  7.3 us (16%)
  local copies, waits for them, and re-layouts  4.93 us (11%)
  other arithmetic  0.83 us (2%)
    all_to_all x1, waiting for transfers between devices, dense_path(): mine = lax.all_to_all(wide, AXES, 0, 0, tiled=True)  23.9 us
    pallas_call x1, Pallas kernels, dense_call(): pl.pallas_call(lambda *refs: dense_kernel(ITERS, tile, beta_lane, PROBE_P...  8.25 us
    all_to_all x1, starting transfers between devices, dense_path(): mine = lax.all_to_all(wide, AXES, 0, 0, tiled=True)  7.3 us
    unnamed x10, local copies, waits for them, and re-layouts  1.55 us
    ppermute x1, waiting for transfers between devices, dense_path(): other = lax.ppermute(mine, 'row', [(r, r ^ 1) for r in range(n_row)])  1.24 us
    broadcast_in_dim x1, local copies, waits for them, and re-layouts, dense_path(): jnp.broadcast_to(halves[None, :, None], (n_row // 2, 2, per_row, half_s,...  1.01 us
  transfers between devices with their start and end apart: 2, of which 2 were waited for; matrix products, arithmetic and copies ran while one was open for 3% of the time, Pallas kernels for 0%

profile of v18, /device:TPU:0, one launch (start us, length us, event | category | flops | bytes accessed | tf_op | source)
XLA Modules:
  0.0 46.5 jit_solution(10574520810001236556)
XLA Ops:
  0.0 0.0 copy-start.2
  0.0 0.0 copy-start.1
  0.0 0.7 %convert_convert_fusion = bf16[2,8]{1,0:T(2,128)(2,1)S(1)} fusion(s32[2,8]{1,0:T(2,128)} %param.7), kind=kLoop, calls=%fused_computation.30 | loop fusion | flops 32 | bytes 96 | tf_op jit(solution)/shard_map/convert.12
  0.7 0.1 reshape.141
  0.8 0.1 tile.19
  0.9 0.8 %copy.18 = bf16[1,32]{0,1:T(8,128)(2,1)S(1)} copy(bf16[1,32]{1,0:T(2,128)(2,1)} %bitcast.16) | data formatting | bytes 128 | tf_op jit(solution)/shard_map/convert_element_type | solution.py:153
  1.6 0.0 copy-done.2
  1.7 0.1 maximum_bitcast_fusion
  1.7 0.0 copy-done.1
  1.8 1.0 %broadcast_in_dim.17 = bf16[2,2,8,16,896]{4,3,2,1,0:T(8,128)(2,1)} broadcast(bf16[2,16,896]{2,1,0:T(8,128)(2,1)S(1)} %bitcast.15), dimensions={1,3,4} | broadcast | bytes 974848 | tf_op jit(solution)/shard_map/broadcast_in_dim | solution.py:163
  2.8 7.3 %all-to-all-start = ((bf16[32,16,896]{2,1,0:T(8,128)(2,1)}), bf16[32,16,896]{2,1,0:T(8,128)(2,1)S(1)}, u32[]{:S(2)}, u32[]{:S(2)}) async-start(bf16[32,16,896]{2,1,0:T(8,128)(2,1)} %bitcast.3), calls=%async_computation | async-start | bytes 1835008 | tf_op jit(solution)/shard_map/all_to_all | solution.py:166
  10.1 0.1 broadcast_in_dim.38
  10.2 0.0 copy-start.3
  10.2 0.1 mul.25
  10.2 0.6 %copy-done.3 = s32[8]{0:T(128)S(1)} copy-done((s32[8]{0:T(128)S(1)}, s32[8]{0:T(128)}, u32[]{:S(2)}) %copy-start.3) | copy-done | bytes 56
  10.8 0.1 broadcast_in_dim.39
  10.9 0.1 reshape.140
  11.0 23.9 %all-to-all-done = bf16[32,16,896]{2,1,0:T(8,128)(2,1)S(1)} async-done(((bf16[32,16,896]{2,1,0:T(8,128)(2,1)}), bf16[32,16,896]{2,1,0:T(8,128)(2,1)S(1)}, u32[]{:S(2)}, u32[]{:S(2)}) %all-to-all-start) | async-done | bytes 917536 | tf_op jit(solution)/shard_map/all_to_all | solution.py:166
  34.8 0.0 copy-start
  34.8 0.0 collective-permute-start
  34.9 0.2 slice_reduce_fusion
  35.1 0.1 reshape.142
  35.3 0.1 broadcast_in_dim.18
  35.3 0.1 reshape.139
  35.5 0.6 %broadcast_bitcast_fusion.refs_2_ = f32[1,16,1024]{2,1,0:T(8,128)} fusion(f32[8,1024]{1,0:T(8,128)S(1)} %and_select_fusion), kind=kLoop, calls=%fused_computation.4 | loop fusion | bytes 98304 | tf_op jit(solution)/shard_map/tile | solution.py:111
  36.1 1.2 %collective-permute-done = bf16[32,16,896]{2,1,0:T(8,128)(2,1)S(1)} collective-permute-done((bf16[32,16,896]{2,1,0:T(8,128)(2,1)S(1)}, bf16[32,16,896]{2,1,0:T(8,128)(2,1)S(1)}, u32[]{:S(2)}, u32[]{:S(2)}) %collective-permute-start) | collective-permute-done | bytes 917536 | tf_op jit(solution)/shard_map/ppermute | solution.py:167
  37.3 0.0 copy-start.4
  37.3 0.0 copy-done
  37.3 0.9 %copy-done.4 = bf16[32,16,896]{2,1,0:T(8,128)(2,1)} copy-done((bf16[32,16,896]{2,1,0:T(8,128)(2,1)}, bf16[32,16,896]{2,1,0:T(8,128)(2,1)S(1)}, u32[]{:S(2)}) %copy-start.4) | copy-done | bytes 917528
  38.3 8.2 %shard_map.55 = f32[32,64]{1,0:T(8,128)} custom-call(bf16[512,896]{1,0:T(8,128)(2,1)} %bitcast.14, bf16[512,896]{1,0:T(8,128)(2,1)} %bitcast.17, f32[1,16,1024]{2,1,0:T(8,128)} %broadcast_bitcast_fusion.refs_2_), custom_call_target="tpu_custom_call" | custom-call | flops 2147483648 | bytes 2097152 | tf_op jit(solution)/shard_map/pallas_call | solution.py:114
  (10 shorter events, 0.1 us)
Async XLA Ops:
  0.0 1.6 %copy-start.2 = (f32[64,32]{0,1:T(8,128)S(1)}, f32[64,32]{0,1:T(8,128)}, u32[]{:S(2)}) copy-start(f32[64,32]{0,1:T(8,128)} %param.9) | copy-start | bytes 24580
  0.0 1.7 %copy-start.1 = (bf16[32,768]{1,0:T(8,128)(2,1)S(1)}, bf16[32,768]{1,0:T(8,128)(2,1)}, u32[]{:S(2)}) copy-start(bf16[32,768]{1,0:T(8,128)(2,1)} %param.5) | copy-start | bytes 147460
  2.8 32.1 %all-to-all-start = ((bf16[32,16,896]{2,1,0:T(8,128)(2,1)}), bf16[32,16,896]{2,1,0:T(8,128)(2,1)S(1)}, u32[]{:S(2)}, u32[]{:S(2)}) async-start(bf16[32,16,896]{2,1,0:T(8,128)(2,1)} %bitcast.3), calls=%async_computation | async-start | bytes 1835008 | tf_op jit(solution)/shard_map/all_to_all | solution.py:166
  10.2 0.7 %copy-start.3 = (s32[8]{0:T(128)S(1)}, s32[8]{0:T(128)}, u32[]{:S(2)}) copy-start(s32[8]{0:T(128)} %param.8) | copy-start | bytes 100
  34.8 2.5 %copy-start = (bf16[32,16,896]{2,1,0:T(8,128)(2,1)}, bf16[32,16,896]{2,1,0:T(8,128)(2,1)S(1)}, u32[]{:S(2)}) copy-start(bf16[32,16,896]{2,1,0:T(8,128)(2,1)S(1)} %all-to-all-done) | copy-start | bytes 2752516
  34.8 2.5 %collective-permute-start = (bf16[32,16,896]{2,1,0:T(8,128)(2,1)S(1)}, bf16[32,16,896]{2,1,0:T(8,128)(2,1)S(1)}, u32[]{:S(2)}, u32[]{:S(2)}) collective-permute-start(bf16[32,16,896]{2,1,0:T(8,128)(2,1)S(1)} %all-to-all-done), channel_id=1, source_target_pairs={{0,8},{8,0},{16,24},{24,16},{1,9},{9,1},{17,25},{25,17},{2,10},{10... | collective-permute-start | bytes 2752520 | tf_op jit(solution)/shard_map/ppermute | solution.py:167
  37.3 1.0 %copy-start.4 = (bf16[32,16,896]{2,1,0:T(8,128)(2,1)}, bf16[32,16,896]{2,1,0:T(8,128)(2,1)S(1)}, u32[]{:S(2)}) copy-start(bf16[32,16,896]{2,1,0:T(8,128)(2,1)S(1)} %collective-permute-done) | copy-start | bytes 2752516

commit v19 on v15

--- a/solution.py
+++ b/solution.py
@@ -36,7 +36,7 @@
     return jnp.concatenate([low, high], axis=1)[:, : x.shape[0]]
 
 
-def dense_kernel(n_iter, tile, beta_lane, n_parts, mine_ref, other_ref, rowmask_ref, out_ref, unit_t, unit_s, scale_s, aff_s, state_s):
+def dense_kernel(n_iter, tile, beta_lane, n_parts, mine_ref, other_ref, rowmask_ref, out_ref, unit_t, unit_s, scale_s, aff_s, state_s, gram_s):
     feat, files = unit_t.shape
     half = files // 2
     runs = half // tile
@@ -50,6 +50,7 @@
         scale_s[k * half : (k + 1) * half, :] = (
             ref[:, beta_lane : beta_lane + 1].astype(jnp.float32) / feat
         )
+    gram_s[...] = jnp.dot(unit_s[...], unit_t[...], preferred_element_type=jnp.float32)
     per_tile = rowmask_ref.shape[1]
     run = tile // per_tile
     col_pos = lax.broadcasted_iota(jnp.int32, (tile, files), 1)
@@ -57,8 +58,7 @@
 
     def step(t, colsum):
         p0 = pl.multiple_of(t * tile, tile)
-        gram = jnp.dot(unit_s[pl.ds(p0, tile), :], unit_t[...], preferred_element_type=jnp.float32)
-        scores = gram * scale_s[pl.ds(p0, tile), :]
+        scores = gram_s[pl.ds(p0, tile), :] * scale_s[pl.ds(p0, tile), :]
         runs_here = rowmask_ref[t % runs]
         block_row = jnp.broadcast_to(runs_here[:, None, :], (per_tile, run, files)).reshape(tile, files)
         ok = (block_row > 0.0) & (row_pos + p0 != col_pos)
@@ -120,6 +120,7 @@
             pltpu.VMEM((files, 1), jnp.float32),
             pltpu.VMEM((files, files), jnp.bfloat16),
             pltpu.VMEM((files, n_probe), jnp.float32),
+            pltpu.VMEM((files, files), jnp.float32),
         ],
         cost_estimate=pl.CostEstimate(
             flops=2 * files * files * feat + 4 * ITERS * files * files * n_probe,

time: 46.2 us -> 47.1 us (1.019)
  Pallas kernels: 8.86 us -> 9.71 us
    pallas_call x1, Pallas kernels: 8.86 us -> 9.71 us  [dense_call(): pl.pallas_call(lambda *refs: dense_kernel(ITERS, tile, beta_lane, PROBE_P...]
where the time goes in v19:
time: 47.1 us; the launch traced here: 46.8 us
  blocking collectives  31.9 us (68%)
  Pallas kernels  9.71 us (21%)
  local copies, waits for them, and re-layouts  3.39 us (7%)
  other arithmetic  1.44 us (3%)
    all_to_all x1, blocking collectives, dense_path(): mine = lax.all_to_all(wide, AXES, 0, 0, tiled=True)  31.9 us
    pallas_call x1, Pallas kernels, dense_call(): pl.pallas_call(lambda *refs: dense_kernel(ITERS, tile, beta_lane, PROBE_P...  9.71 us
    unnamed x10, local copies, waits for them, and re-layouts  1.57 us
  transfers between devices with their start and end apart: 1, of which 1 were waited for; matrix products, arithmetic and copies ran while one was open for 3% of the time, Pallas kernels for 0%

profile of v19, /device:TPU:0, one launch (start us, length us, event | category | flops | bytes accessed | tf_op | source)
XLA Modules:
  0.0 46.8 jit_solution(18160028854329790355)
XLA Ops:
  0.0 0.0 copy-start.2
  0.0 0.0 copy-start.1
  0.0 0.7 %convert_convert_fusion = bf16[2,8]{1,0:T(2,128)(2,1)S(1)} fusion(s32[2,8]{1,0:T(2,128)} %param.7), kind=kLoop, calls=%fused_computation.29 | loop fusion | flops 32 | bytes 96 | tf_op jit(solution)/shard_map/convert.12
  0.7 0.1 reshape.151
  0.8 0.1 tile.9
  0.9 0.8 %copy.18 = bf16[1,32]{0,1:T(8,128)(2,1)S(1)} copy(bf16[1,32]{1,0:T(2,128)(2,1)} %bitcast.15) | data formatting | bytes 128 | tf_op jit(solution)/shard_map/convert_element_type | solution.py:152
  1.6 0.0 copy-done.2
  1.7 0.1 maximum_bitcast_fusion
  1.7 0.0 copy-done.1
  1.8 0.1 broadcast_in_dim.17
  1.8 31.9 %all_to_all.5 = bf16[32,16,896]{2,1,0:T(8,128)(2,1)S(1)} all-to-all(bf16[32,16,896]{2,1,0:T(8,128)(2,1)S(1)} %bitcast.12), channel_id=1, replica_groups=mesh['row'=4,'col'=8] {'row','col'}, dimensions={0} | all-to-all | bytes 1835008 | tf_op jit(solution)/shard_map/all_to_all | solution.py:165
  33.7 0.0 copy-start
  33.7 0.0 collective-permute-start
  33.7 0.1 broadcast_in_dim.38
  33.8 0.0 copy-start.3
  33.8 0.1 mul.25
  33.9 0.6 %copy-done.3 = s32[8]{0:T(128)S(1)} copy-done((s32[8]{0:T(128)S(1)}, s32[8]{0:T(128)}, u32[]{:S(2)}) %copy-start.3) | copy-done | bytes 56
  34.5 0.1 broadcast_in_dim.39
  34.5 0.1 reshape.150
  34.6 0.2 slice_reduce_fusion
  34.9 0.1 reshape.152
  35.0 0.1 broadcast_in_dim.18
  35.1 0.1 reshape.149
  35.2 0.6 %and_select_fusion.refs_2_ = f32[1,8,1024]{2,1,0:T(8,128)} fusion(pred[1,8,1024]{2,1,0:T(8,128)(4,1)S(1)} %reshape.149, pred[1024]{0:T(1024)(128)(4,1)S(1)} %fusion.6), kind=kLoop, calls=%fused_computation.4 | loop fusion | flops 16384 | bytes 41984 | tf_op jit(solution)/shard_map/jit(_where)/select_n | solution.py:182
  35.8 0.4 collective-permute-done
  36.2 0.0 copy-start.4
  36.2 0.0 copy-done
  36.2 0.9 %copy-done.4 = bf16[32,16,896]{2,1,0:T(8,128)(2,1)} copy-done((bf16[32,16,896]{2,1,0:T(8,128)(2,1)}, bf16[32,16,896]{2,1,0:T(8,128)(2,1)S(1)}, u32[]{:S(2)}) %copy-start.4) | copy-done | bytes 917528
  37.1 9.7 %shard_map.55 = f32[32,64]{1,0:T(8,128)} custom-call(bf16[512,896]{1,0:T(8,128)(2,1)} %bitcast.13, bf16[512,896]{1,0:T(8,128)(2,1)} %bitcast.16, f32[1,8,1024]{2,1,0:T(8,128)} %and_select_fusion.refs_2_), custom_call_target="tpu_custom_call" | custom-call | flops 2147483648 | bytes 2097152 | tf_op jit(solution)/shard_map/pallas_call | solution.py:112
  (9 shorter events, 0.1 us)
Async XLA Ops:
  0.0 1.6 %copy-start.2 = (f32[64,32]{0,1:T(8,128)S(1)}, f32[64,32]{0,1:T(8,128)}, u32[]{:S(2)}) copy-start(f32[64,32]{0,1:T(8,128)} %param.9) | copy-start | bytes 24580
  0.0 1.7 %copy-start.1 = (bf16[32,768]{1,0:T(8,128)(2,1)S(1)}, bf16[32,768]{1,0:T(8,128)(2,1)}, u32[]{:S(2)}) copy-start(bf16[32,768]{1,0:T(8,128)(2,1)} %param.5) | copy-start | bytes 147460
  33.7 2.5 %copy-start = (bf16[32,16,896]{2,1,0:T(8,128)(2,1)}, bf16[32,16,896]{2,1,0:T(8,128)(2,1)S(1)}, u32[]{:S(2)}) copy-start(bf16[32,16,896]{2,1,0:T(8,128)(2,1)S(1)} %all_to_all.5) | copy-start | bytes 2752516
  33.7 2.5 %collective-permute-start = (bf16[32,16,896]{2,1,0:T(8,128)(2,1)S(1)}, bf16[32,16,896]{2,1,0:T(8,128)(2,1)S(1)}, u32[]{:S(2)}, u32[]{:S(2)}) collective-permute-start(bf16[32,16,896]{2,1,0:T(8,128)(2,1)S(1)} %all_to_all.5), channel_id=1, source_target_pairs={{0,8},{8,0},{16,24},{24,16},{1,9},{9,1},{17,25},{25,17},{2,10},{10... | collective-permute-start | bytes 2752520 | tf_op jit(solution)/shard_map/ppermute | solution.py:166
  33.8 0.7 %copy-start.3 = (s32[8]{0:T(128)S(1)}, s32[8]{0:T(128)}, u32[]{:S(2)}) copy-start(s32[8]{0:T(128)} %param.8) | copy-start | bytes 100
  36.2 0.9 %copy-start.4 = (bf16[32,16,896]{2,1,0:T(8,128)(2,1)}, bf16[32,16,896]{2,1,0:T(8,128)(2,1)S(1)}, u32[]{:S(2)}) copy-start(bf16[32,16,896]{2,1,0:T(8,128)(2,1)S(1)} %collective-permute-done) | copy-start | bytes 2752516
